TPU v7x, 32 devices: a whole 2x2x4 slice. The times are simulated.
32 devices in a mesh: date: 16 (over z, x, core), strip: 2 (over y).
Axes of the slice: x: 2, y: 2, z: 4, core: 2. Of those that a mesh axis runs over, the one named last changes fastest.
Arguments:
- slc: bfloat16 [128, 2, 512, 384], P('date', None, 'strip'), as said below
- offsets: int32 [128, 3], P('date'), may hold values from 1 to 3
- owner: int32 [16], replicated, may hold values from 0 to 15, each once
Outputs:
- interferograms: float32 [128, 3, 2, 32, 96], P('date', None, None, 'strip')
- coherence: float32 [128, 3, 32, 96], P('date', None, 'strip')
- network_mean: float32 [16, 2, 32, 6], P('date', None, 'strip')
Inputs may be any that keep to these rules, and one draw needn't show every extreme that they name: `slc`: each image is a common scene turned by a phase of its date plus noise of its date.
All inputs are finite; a program needn't handle non-finite values.
Results may differ from a plain program's by a relative error of at most 0.0003.
Values may be sent and summed in bfloat16 or wider, within the bound.
No kernel may reach another device: no remote copies, remote signals or barrier semaphores. Data moves between devices by JAX's collectives and lax.ppermute only.
A program may use at most 128 MiB of HBM per device.

v0:
```python
import jax
import jax.numpy as jnp
from jax import lax
from jax.sharding import PartitionSpec as P

NB = 3
LR = 16
LA = 4


def shifted(value, axis, steps):
    count = lax.axis_size(axis)
    pairs = [(source, (source + steps) % count) for source in range(count)]
    return lax.ppermute(value, axis, pairs)


def pooling(cols):
    lines = jnp.arange(cols, dtype=jnp.int32)
    cells = jnp.arange(cols // LA, dtype=jnp.int32)
    return (lines[:, None] // LA == cells[None, :]).astype(jnp.float32)


def looks(field, pool):
    count, rows, cols = field.shape
    ranged = field.reshape(count, rows // LR, LR, cols).sum(2)
    pooled = jnp.einsum("nra,ab->nrb", ranged, pool, precision=lax.Precision.HIGHEST)
    return pooled * (1.0 / (LR * LA))


def pair_block(own_images, extended, block_offsets):
    count = own_images.shape[0]
    own = own_images.astype(jnp.float32)
    pool = pooling(own.shape[3])
    pairs = []
    coher = []
    for slot in range(NB):
        step_off = block_offsets[:, slot][:, None, None, None]
        chosen = extended[NB : NB + count]
        for dist in range(NB - 1, 0, -1):
            chosen = jnp.where(step_off == dist, extended[dist : dist + count], chosen)
        other = chosen.astype(jnp.float32)
        real_part = looks(own[:, 0] * other[:, 0] + own[:, 1] * other[:, 1], pool)
        imag_part = looks(own[:, 1] * other[:, 0] - own[:, 0] * other[:, 1], pool)
        power_a = looks(own[:, 0] * own[:, 0] + own[:, 1] * own[:, 1], pool)
        power_b = looks(other[:, 0] * other[:, 0] + other[:, 1] * other[:, 1], pool)
        pairs.append(jnp.stack([real_part, imag_part], 1))
        coher.append(
            jnp.sqrt(real_part * real_part + imag_part * imag_part)
            / jnp.sqrt(power_a * power_b + 1e-06)
        )
    return (jnp.stack(pairs, 1), jnp.stack(coher, 1))


def on_device(slc, offsets, owner):
    count = slc.shape[0]
    rim = shifted(slc[:NB], "date", -1)
    extended = jnp.concatenate([slc, rim], 0)
    interferograms, coherence = pair_block(slc, extended, offsets)
    weighted = jnp.concatenate([coherence[:, :, None] * interferograms, coherence[:, :, None]], 2)
    tile_count = owner.shape[0]
    rows_loc = weighted.shape[3]
    width = weighted.shape[4] // tile_count
    slots = jnp.arange(tile_count, dtype=jnp.int32)
    onehot = (owner[None, :] == slots[:, None]).astype(jnp.float32)
    flat = weighted.reshape(count * NB, 3, rows_loc, tile_count, width).transpose(3, 0, 1, 2, 4)
    slotted = jnp.einsum("st,tpcrw->spcrw", onehot, flat, precision=lax.Precision.HIGHEST)
    sums = lax.all_to_all(slotted, "date", split_axis=0, concat_axis=1, tiled=True).sum(1)
    network_mean = sums[:, :2] / (1.0 + sums[:, 2:3])
    return (interferograms, coherence, network_mean)


def solution(mesh):
    placed = (P("date", None, "strip", None), P("date", None), P())
    return jax.shard_map(
        on_device,
        mesh=mesh,
        in_specs=placed,
        out_specs=(
            P("date", None, None, "strip", None),
            P("date", None, "strip", None),
            P("date", None, "strip", None),
        ),
        check_vma=False,
    )
```

profile of v0, /device:TPU:0, one launch (start us, length us, event | category | flops | bytes accessed | tf_op | source)
XLA Modules:
  0.0 118.8 jit_solution(13078564321171893398)
XLA Ops:
  0.6 1.4 %slice.36 = bf16[3,2,256,384]{3,2,1,0:T(8,128)(2,1)S(1)} slice(bf16[8,2,256,384]{3,2,1,0:T(8,128)(2,1)} %param.3), slice={[0:3], [0:2], [0:256], [0:384]} | slice | bytes 2359296 | tf_op jit(solution)/shard_map/slice | solution.py:56
  2.0 5.5 %collective-permute-start = (bf16[3,2,256,384]{3,2,1,0:T(8,128)(2,1)S(1)}, bf16[3,2,256,384]{3,2,1,0:T(8,128)(2,1)S(1)}, u32[]{:S(2)}, u32[]{:S(2)}) collective-permute-start(bf16[3,2,256,384]{3,2,1,0:T(8,128)(2,1)S(1)} %slice.36), channel_id=1, source_target_pairs={{0,30},{2,0},{4,2},{6,4},{8,6},{10,8},{12,10},{14,12},{16,14},{18,... | collective-permute-start | bytes 3538952 | tf_op jit(solution)/shard_map/ppermute | solution.py:14
  7.5 0.8 compare_bitcast_fusion.5
  8.3 3.7 %fusion.47 = (f32[8,2,256,384]{3,2,1,0:T(8,128)S(1)}, bf16[11,2,256,384]{3,2,1,0:T(8,128)(2,1)S(1)}) fusion(bf16[8,2,256,384]{3,2,1,0:T(8,128)(2,1)} %param.3), kind=kLoop, calls=%fused_computation.82 | loop fusion | flops 1572863 | bytes 12582912 | tf_op jit(solution)/shard_map/convert_element_type | solution.py:32
  12.1 9.2 %collective-permute-done = bf16[3,2,256,384]{3,2,1,0:T(8,128)(2,1)S(1)} collective-permute-done((bf16[3,2,256,384]{3,2,1,0:T(8,128)(2,1)S(1)}, bf16[3,2,256,384]{3,2,1,0:T(8,128)(2,1)S(1)}, u32[]{:S(2)}, u32[]{:S(2)}) %collective-permute-start) | collective-permute-done | bytes 1179680 | tf_op jit(solution)/shard_map/ppermute | solution.py:14
  21.5 5.4 %select_convert_fusion.2 = (f32[8,2,256,384]{3,2,1,0:T(8,128)S(1)}, f32[8,2,256,384]{3,2,1,0:T(8,128)}, f32[8,2,256,384]{3,2,1,0:T(8,128)}) fusion(pred[8]{0:T(512)(128)(4,1)S(1)} %get-tuple-element.32, pred[8]{0:T(512)(128)(4,1)S(1)} %get-tuple-element.31, bf16[11,2,256,384]{3,2,1,0:T(8,128)(2,1)S(1)} %constant_dynamic-update-slice_fusion, ...), kind=kLoop, calls=%fused_computation.12 | loop fusion | flops 14155776 | bytes 28311600 | tf_op jit(solution)/shard_map/convert_element_type | solution.py:41
  26.9 4.0 %multiply_add_fusion.6 = (f32[8,1,256,384]{3,2,1,0:T(8,128)S(1)}, f32[8,1,256,384]{3,2,1,0:T(8,128)}, f32[8,1,256,384]{3,2,1,0:T(8,128)}, f32[8,1,256,384]{3,2,1,0:T(8,128)}) fusion(f32[8,2,256,384]{3,2,1,0:T(8,128)S(1)} %get-tuple-element.26, f32[8,2,256,384]{3,2,1,0:T(8,128)S(1)} %get-tuple-element.29), kind=kLoop, calls=%fused_computation.11 | loop fusion | flops 9437184 | bytes 25165824 | tf_op jit(solution)/shard_map/add | solution.py:42
  30.9 2.4 %reduce_sum.115 = f32[8,16,384]{2,1,0:T(8,128)S(1)} reduce(f32[8,16,16,384]{3,2,1,0:T(8,128)} %bitcast.97, f32[]{:T(128)} %constant.21.clone.1), dimensions={2}, to_apply=%region_6.7 | reduce | flops 737280 | bytes 3342340 | tf_op jit(solution)/shard_map/reduce_sum | solution.py:25
  33.3 3.1 %reduce_sum.110 = f32[8,16,384]{2,1,0:T(8,128)} reduce(f32[8,16,16,384]{3,2,1,0:T(8,128)} %bitcast.96, f32[]{:T(128)} %constant.21.clone.1), dimensions={2}, to_apply=%region_1.2 | reduce | flops 737280 | bytes 3342340 | tf_op jit(solution)/shard_map/reduce_sum | solution.py:25
  36.6 1.2 convolution_multiply_fusion.8
  37.8 0.5 reduce_sum.109
  38.3 0.9 convolution_multiply_fusion.9
  39.2 2.5 %reduce_sum.116 = f32[8,16,384]{2,1,0:T(8,128)S(1)} reduce(f32[8,16,16,384]{3,2,1,0:T(8,128)} %bitcast.91, f32[]{:T(128)} %constant.21.clone.1), dimensions={2}, to_apply=%region_7.8 | reduce | flops 737280 | bytes 3342340 | tf_op jit(solution)/shard_map/reduce_sum | solution.py:25
  41.7 5.0 %multiply_add_fusion = f32[8,1,256,384]{3,2,1,0:T(8,128)} fusion(f32[8,2,256,384]{3,2,1,0:T(8,128)} %get-tuple-element.28), kind=kLoop, calls=%fused_computation | loop fusion | flops 2359296 | bytes 9437184 | tf_op jit(solution)/shard_map/add | solution.py:45
  46.8 9.4 %multiply_add_fusion.5 = (f32[8,1,256,384]{3,2,1,0:T(8,128)}, f32[8,1,256,384]{3,2,1,0:T(8,128)}, f32[8,1,256,384]{3,2,1,0:T(8,128)}, f32[8,1,256,384]{3,2,1,0:T(8,128)}, f32[8,1,256,384]{3,2,1,0:T(8,128)}) fusion(f32[8,2,256,384]{3,2,1,0:T(8,128)} %get-tuple-element.27, f32[8,2,256,384]{3,2,1,0:T(8,128)S(1)} %bitcast.88, f32[8,2,256,384]{3,2,1,0:T(8,128)} %get-tuple-element.28), kind=kLoop, calls=%fused_computation.8 | loop fusion | flops 11796480 | bytes 34603008 | tf_op jit(solution)/shard_map/add | solution.py:42
  56.1 3.2 %reduce_sum.112 = f32[8,16,384]{2,1,0:T(8,128)} reduce(f32[8,16,16,384]{3,2,1,0:T(8,128)} %bitcast.95, f32[]{:T(128)} %constant.21.clone.1), dimensions={2}, to_apply=%region_3.4 | reduce | flops 737280 | bytes 3342340 | tf_op jit(solution)/shard_map/reduce_sum | solution.py:25
  59.4 1.8 %convolution_multiply_fusion.6 = f32[8,16,96]{2,1,0:T(8,128)} fusion(f32[8,16,384]{2,1,0:T(8,128)} %reduce_sum.112, s32[384]{0:T(512)S(1)} %add_select_fusion), kind=kOutput, calls=%fused_computation.23 | convolution fusion | flops 56672256 | bytes 247296 | tf_op jit(solution)/shard_map/nra,ab->nrb/dot_general | solution.py:26
  61.2 1.2 reduce_sum.111
  62.3 1.8 %convolution_multiply_fusion.7 = f32[8,16,96]{2,1,0:T(8,128)} fusion(f32[8,16,384]{2,1,0:T(8,128)} %reduce_sum.111, s32[384]{0:T(512)S(1)} %add_select_fusion), kind=kOutput, calls=%fused_computation.24 | convolution fusion | flops 56672256 | bytes 247296 | tf_op jit(solution)/shard_map/nra,ab->nrb/dot_general | solution.py:26
  64.1 3.2 %reduce_sum.117 = f32[8,16,384]{2,1,0:T(8,128)} reduce(f32[8,16,16,384]{3,2,1,0:T(8,128)} %bitcast.92, f32[]{:T(128)} %constant.21.clone.1), dimensions={2}, to_apply=%region_8.9 | reduce | flops 737280 | bytes 3342340 | tf_op jit(solution)/shard_map/reduce_sum | solution.py:25
  67.4 3.1 %reduce_sum.114 = f32[8,16,384]{2,1,0:T(8,128)} reduce(f32[8,16,16,384]{3,2,1,0:T(8,128)} %bitcast.90, f32[]{:T(128)} %constant.21.clone.1), dimensions={2}, to_apply=%region_5.6 | reduce | flops 737280 | bytes 3342340 | tf_op jit(solution)/shard_map/reduce_sum | solution.py:25
  70.4 1.2 convolution_multiply_fusion.4
  71.6 1.2 reduce_sum.113
  72.8 1.2 %convolution_multiply_fusion.5 = f32[8,16,96]{2,1,0:T(8,128)S(1)} fusion(f32[8,16,384]{2,1,0:T(8,128)} %reduce_sum.113, s32[384]{0:T(512)S(1)} %add_select_fusion), kind=kOutput, calls=%fused_computation.22 | convolution fusion | flops 56672256 | bytes 247296 | tf_op jit(solution)/shard_map/nra,ab->nrb/dot_general | solution.py:26
  74.1 2.4 %reduce_sum.118 = f32[8,16,384]{2,1,0:T(8,128)S(1)} reduce(f32[8,16,16,384]{3,2,1,0:T(8,128)} %bitcast.98, f32[]{:T(128)} %constant.21.clone.1), dimensions={2}, to_apply=%region_9.10 | reduce | flops 737280 | bytes 3342340 | tf_op jit(solution)/shard_map/reduce_sum | solution.py:25
  76.5 0.3 fusion.7
  76.8 0.3 fusion.12
  77.1 0.3 fusion.17
  77.4 0.7 copy-done.4
  78.1 0.4 copy.31
  78.6 1.3 %concatenate.10 = f32[24,1,16,16,6]{2,4,3,0,1:T(8,128)} reshape(f32[8,3,16,96]{2,3,1,0:T(8,128)S(1)} %copy.31) | data formatting | bytes 294912 | tf_op jit(solution)/shard_map/concatenate | solution.py:59
  79.9 1.0 copy.32
  80.9 0.9 maximum_bitcast_fusion.4
  81.8 1.0 maximum_bitcast_fusion.2
  82.8 1.2 %copy.33 = f32[8,3,2,16,96]{3,2,4,1,0:T(2,128)S(1)} copy(f32[8,3,2,16,96]{4,3,0,2,1:T(8,128)S(1)} %pad_maximum_fusion) | data formatting | bytes 589824 | tf_op jit(solution)/shard_map/stack | solution.py:51
  84.0 2.9 %copy.34 = f32[24,2,16,16,6]{0,3,4,2,1:T(8,128)} copy(f32[24,2,16,16,6]{2,1,4,3,0:T(2,128)S(1)} %bitcast.100) | data formatting | bytes 589824 | tf_op jit(solution)/shard_map/stack | solution.py:51
  87.0 2.4 %copy.36 = f32[24,1,16,16,6]{0,3,4,2,1:T(8,128)S(1)} copy(f32[24,1,16,16,6]{2,4,3,0,1:T(8,128)} %concatenate.10) | data formatting | bytes 294912 | tf_op jit(solution)/shard_map/concatenate | solution.py:59
  89.5 1.3 %fusion = f32[16,24,3,16,6]{1,0,4,3,2:T(8,128)S(1)} fusion(f32[24,1,16,16,6]{0,3,4,2,1:T(8,128)S(1)} %copy.36, f32[24,2,16,16,6]{0,3,4,2,1:T(8,128)S(1)} %broadcast_multiply_fusion, s32[16]{0:T(128)S(1)} %copy-done.13), kind=kOutput, calls=%fused_computation.14 | convolution fusion | flops 21344512 | bytes 884800 | tf_op jit(solution)/shard_map/st,tpcrw->spcrw/dot_general | solution.py:66
  90.9 1.4 %copy.48 = f32[16,24,3,16,6]{1,3,4,2,0:T(8,128)S(1)} copy(f32[16,24,3,16,6]{1,0,4,3,2:T(8,128)S(1)} %fusion) | data formatting | bytes 884736 | tf_op jit(solution)/shard_map/st,tpcrw->spcrw/dot_general | solution.py:66
  92.2 2.7 %reshape.187 = f32[16,1,6912]{2,1,0:T(1,128)} reshape(f32[16,3,6,16,24]{4,3,2,1,0:T(8,128)S(1)} %bitcast.99) | data formatting | bytes 884736
  94.9 6.0 %all-to-all-start = ((f32[16,1,6912]{2,1,0:T(1,128)}), f32[16,1,6912]{2,1,0:T(1,128)S(1)}, u32[]{:S(2)}, u32[]{:S(2)}) async-start(f32[16,1,6912]{2,1,0:T(1,128)} %reshape.187), calls=%async_computation | async-start | bytes 884736 | tf_op jit(solution)/shard_map/all_to_all | solution.py:67
  100.9 0.7 copy.42
  101.6 0.8 copy.41
  102.4 11.5 %all-to-all-done = f32[16,1,6912]{2,1,0:T(1,128)S(1)} async-done(((f32[16,1,6912]{2,1,0:T(1,128)}), f32[16,1,6912]{2,1,0:T(1,128)S(1)}, u32[]{:S(2)}, u32[]{:S(2)}) %all-to-all-start) | async-done | bytes 442400 | tf_op jit(solution)/shard_map/all_to_all | solution.py:67
  113.8 0.5 broadcast.116
  114.4 1.7 %reduce.3 = f32[16,6912]{1,0:T(8,128)S(1)} reduce(f32[16,1,6912]{2,1,0:T(1,128)S(1)} %all-to-all-done, f32[]{:T(128)} %broadcast.116), dimensions={1}, to_apply=%all_to_all.2.reduce_sub_computation | reduce | bytes 884740 | tf_op jit(solution)/shard_map/all_to_all | solution.py:67
  116.1 1.7 %reshape.188 = f32[16,3,6,16,24]{4,3,2,1,0:T(8,128)S(1)} reshape(f32[16,6912]{1,0:T(8,128)S(1)} %reduce.3) | data formatting | bytes 884736
  118.1 0.7 copy.43
  (43 shorter events, 1.3 us)
Async XLA Ops:
  2.0 19.2 %collective-permute-start = (bf16[3,2,256,384]{3,2,1,0:T(8,128)(2,1)S(1)}, bf16[3,2,256,384]{3,2,1,0:T(8,128)(2,1)S(1)}, u32[]{:S(2)}, u32[]{:S(2)}) collective-permute-start(bf16[3,2,256,384]{3,2,1,0:T(8,128)(2,1)S(1)} %slice.36), channel_id=1, source_target_pairs={{0,30},{2,0},{4,2},{6,4},{8,6},{10,8},{12,10},{14,12},{16,14},{18,... | collective-permute-start | bytes 3538952 | tf_op jit(solution)/shard_map/ppermute | solution.py:14
  12.0 14.9 %copy-start = (f32[8,2,256,384]{3,2,1,0:T(8,128)}, f32[8,2,256,384]{3,2,1,0:T(8,128)S(1)}, u32[]{:S(2)}) copy-start(f32[8,2,256,384]{3,2,1,0:T(8,128)S(1)} %get-tuple-element.29) | copy-start | bytes 18874372
  37.8 38.7 %copy-start.9 = (f32[8,16,96]{2,1,0:T(8,128)}, f32[8,16,96]{2,1,0:T(8,128)S(1)}, u32[]{:S(2)}) copy-start(f32[8,16,96]{2,1,0:T(8,128)S(1)} %convolution_multiply_fusion.8) | copy-start | bytes 147460
  39.2 7.6 %slice-start = ((s8[6291456]{0:T(1024)(128)(4,1)}), s8[2097152]{0:T(1024)(128)(4,1)S(1)}, s32[]{:S(2)}) async-start(s8[6291456]{0:T(1024)(128)(4,1)} %bitcast.87), calls=%async_computation.1 | async-start | bytes 4194304
  41.7 5.0 %slice-start.1 = ((s8[6291456]{0:T(1024)(128)(4,1)}), s8[4194304]{0:T(1024)(128)(4,1)S(1)}, s32[]{:S(2)}) async-start(s8[6291456]{0:T(1024)(128)(4,1)} %bitcast.87), calls=%async_computation.2 | async-start | bytes 8388608
  56.1 5.0 %copy-start.2 = (f32[8,1,256,384]{3,2,1,0:T(8,128)S(1)}, f32[8,1,256,384]{3,2,1,0:T(8,128)}, u32[]{:S(2)}) copy-start(f32[8,1,256,384]{3,2,1,0:T(8,128)} %get-tuple-element.17) | copy-start | bytes 9437188
  64.1 7.5 %copy-start.1 = (f32[8,1,256,384]{3,2,1,0:T(8,128)S(1)}, f32[8,1,256,384]{3,2,1,0:T(8,128)}, u32[]{:S(2)}) copy-start(f32[8,1,256,384]{3,2,1,0:T(8,128)} %get-tuple-element.25) | copy-start | bytes 9437188
  71.6 5.5 %copy-start.7 = (f32[8,16,96]{2,1,0:T(8,128)}, f32[8,16,96]{2,1,0:T(8,128)S(1)}, u32[]{:S(2)}) copy-start(f32[8,16,96]{2,1,0:T(8,128)S(1)} %convolution_multiply_fusion.4) | copy-start | bytes 147460
  72.8 3.7 %copy-start.10 = (f32[8,16,96]{2,1,0:T(8,128)S(1)}, f32[8,16,96]{2,1,0:T(8,128)}, u32[]{:S(2)}) copy-start(f32[8,16,96]{2,1,0:T(8,128)} %convolution_multiply_fusion.9) | copy-start | bytes 147460
  72.8 4.0 %copy-start.6 = (f32[8,16,384]{2,1,0:T(8,128)S(1)}, f32[8,16,384]{2,1,0:T(8,128)}, u32[]{:S(2)}) copy-start(f32[8,16,384]{2,1,0:T(8,128)} %reduce_sum.117) | copy-start | bytes 589828
  72.8 4.0 %copy-start.11 = (f32[8,16,96]{2,1,0:T(8,128)S(1)}, f32[8,16,96]{2,1,0:T(8,128)}, u32[]{:S(2)}) copy-start(f32[8,16,96]{2,1,0:T(8,128)} %convolution_multiply_fusion.6) | copy-start | bytes 147460
  72.8 4.0 %copy-start.12 = (f32[8,16,96]{2,1,0:T(8,128)S(1)}, f32[8,16,96]{2,1,0:T(8,128)}, u32[]{:S(2)}) copy-start(f32[8,16,96]{2,1,0:T(8,128)} %convolution_multiply_fusion.7) | copy-start | bytes 147460
  74.1 3.3 %copy-start.8 = (f32[8,16,96]{2,1,0:T(8,128)}, f32[8,16,96]{2,1,0:T(8,128)S(1)}, u32[]{:S(2)}) copy-start(f32[8,16,96]{2,1,0:T(8,128)S(1)} %convolution_multiply_fusion.5) | copy-start | bytes 147460
  77.4 0.7 copy-start.4
  87.0 2.4 %copy-start.3 = (f32[24,2,16,16,6]{0,3,4,2,1:T(8,128)S(1)}, f32[24,2,16,16,6]{0,3,4,2,1:T(8,128)}, u32[]{:S(2)}) copy-start(f32[24,2,16,16,6]{0,3,4,2,1:T(8,128)} %copy.34) | copy-start | bytes 884740
  87.0 2.5 %copy-start.13 = (s32[16]{0:T(128)S(1)}, s32[16]{0:T(128)}, u32[]{:S(2)}) copy-start(s32[16]{0:T(128)} %param.5) | copy-start | bytes 196
  90.8 10.1 %copy-start.5 = (f32[8,3,16,96]{3,2,0,1:T(8,128)S(1)}, f32[8,3,16,96]{3,2,0,1:T(8,128)}, u32[]{:S(2)}) copy-start(f32[8,3,16,96]{3,2,0,1:T(8,128)} %copy-done.4) | copy-start | bytes 442372
  94.9 18.9 %all-to-all-start = ((f32[16,1,6912]{2,1,0:T(1,128)}), f32[16,1,6912]{2,1,0:T(1,128)S(1)}, u32[]{:S(2)}, u32[]{:S(2)}) async-start(f32[16,1,6912]{2,1,0:T(1,128)} %reshape.187), calls=%async_computation | async-start | bytes 884736 | tf_op jit(solution)/shard_map/all_to_all | solution.py:67
where the time goes:
time: 119 us
  other arithmetic  55.1 us (46%)
  waiting for transfers between devices  20.6 us (17%)
  local copies, waits for them, and re-layouts  20.2 us (17%)
  starting transfers between devices  11.5 us (10%)
  matrix products  10.4 us (9%)
    reduce_sum x10, other arithmetic, looks(): ranged = field.reshape(count, rows // LR, LR, cols).sum(2)  22.8 us
    add x2, other arithmetic, pair_block(): real_part = looks(own[:, 0] * other[:, 0] + own[:, 1] * other[:, 1], pool)  13.3 us
    all_to_all x1, waiting for transfers between devices, on_device(): lax.all_to_all(slotted, 'date', split_axis=0, concat_axis=1, tiled=True)  11.5 us
    ppermute x1, waiting for transfers between devices, shifted(): return lax.ppermute(value, axis, pairs)  9.19 us
    dot_general x10, matrix products, looks(): jnp.einsum('nra,ab->nrb', ranged, pool, precision=lax.Precision.HIGHEST)  9.11 us
    unnamed x38, local copies, waits for them, and re-layouts  7.37 us
    all_to_all x1, starting transfers between devices, on_device(): lax.all_to_all(slotted, 'date', split_axis=0, concat_axis=1, tiled=True)  5.98 us
    ppermute x1, starting transfers between devices, shifted(): return lax.ppermute(value, axis, pairs)  5.5 us
  transfers between devices with their start and end apart: 2, of which 2 were waited for; matrix products, arithmetic and copies ran while one was open for 5% of the time, Pallas kernels for 0%

commit v1 on v0

v1 whole, which is shorter than its diff:
```python
import jax
import jax.numpy as jnp
from jax import lax
from jax.experimental import pallas as pl
from jax.experimental.pallas import tpu as pltpu
from jax.sharding import PartitionSpec as P

NB = 3
LR = 16
LA = 4


def shifted(value, axis, steps):
    count = lax.axis_size(axis)
    pairs = [(source, (source + steps) % count) for source in range(count)]
    return lax.ppermute(value, axis, pairs)


def split_pool(field, pool):
    hi = field.astype(jnp.bfloat16)
    rest = field - hi.astype(jnp.float32)
    mid = rest.astype(jnp.bfloat16)
    lo = (rest - mid.astype(jnp.float32)).astype(jnp.bfloat16)
    out = jnp.dot(hi, pool, preferred_element_type=jnp.float32)
    out = out + jnp.dot(mid, pool, preferred_element_type=jnp.float32)
    return out + jnp.dot(lo, pool, preferred_element_type=jnp.float32)


def make_kernel(count, rim_count, rows, cols):
    groups = rows // LR
    cells = cols // LA
    total = count + rim_count
    ctiles = cols // 128

    def kernel(off_ref, slc_ref, rim_ref, ifg_ref, coh_ref, ws_ref, xf, pacc, racc, pw):
        def conv_own(j, c):
            for ct in range(ctiles):
                xf[j, :, ct] = slc_ref[j, :, :, pl.ds(ct * 128, 128)].astype(jnp.float32)
            return c

        lax.fori_loop(0, count, conv_own, 0)

        def conv_rim(j, c):
            for ct in range(ctiles):
                xf[count + j, :, ct] = rim_ref[j, :, :, pl.ds(ct * 128, 128)].astype(jnp.float32)
            return c

        lax.fori_loop(0, rim_count, conv_rim, 0)

        lines = lax.broadcasted_iota(jnp.int32, (cols, cells), 0)
        cell = lax.broadcasted_iota(jnp.int32, (cols, cells), 1)
        pool = jnp.where(lines // LA == cell, 1.0 / (LR * LA), 0.0).astype(jnp.bfloat16)

        def strided(j, comp, s, ct):
            return xf[j, comp, ct, pl.ds(s, groups, stride=LR), :]

        def power(j, c):
            for ct in range(ctiles):
                acc = jnp.zeros((groups, 128), jnp.float32)
                for s in range(LR):
                    x0 = strided(j, 0, s, ct)
                    x1 = strided(j, 1, s, ct)
                    acc = acc + (x0 * x0 + x1 * x1)
                pacc[j, :, pl.ds(ct * 128, 128)] = acc
            return c

        lax.fori_loop(0, total, power, 0)
        pw[...] = split_pool(pacc[...].reshape(total * groups, cols), pool).reshape(total, groups, cells)

        def pairs(i, c):
            parts = [jnp.clip(i + off_ref[i, k], 0, total - 1) for k in range(NB)]
            for ct in range(ctiles):
                re = [jnp.zeros((groups, 128), jnp.float32) for _ in range(NB)]
                im = [jnp.zeros((groups, 128), jnp.float32) for _ in range(NB)]
                for s in range(LR):
                    a0 = strided(i, 0, s, ct)
                    a1 = strided(i, 1, s, ct)
                    for k in range(NB):
                        b0 = strided(parts[k], 0, s, ct)
                        b1 = strided(parts[k], 1, s, ct)
                        re[k] = re[k] + (a0 * b0 + a1 * b1)
                        im[k] = im[k] + (a1 * b0 - a0 * b1)
                for k in range(NB):
                    racc[i, k, 0, :, pl.ds(ct * 128, 128)] = re[k]
                    racc[i, k, 1, :, pl.ds(ct * 128, 128)] = im[k]
            return c

        lax.fori_loop(0, count, pairs, 0)
        pooled = split_pool(racc[...].reshape(count * NB * 2 * groups, cols), pool)
        ifg_ref[...] = pooled.reshape(count, NB, 2, groups, cells)

        def coher(i, ws):
            wr, wi, wc = ws
            pa = pw[i]
            for k in range(NB):
                j = jnp.clip(i + off_ref[i, k], 0, total - 1)
                pb = pw[j]
                re = ifg_ref[i, k, 0]
                im = ifg_ref[i, k, 1]
                co = jnp.sqrt(re * re + im * im) / jnp.sqrt(pa * pb + 1e-06)
                coh_ref[i, k] = co
                wr = wr + co * re
                wi = wi + co * im
                wc = wc + co
            return (wr, wi, wc)

        zero = jnp.zeros((groups, cells), jnp.float32)
        wr, wi, wc = lax.fori_loop(0, count, coher, (zero, zero, zero))
        ws_ref[0] = wr
        ws_ref[1] = wi
        ws_ref[2] = wc

    return kernel


def local_math(slc, rim, offsets):
    count, _, rows, cols = slc.shape
    rim_count = rim.shape[0]
    groups = rows // LR
    cells = cols // LA
    total = count + rim_count
    vmem = pltpu.VMEM
    return pl.pallas_call(
        make_kernel(count, rim_count, rows, cols),
        out_shape=(
            jax.ShapeDtypeStruct((count, NB, 2, groups, cells), jnp.float32),
            jax.ShapeDtypeStruct((count, NB, groups, cells), jnp.float32),
            jax.ShapeDtypeStruct((3, groups, cells), jnp.float32),
        ),
        in_specs=[
            pl.BlockSpec(memory_space=pltpu.SMEM),
            pl.BlockSpec(memory_space=vmem),
            pl.BlockSpec(memory_space=vmem),
        ],
        out_specs=(
            pl.BlockSpec(memory_space=vmem),
            pl.BlockSpec(memory_space=vmem),
            pl.BlockSpec(memory_space=vmem),
        ),
        scratch_shapes=[
            pltpu.VMEM((total, 2, cols // 128, rows, 128), jnp.float32),
            pltpu.VMEM((total, groups, cols), jnp.float32),
            pltpu.VMEM((count, NB, 2, groups, cols), jnp.float32),
            pltpu.VMEM((total, groups, cells), jnp.float32),
        ],
        compiler_params=pltpu.CompilerParams(vmem_limit_bytes=48 * 1024 * 1024),
    )(offsets, slc, rim)


def on_device(slc, offsets, owner):
    rim = shifted(slc[:NB], "date", -1)
    interferograms, coherence, ws = local_math(slc, rim, offsets)
    tile_count = owner.shape[0]
    rows_loc = ws.shape[1]
    width = ws.shape[2] // tile_count
    tiles = ws.reshape(3, rows_loc, tile_count, width).transpose(2, 0, 1, 3)
    slotted = jnp.zeros_like(tiles).at[owner].set(tiles)
    sums = lax.all_to_all(slotted, "date", split_axis=0, concat_axis=0, tiled=True).sum(0)
    network_mean = (sums[:2] / (1.0 + sums[2:3]))[None]
    return (interferograms, coherence, network_mean)


def solution(mesh):
    placed = (P("date", None, "strip", None), P("date", None), P())
    return jax.shard_map(
        on_device,
        mesh=mesh,
        in_specs=placed,
        out_specs=(
            P("date", None, None, "strip", None),
            P("date", None, "strip", None),
            P("date", None, "strip", None),
        ),
        check_vma=False,
    )
```

time: 119 us -> 51.8 us (0.44)
  other arithmetic: 55.1 us -> 0.74 us
  local copies, waits for them, and re-layouts: 20.2 us -> 5.91 us
  Pallas kernels: 0 us -> 12.7 us
  blocking collectives: 0 us -> 12.4 us
  matrix products: 10.4 us -> 0 us
  waiting for transfers between devices: 20.6 us -> 13.6 us
  starting transfers between devices: 11.5 us -> 5.5 us
    reduce_sum x11 -> x1, other arithmetic: 23 us -> 0.02 us  [on_device(): lax.all_to_all(slotted, 'date', split_axis=0, concat_axis=0, tiled=True)]
    add x3 -> x0, other arithmetic: 18.4 us -> none  [the longest x2 13.3 us: pair_block(): real_part = looks(own[:, 0] * other[:, 0] + own[:, 1] * other[:, 1], pool)]
    pallas_call x0 -> x1, Pallas kernels: none -> 12.7 us  [local_math(): pl.pallas_call(make_kernel(count, rim_count, rows, cols), out_shape=(jax....]
    all_to_all x0 -> x1, blocking collectives: none -> 12.4 us  [on_device(): lax.all_to_all(slotted, 'date', split_axis=0, concat_axis=0, tiled=True)]
    all_to_all x1 -> x0, waiting for transfers between devices: 11.5 us -> none  [on_device(): lax.all_to_all(slotted, 'date', split_axis=0, concat_axis=1, tiled=True)]
    dot_general x11 -> x0, matrix products: 10.4 us -> none  [the longest x10 9.11 us: looks(): jnp.einsum('nra,ab->nrb', ranged, pool, precision=lax.Precision.HIGHEST)]
    convert_element_type x2 -> x0, other arithmetic: 9.12 us -> none  [the longest x1 5.41 us: pair_block(): other = chosen.astype(jnp.float32)]
    all_to_all x1 -> x0, starting transfers between devices: 5.98 us -> none  [on_device(): lax.all_to_all(slotted, 'date', split_axis=0, concat_axis=1, tiled=True)]
  transfers between devices with their start and end apart: 2 -> 1, of which waited for: 2 -> 1; matrix products, arithmetic and copies ran while one was open for 5% -> 0% of each run, Pallas kernels for 0% -> 0%
where the time goes in v1:
time: 51.8 us; the launch traced here: 51.6 us
  waiting for transfers between devices  13.6 us (26%)
  Pallas kernels  12.7 us (25%)
  blocking collectives  12.4 us (24%)
  local copies, waits for them, and re-layouts  5.91 us (11%)
  starting transfers between devices  5.5 us (11%)
  other arithmetic  0.74 us (1%)
  between operations  0.74 us (1%)
    ppermute x1, waiting for transfers between devices, shifted(): return lax.ppermute(value, axis, pairs)  13.6 us
    pallas_call x1, Pallas kernels, local_math(): pl.pallas_call(make_kernel(count, rim_count, rows, cols), out_shape=(jax....  12.7 us
    all_to_all x1, blocking collectives, on_device(): lax.all_to_all(slotted, 'date', split_axis=0, concat_axis=0, tiled=True)  12.4 us
    ppermute x1, starting transfers between devices, shifted(): return lax.ppermute(value, axis, pairs)  5.5 us
    unnamed x10, local copies, waits for them, and re-layouts  2.8 us
    slice x1, local copies, waits for them, and re-layouts, on_device(): rim = shifted(slc[:NB], 'date', -1)  1.4 us
    scatter x1, local copies, waits for them, and re-layouts, on_device(): slotted = jnp.zeros_like(tiles).at[owner].set(tiles)  1.04 us
  transfers between devices with their start and end apart: 1, of which 1 were waited for; matrix products, arithmetic and copies ran while one was open for 0% of the time, Pallas kernels for 0%

profile of v1, /device:TPU:0, one launch (start us, length us, event | category | flops | bytes accessed | tf_op | source)
XLA Modules:
  0.0 51.6 jit_solution(14460403272461819153)
XLA Ops:
  0.6 0.0 copy-start.1
  0.6 0.0 copy-start.2
  0.7 1.4 %slice.9 = bf16[3,2,256,384]{3,2,1,0:T(8,128)(2,1)S(1)} slice(bf16[8,2,256,384]{3,2,1,0:T(8,128)(2,1)} %slc_ref.1), slice={[0:3], [0:2], [0:256], [0:384]} | slice | bytes 2359296 | tf_op jit(solution)/shard_map/slice | solution.py:151
  2.1 5.5 %collective-permute-start = (bf16[3,2,256,384]{3,2,1,0:T(8,128)(2,1)S(1)}, bf16[3,2,256,384]{3,2,1,0:T(8,128)(2,1)S(1)}, u32[]{:S(2)}, u32[]{:S(2)}) collective-permute-start(bf16[3,2,256,384]{3,2,1,0:T(8,128)(2,1)S(1)} %slice.9), channel_id=1, source_target_pairs={{0,30},{2,0},{4,2},{6,4},{8,6},{10,8},{12,10},{14,12},{16,14},{18,... | collective-permute-start | bytes 3538952 | tf_op jit(solution)/shard_map/ppermute | solution.py:16
  7.6 0.0 copy-done.1
  7.6 0.1 copy.9.off_ref
  7.6 0.0 copy-done.2
  7.6 13.6 %collective-permute-done.rim_ref = bf16[3,2,256,384]{3,2,1,0:T(8,128)(2,1)S(1)} collective-permute-done((bf16[3,2,256,384]{3,2,1,0:T(8,128)(2,1)S(1)}, bf16[3,2,256,384]{3,2,1,0:T(8,128)(2,1)S(1)}, u32[]{:S(2)}, u32[]{:S(2)}) %collective-permute-start) | collective-permute-done | bytes 1179680 | tf_op jit(solution)/shard_map/ppermute | solution.py:16
  21.3 0.0 copy-start
  21.3 1.9 %copy-done = bf16[8,2,256,384]{3,2,1,0:T(8,128)(2,1)S(1)} copy-done((bf16[8,2,256,384]{3,2,1,0:T(8,128)(2,1)S(1)}, bf16[8,2,256,384]{3,2,1,0:T(8,128)(2,1)}, u32[]{:S(2)}) %copy-start) | copy-done | bytes 3145752
  23.2 12.7 %shard_map.58 = (f32[8,3,2,16,96]{4,3,2,1,0:T(8,128)}, f32[8,3,16,96]{3,2,1,0:T(8,128)}, f32[3,16,96]{2,1,0:T(8,128)S(1)}) custom-call(s32[8,3]{1,0:T(8,128)S(1)} %copy.9.off_ref, bf16[8,2,256,384]{3,2,1,0:T(8,128)(2,1)S(1)} %copy-done, bf16[3,2,256,384]{3,2,1,0:T(8,128)(2,1)S(1)} %collective-permute-done.rim_ref), custom_call_target="tpu_custom_call" | custom-call | tf_op jit(solution)/shard_map/pallas_call | solution.py:123
  35.9 0.1 copy.10
  36.0 1.0 %scatter_fusion = f32[16,3,16,6]{2,3,1,0:T(8,128)S(1)} fusion(f32[16,3,16,6]{2,3,1,0:T(8,128)S(1)} %broadcast_in_dim.9, s32[16]{0:T(128)S(1)} %compare_select_fusion, f32[16,3,16,6]{2,3,1,0:T(8,128)S(1)} %copy.11), kind=kCustom, calls=%fused_computation | custom fusion | bytes 55360 | tf_op jit(solution)/shard_map/scatter | solution.py:157
  37.1 0.1 reshape.19
  37.2 12.4 %all_to_all.5 = f32[16,1,288]{2,1,0:T(1,128)S(1)} all-to-all(f32[16,1,288]{2,1,0:T(1,128)S(1)} %reshape.19), channel_id=1, replica_groups=mesh['date'=16,'strip'=2] {'date'}, dimensions={0} | all-to-all | bytes 36864 | tf_op jit(solution)/shard_map/all_to_all | solution.py:158
  49.6 0.5 broadcast.10
  50.1 0.7 %reduce = f32[16,288]{1,0:T(8,128)S(1)} reduce(f32[16,1,288]{2,1,0:T(1,128)S(1)} %all_to_all.5, f32[]{:T(128)} %broadcast.10), dimensions={1}, to_apply=%all_to_all.3.reduce_sub_computation | reduce | bytes 36868 | tf_op jit(solution)/shard_map/all_to_all | solution.py:158
  50.8 0.1 reshape.20
  51.0 0.6 %copy.12 = f32[1,2,16,6]{2,1,3,0:T(2,128)} copy(f32[1,2,16,6]{2,3,1,0:T(8,128)S(1)} %fusion) | data formatting | bytes 1536
  (7 shorter events, 0.1 us)
Async XLA Ops:
  0.6 6.9 %copy-start.1 = (s32[8,3]{0,1:T(4,128)S(1)}, s32[8,3]{0,1:T(4,128)}, u32[]{:S(2)}) copy-start(s32[8,3]{0,1:T(4,128)} %param.4) | copy-start | bytes 292
  0.6 7.0 %copy-start.2 = (s32[16]{0:T(128)S(1)}, s32[16]{0:T(128)}, u32[]{:S(2)}) copy-start(s32[16]{0:T(128)} %param.5) | copy-start | bytes 196
  2.1 19.2 %collective-permute-start = (bf16[3,2,256,384]{3,2,1,0:T(8,128)(2,1)S(1)}, bf16[3,2,256,384]{3,2,1,0:T(8,128)(2,1)S(1)}, u32[]{:S(2)}, u32[]{:S(2)}) collective-permute-start(bf16[3,2,256,384]{3,2,1,0:T(8,128)(2,1)S(1)} %slice.9), channel_id=1, source_target_pairs={{0,30},{2,0},{4,2},{6,4},{8,6},{10,8},{12,10},{14,12},{16,14},{18,... | collective-permute-start | bytes 3538952 | tf_op jit(solution)/shard_map/ppermute | solution.py:16
  21.3 1.9 %copy-start = (bf16[8,2,256,384]{3,2,1,0:T(8,128)(2,1)S(1)}, bf16[8,2,256,384]{3,2,1,0:T(8,128)(2,1)}, u32[]{:S(2)}) copy-start(bf16[8,2,256,384]{3,2,1,0:T(8,128)(2,1)} %slc_ref.1) | copy-start | bytes 9437188

commit v2 on v1

--- a/solution.py
+++ b/solution.py
@@ -26,26 +26,24 @@
     return out + jnp.dot(lo, pool, preferred_element_type=jnp.float32)
 
 
-def make_kernel(count, rim_count, rows, cols):
+def make_kernel(images, first, dates, rows, cols):
     groups = rows // LR
     cells = cols // LA
-    total = count + rim_count
+    total = len(images)
     ctiles = cols // 128
 
-    def kernel(off_ref, slc_ref, rim_ref, ifg_ref, coh_ref, ws_ref, xf, pacc, racc, pw):
-        def conv_own(j, c):
+    def kernel(off_ref, *refs):
+        srcs = refs[:-9]
+        ifg_ref, coh_ref, ws_ref, raw, xf, pacc, racc, pw, sem = refs[-9:]
+        copies = []
+        for t, (src, lead) in enumerate(images):
+            cp = pltpu.make_async_copy(srcs[src].at[lead], raw.at[t], sem.at[t])
+            cp.start()
+            copies.append(cp)
+        for t in range(total):
+            copies[t].wait()
             for ct in range(ctiles):
-                xf[j, :, ct] = slc_ref[j, :, :, pl.ds(ct * 128, 128)].astype(jnp.float32)
-            return c
-
-        lax.fori_loop(0, count, conv_own, 0)
-
-        def conv_rim(j, c):
-            for ct in range(ctiles):
-                xf[count + j, :, ct] = rim_ref[j, :, :, pl.ds(ct * 128, 128)].astype(jnp.float32)
-            return c
-
-        lax.fori_loop(0, rim_count, conv_rim, 0)
+                xf[t, :, ct] = raw[t, :, :, pl.ds(ct * 128, 128)].astype(jnp.float32)
 
         lines = lax.broadcasted_iota(jnp.int32, (cols, cells), 0)
         cell = lax.broadcasted_iota(jnp.int32, (cols, cells), 1)
@@ -67,14 +65,17 @@
         lax.fori_loop(0, total, power, 0)
         pw[...] = split_pool(pacc[...].reshape(total * groups, cols), pool).reshape(total, groups, cells)
 
+        def partner(i, k):
+            return jnp.clip(first + i + off_ref[i, k], 0, total - 1)
+
         def pairs(i, c):
-            parts = [jnp.clip(i + off_ref[i, k], 0, total - 1) for k in range(NB)]
+            parts = [partner(i, k) for k in range(NB)]
             for ct in range(ctiles):
                 re = [jnp.zeros((groups, 128), jnp.float32) for _ in range(NB)]
                 im = [jnp.zeros((groups, 128), jnp.float32) for _ in range(NB)]
                 for s in range(LR):
-                    a0 = strided(i, 0, s, ct)
-                    a1 = strided(i, 1, s, ct)
+                    a0 = strided(first + i, 0, s, ct)
+                    a1 = strided(first + i, 1, s, ct)
                     for k in range(NB):
                         b0 = strided(parts[k], 0, s, ct)
                         b1 = strided(parts[k], 1, s, ct)
@@ -85,16 +86,15 @@
                     racc[i, k, 1, :, pl.ds(ct * 128, 128)] = im[k]
             return c
 
-        lax.fori_loop(0, count, pairs, 0)
-        pooled = split_pool(racc[...].reshape(count * NB * 2 * groups, cols), pool)
-        ifg_ref[...] = pooled.reshape(count, NB, 2, groups, cells)
+        lax.fori_loop(0, dates, pairs, 0)
+        pooled = split_pool(racc[...].reshape(dates * NB * 2 * groups, cols), pool)
+        ifg_ref[...] = pooled.reshape(dates, NB, 2, groups, cells)
 
         def coher(i, ws):
             wr, wi, wc = ws
-            pa = pw[i]
+            pa = pw[first + i]
             for k in range(NB):
-                j = jnp.clip(i + off_ref[i, k], 0, total - 1)
-                pb = pw[j]
+                pb = pw[partner(i, k)]
                 re = ifg_ref[i, k, 0]
                 im = ifg_ref[i, k, 1]
                 co = jnp.sqrt(re * re + im * im) / jnp.sqrt(pa * pb + 1e-06)
@@ -105,7 +105,7 @@
             return (wr, wi, wc)
 
         zero = jnp.zeros((groups, cells), jnp.float32)
-        wr, wi, wc = lax.fori_loop(0, count, coher, (zero, zero, zero))
+        wr, wi, wc = lax.fori_loop(0, dates, coher, (zero, zero, zero))
         ws_ref[0] = wr
         ws_ref[1] = wi
         ws_ref[2] = wc
@@ -113,43 +113,55 @@
     return kernel
 
 
-def local_math(slc, rim, offsets):
-    count, _, rows, cols = slc.shape
-    rim_count = rim.shape[0]
+def local_math(offsets, sources, images, first, dates):
+    _, _, rows, cols = sources[0].shape
     groups = rows // LR
     cells = cols // LA
-    total = count + rim_count
+    total = len(images)
     vmem = pltpu.VMEM
     return pl.pallas_call(
-        make_kernel(count, rim_count, rows, cols),
+        make_kernel(images, first, dates, rows, cols),
         out_shape=(
-            jax.ShapeDtypeStruct((count, NB, 2, groups, cells), jnp.float32),
-            jax.ShapeDtypeStruct((count, NB, groups, cells), jnp.float32),
+            jax.ShapeDtypeStruct((dates, NB, 2, groups, cells), jnp.float32),
+            jax.ShapeDtypeStruct((dates, NB, groups, cells), jnp.float32),
             jax.ShapeDtypeStruct((3, groups, cells), jnp.float32),
         ),
-        in_specs=[
-            pl.BlockSpec(memory_space=pltpu.SMEM),
-            pl.BlockSpec(memory_space=vmem),
-            pl.BlockSpec(memory_space=vmem),
-        ],
+        in_specs=[pl.BlockSpec(memory_space=pltpu.SMEM)]
+        + [pl.BlockSpec(memory_space=pl.ANY) for _ in sources],
         out_specs=(
             pl.BlockSpec(memory_space=vmem),
             pl.BlockSpec(memory_space=vmem),
             pl.BlockSpec(memory_space=vmem),
         ),
         scratch_shapes=[
+            pltpu.VMEM((total, 2, rows, cols), jnp.bfloat16),
             pltpu.VMEM((total, 2, cols // 128, rows, 128), jnp.float32),
             pltpu.VMEM((total, groups, cols), jnp.float32),
-            pltpu.VMEM((count, NB, 2, groups, cols), jnp.float32),
+            pltpu.VMEM((dates, NB, 2, groups, cols), jnp.float32),
             pltpu.VMEM((total, groups, cells), jnp.float32),
+            pltpu.SemaphoreType.DMA((total,)),
         ],
         compiler_params=pltpu.CompilerParams(vmem_limit_bytes=48 * 1024 * 1024),
-    )(offsets, slc, rim)
+    )(offsets, *sources)
 
 
 def on_device(slc, offsets, owner):
+    count = slc.shape[0]
+    inner = count - NB
     rim = shifted(slc[:NB], "date", -1)
-    interferograms, coherence, ws = local_math(slc, rim, offsets)
+    ifg_a, coh_a, ws_a = local_math(
+        offsets[:inner], [slc], [(0, t) for t in range(count)], 0, inner
+    )
+    ifg_b, coh_b, ws_b = local_math(
+        offsets[inner:],
+        [slc, rim],
+        [(0, inner + t) for t in range(NB)] + [(1, t) for t in range(NB)],
+        0,
+        NB,
+    )
+    interferograms = jnp.concatenate([ifg_a, ifg_b], 0)
+    coherence = jnp.concatenate([coh_a, coh_b], 0)
+    ws = ws_a + ws_b
     tile_count = owner.shape[0]
     rows_loc = ws.shape[1]
     width = ws.shape[2] // tile_count

time: 51.8 us -> 44.7 us (0.86)
  blocking collectives: 12.4 us -> 0 us
  waiting for transfers between devices: 13.6 us -> 7 us
  starting transfers between devices: 5.5 us -> 11.5 us
  Pallas kernels: 12.7 us -> 16.3 us
  other arithmetic: 0.74 us -> 2.22 us
  local copies, waits for them, and re-layouts: 5.91 us -> 6.69 us
    all_to_all x1 -> x0, blocking collectives: 12.4 us -> none  [on_device(): lax.all_to_all(slotted, 'date', split_axis=0, concat_axis=0, tiled=True)]
    ppermute x1, waiting for transfers between devices: 13.6 us -> 1.91 us  [shifted(): return lax.ppermute(value, axis, pairs)]
    all_to_all x0 -> x1, starting transfers between devices: none -> 5.99 us  [on_device(): lax.all_to_all(slotted, 'date', split_axis=0, concat_axis=0, tiled=True)]
    all_to_all x0 -> x1, waiting for transfers between devices: none -> 5.09 us  [on_device(): lax.all_to_all(slotted, 'date', split_axis=0, concat_axis=0, tiled=True)]
    pallas_call x1 -> x2, Pallas kernels: 12.7 us -> 16.3 us  [local_math(): pl.pallas_call(make_kernel(images, first, dates, rows, cols), out_shape=(...]
    concatenate x0 -> x2, other arithmetic: none -> 1.48 us  [the longest x1 0.78 us: on_device(): interferograms = jnp.concatenate([ifg_a, ifg_b], 0)]
    unnamed x10 -> x13, local copies, waits for them, and re-layouts: 2.8 us -> 3.51 us
  transfers between devices with their start and end apart: 1 -> 2, of which waited for: 1 -> 2; matrix products, arithmetic and copies ran while one was open for 0% -> 4% of each run, Pallas kernels for 0% -> 22%
where the time goes in v2:
time: 44.7 us; the launch traced here: 44.5 us
  Pallas kernels  16.3 us (36%)
  starting transfers between devices  11.5 us (26%)
  waiting for transfers between devices  7 us (16%)
  local copies, waits for them, and re-layouts  6.69 us (15%)
  other arithmetic  2.22 us (5%)
  between operations  0.77 us (2%)
    pallas_call x2, Pallas kernels, local_math(): pl.pallas_call(make_kernel(images, first, dates, rows, cols), out_shape=(...  16.3 us
    all_to_all x1, starting transfers between devices, on_device(): lax.all_to_all(slotted, 'date', split_axis=0, concat_axis=0, tiled=True)  5.99 us
    ppermute x1, starting transfers between devices, shifted(): return lax.ppermute(value, axis, pairs)  5.5 us
    all_to_all x1, waiting for transfers between devices, on_device(): lax.all_to_all(slotted, 'date', split_axis=0, concat_axis=0, tiled=True)  5.09 us
    unnamed x13, local copies, waits for them, and re-layouts  3.51 us
    ppermute x1, waiting for transfers between devices, shifted(): return lax.ppermute(value, axis, pairs)  1.91 us
    slice x1, local copies, waits for them, and re-layouts, on_device(): rim = shifted(slc[:NB], 'date', -1)  1.4 us
    scatter x1, local copies, waits for them, and re-layouts, on_device(): slotted = jnp.zeros_like(tiles).at[owner].set(tiles)  1.04 us
  transfers between devices with their start and end apart: 2, of which 2 were waited for; matrix products, arithmetic and copies ran while one was open for 4% of the time, Pallas kernels for 22%

profile of v2, /device:TPU:0, one launch (start us, length us, event | category | flops | bytes accessed | tf_op | source)
XLA Modules:
  0.0 44.5 jit_solution(12392098831303978999)
XLA Ops:
  0.6 0.0 copy-start.2
  0.6 1.4 %slice.17 = bf16[3,2,256,384]{3,2,1,0:T(8,128)(2,1)S(1)} slice(bf16[8,2,256,384]{3,2,1,0:T(8,128)(2,1)} %refs_0_.3), slice={[0:3], [0:2], [0:256], [0:384]} | slice | bytes 2359296 | tf_op jit(solution)/shard_map/slice | solution.py:151
  2.0 5.5 %collective-permute-start = (bf16[3,2,256,384]{3,2,1,0:T(8,128)(2,1)S(1)}, bf16[3,2,256,384]{3,2,1,0:T(8,128)(2,1)S(1)}, u32[]{:S(2)}, u32[]{:S(2)}) collective-permute-start(bf16[3,2,256,384]{3,2,1,0:T(8,128)(2,1)S(1)} %slice.17), channel_id=1, source_target_pairs={{0,30},{2,0},{4,2},{6,4},{8,6},{10,8},{12,10},{14,12},{16,14},{18,... | collective-permute-start | bytes 3538952 | tf_op jit(solution)/shard_map/ppermute | solution.py:16
  7.5 0.0 copy-done.2
  7.5 0.1 slice.16
  7.6 0.1 copy.16.off_ref
  7.7 0.1 copy.15.off_ref
  7.8 0.0 copy-start
  7.8 1.9 %copy-done = bf16[8,2,256,384]{3,2,1,0:T(8,128)(2,1)S(1)} copy-done((bf16[8,2,256,384]{3,2,1,0:T(8,128)(2,1)S(1)}, bf16[8,2,256,384]{3,2,1,0:T(8,128)(2,1)}, u32[]{:S(2)}) %copy-start) | copy-done | bytes 3145752
  9.7 0.0 copy-start.3
  9.7 0.0 copy-start.1
  9.7 9.6 %shard_map.58 = (f32[5,3,2,16,96]{4,3,2,1,0:T(8,128)S(1)}, f32[5,3,16,96]{3,2,1,0:T(8,128)S(1)}, f32[3,16,96]{2,1,0:T(8,128)S(1)}) custom-call(s32[5,3]{1,0:T(8,128)S(1)} %copy.15.off_ref, bf16[8,2,256,384]{3,2,1,0:T(8,128)(2,1)S(1)} %copy-done), custom_call_target="tpu_custom_call" | custom-call | tf_op jit(solution)/shard_map/pallas_call | solution.py:122
  19.3 0.0 copy-done.3
  19.3 1.9 %collective-permute-done.refs_1_ = bf16[3,2,256,384]{3,2,1,0:T(8,128)(2,1)S(1)} collective-permute-done((bf16[3,2,256,384]{3,2,1,0:T(8,128)(2,1)S(1)}, bf16[3,2,256,384]{3,2,1,0:T(8,128)(2,1)S(1)}, u32[]{:S(2)}, u32[]{:S(2)}) %collective-permute-start) | collective-permute-done | bytes 1179680 | tf_op jit(solution)/shard_map/ppermute | solution.py:16
  21.3 0.0 copy-done.1
  21.3 6.7 %shard_map.59 = (f32[3,3,2,16,96]{4,3,2,1,0:T(8,128)S(1)}, f32[3,3,16,96]{3,2,1,0:T(8,128)S(1)}, f32[3,16,96]{2,1,0:T(8,128)S(1)}) custom-call(s32[3,3]{1,0:T(4,128)S(1)} %copy.16.off_ref, bf16[8,2,256,384]{3,2,1,0:T(8,128)(2,1)S(1)} %copy-done.1, bf16[3,2,256,384]{3,2,1,0:T(8,128)(2,1)S(1)} %collective-permute-done.refs_1_), custom_call_target="tpu_custom_call" | custom-call | tf_op jit(solution)/shard_map/pallas_call | solution.py:122
  28.0 0.1 copy.12
  28.2 1.0 %scatter_fusion = f32[16,3,16,6]{2,3,1,0:T(8,128)S(1)} fusion(f32[16,3,16,6]{2,3,1,0:T(8,128)S(1)} %broadcast_in_dim.9, s32[16]{0:T(128)S(1)} %compare_select_fusion, f32[16,3,16,6]{2,3,1,0:T(8,128)S(1)} %copy.13), kind=kCustom, calls=%fused_computation | custom fusion | bytes 55360 | tf_op jit(solution)/shard_map/scatter | solution.py:169
  29.2 0.7 %reshape.19 = f32[16,1,288]{2,1,0:T(1,128)} reshape(f32[16,3,6,16]{3,2,1,0:T(8,128)S(1)} %bitcast.11) | data formatting | bytes 36864
  29.9 6.0 %all-to-all-start = ((f32[16,1,288]{2,1,0:T(1,128)}), f32[16,1,288]{2,1,0:T(1,128)S(1)}, u32[]{:S(2)}, u32[]{:S(2)}) async-start(f32[16,1,288]{2,1,0:T(1,128)} %reshape.19), calls=%async_computation | async-start | bytes 49152 | tf_op jit(solution)/shard_map/all_to_all | solution.py:170
  35.9 0.8 %pad_maximum_fusion = f32[8,3,2,16,96]{4,3,2,1,0:T(8,128)} fusion(f32[3,3,2,16,96]{4,3,2,1,0:T(8,128)S(1)} %get-tuple-element.10, f32[5,3,2,16,96]{4,3,2,1,0:T(8,128)S(1)} %get-tuple-element.9), kind=kLoop, calls=%fused_computation.1 | loop fusion | flops 73728 | bytes 589824 | tf_op jit(solution)/shard_map/concatenate | solution.py:162
  36.7 0.7 %pad_maximum_fusion.1 = f32[8,3,16,96]{3,2,1,0:T(8,128)} fusion(f32[3,3,16,96]{3,2,1,0:T(8,128)S(1)} %get-tuple-element.12, f32[5,3,16,96]{3,2,1,0:T(8,128)S(1)} %get-tuple-element.11), kind=kLoop, calls=%fused_computation.2 | loop fusion | flops 36864 | bytes 294912 | tf_op jit(solution)/shard_map/concatenate | solution.py:163
  37.4 5.1 %all-to-all-done = f32[16,1,288]{2,1,0:T(1,128)S(1)} async-done(((f32[16,1,288]{2,1,0:T(1,128)}), f32[16,1,288]{2,1,0:T(1,128)S(1)}, u32[]{:S(2)}, u32[]{:S(2)}) %all-to-all-start) | async-done | bytes 18464 | tf_op jit(solution)/shard_map/all_to_all | solution.py:170
  42.5 0.5 %broadcast.10 = f32[]{:T(128)} broadcast(f32[]{:T(128)} %constant.17), dimensions={} | broadcast | bytes 8 | tf_op jit(solution)/shard_map/all_to_all | solution.py:170
  43.0 0.7 %reduce = f32[16,288]{1,0:T(8,128)S(1)} reduce(f32[16,1,288]{2,1,0:T(1,128)S(1)} %all-to-all-done, f32[]{:T(128)} %broadcast.10), dimensions={1}, to_apply=%all_to_all.3.reduce_sub_computation | reduce | bytes 36868 | tf_op jit(solution)/shard_map/all_to_all | solution.py:170
  43.7 0.1 reshape.20
  43.9 0.6 %copy.14 = f32[1,2,16,6]{2,1,3,0:T(2,128)} copy(f32[1,2,16,6]{2,3,1,0:T(8,128)S(1)} %fusion) | data formatting | bytes 1536
  (8 shorter events, 0.1 us)
Async XLA Ops:
  0.6 6.9 %copy-start.2 = (s32[8,3]{0,1:T(4,128)S(1)}, s32[8,3]{0,1:T(4,128)}, u32[]{:S(2)}) copy-start(s32[8,3]{0,1:T(4,128)} %param.4) | copy-start | bytes 292
  2.0 19.2 %collective-permute-start = (bf16[3,2,256,384]{3,2,1,0:T(8,128)(2,1)S(1)}, bf16[3,2,256,384]{3,2,1,0:T(8,128)(2,1)S(1)}, u32[]{:S(2)}, u32[]{:S(2)}) collective-permute-start(bf16[3,2,256,384]{3,2,1,0:T(8,128)(2,1)S(1)} %slice.17), channel_id=1, source_target_pairs={{0,30},{2,0},{4,2},{6,4},{8,6},{10,8},{12,10},{14,12},{16,14},{18,... | collective-permute-start | bytes 3538952 | tf_op jit(solution)/shard_map/ppermute | solution.py:16
  7.8 1.9 %copy-start = (bf16[8,2,256,384]{3,2,1,0:T(8,128)(2,1)S(1)}, bf16[8,2,256,384]{3,2,1,0:T(8,128)(2,1)}, u32[]{:S(2)}) copy-start(bf16[8,2,256,384]{3,2,1,0:T(8,128)(2,1)} %refs_0_.3) | copy-start | bytes 9437188
  9.7 9.6 %copy-start.3 = (s32[16]{0:T(128)S(1)}, s32[16]{0:T(128)}, u32[]{:S(2)}) copy-start(s32[16]{0:T(128)} %param.5) | copy-start | bytes 196
  9.7 11.6 %copy-start.1 = (bf16[8,2,256,384]{3,2,1,0:T(8,128)(2,1)S(1)}, bf16[8,2,256,384]{3,2,1,0:T(8,128)(2,1)}, u32[]{:S(2)}) copy-start(bf16[8,2,256,384]{3,2,1,0:T(8,128)(2,1)} %refs_0_.3) | copy-start | bytes 9437188
  29.9 12.6 %all-to-all-start = ((f32[16,1,288]{2,1,0:T(1,128)}), f32[16,1,288]{2,1,0:T(1,128)S(1)}, u32[]{:S(2)}, u32[]{:S(2)}) async-start(f32[16,1,288]{2,1,0:T(1,128)} %reshape.19), calls=%async_computation | async-start | bytes 49152 | tf_op jit(solution)/shard_map/all_to_all | solution.py:170

commit v3 on v2

--- a/solution.py
+++ b/solution.py
@@ -42,24 +42,38 @@
             copies.append(cp)
         for t in range(total):
             copies[t].wait()
-            for ct in range(ctiles):
-                xf[t, :, ct] = raw[t, :, :, pl.ds(ct * 128, 128)].astype(jnp.float32)
+            xf[t] = raw[t].astype(jnp.float32)
 
         lines = lax.broadcasted_iota(jnp.int32, (cols, cells), 0)
         cell = lax.broadcasted_iota(jnp.int32, (cols, cells), 1)
         pool = jnp.where(lines // LA == cell, 1.0 / (LR * LA), 0.0).astype(jnp.bfloat16)
-
-        def strided(j, comp, s, ct):
-            return xf[j, comp, ct, pl.ds(s, groups, stride=LR), :]
+        sub = lax.broadcasted_iota(jnp.int32, (8, 128), 0)
+        masks = {k: (sub % (2 * k)) < k for k in (4, 2, 1)}
+
+        def combine(x, y, k):
+            m = masks[k]
+            return jnp.where(m, x + pltpu.roll(x, 8 - k, 0), y + pltpu.roll(y, k, 0))
+
+        def fold(parts):
+            q = [combine(parts[g], parts[g + 4], 4) for g in range(4)]
+            r = [combine(q[0], q[2], 2), combine(q[1], q[3], 2)]
+            return combine(r[0], r[1], 1)
+
+        def rows_of(j, comp, g, ct):
+            return xf[j, comp, pl.ds(g * LR, LR), pl.ds(ct * 128, 128)]
+
+        def half(v):
+            return v[:8] + v[8:]
 
         def power(j, c):
             for ct in range(ctiles):
-                acc = jnp.zeros((groups, 128), jnp.float32)
-                for s in range(LR):
-                    x0 = strided(j, 0, s, ct)
-                    x1 = strided(j, 1, s, ct)
-                    acc = acc + (x0 * x0 + x1 * x1)
-                pacc[j, :, pl.ds(ct * 128, 128)] = acc
+                for blk in range(groups // 8):
+                    parts = []
+                    for g in range(blk * 8, blk * 8 + 8):
+                        x0 = rows_of(j, 0, g, ct)
+                        x1 = rows_of(j, 1, g, ct)
+                        parts.append(half(x0 * x0 + x1 * x1))
+                    pacc[j, pl.ds(blk * 8, 8), pl.ds(ct * 128, 128)] = fold(parts)
             return c
 
         lax.fori_loop(0, total, power, 0)
@@ -69,21 +83,21 @@
             return jnp.clip(first + i + off_ref[i, k], 0, total - 1)
 
         def pairs(i, c):
-            parts = [partner(i, k) for k in range(NB)]
-            for ct in range(ctiles):
-                re = [jnp.zeros((groups, 128), jnp.float32) for _ in range(NB)]
-                im = [jnp.zeros((groups, 128), jnp.float32) for _ in range(NB)]
-                for s in range(LR):
-                    a0 = strided(first + i, 0, s, ct)
-                    a1 = strided(first + i, 1, s, ct)
-                    for k in range(NB):
-                        b0 = strided(parts[k], 0, s, ct)
-                        b1 = strided(parts[k], 1, s, ct)
-                        re[k] = re[k] + (a0 * b0 + a1 * b1)
-                        im[k] = im[k] + (a1 * b0 - a0 * b1)
-                for k in range(NB):
-                    racc[i, k, 0, :, pl.ds(ct * 128, 128)] = re[k]
-                    racc[i, k, 1, :, pl.ds(ct * 128, 128)] = im[k]
+            for k in range(NB):
+                j = partner(i, k)
+                for ct in range(ctiles):
+                    for blk in range(groups // 8):
+                        re = []
+                        im = []
+                        for g in range(blk * 8, blk * 8 + 8):
+                            a0 = rows_of(first + i, 0, g, ct)
+                            a1 = rows_of(first + i, 1, g, ct)
+                            b0 = rows_of(j, 0, g, ct)
+                            b1 = rows_of(j, 1, g, ct)
+                            re.append(half(a0 * b0 + a1 * b1))
+                            im.append(half(a1 * b0 - a0 * b1))
+                        racc[i, k, 0, pl.ds(blk * 8, 8), pl.ds(ct * 128, 128)] = fold(re)
+                        racc[i, k, 1, pl.ds(blk * 8, 8), pl.ds(ct * 128, 128)] = fold(im)
             return c
 
         lax.fori_loop(0, dates, pairs, 0)
@@ -135,7 +149,7 @@
         ),
         scratch_shapes=[
             pltpu.VMEM((total, 2, rows, cols), jnp.bfloat16),
-            pltpu.VMEM((total, 2, cols // 128, rows, 128), jnp.float32),
+            pltpu.VMEM((total, 2, rows, cols), jnp.float32),
             pltpu.VMEM((total, groups, cols), jnp.float32),
             pltpu.VMEM((dates, NB, 2, groups, cols), jnp.float32),
             pltpu.VMEM((total, groups, cells), jnp.float32),

time: 44.7 us -> 42.6 us (0.953)
  Pallas kernels: 16.3 us -> 10.9 us
  waiting for transfers between devices: 7 us -> 10.3 us
    pallas_call x2, Pallas kernels: 16.3 us -> 10.9 us  [local_math(): pl.pallas_call(make_kernel(images, first, dates, rows, cols), out_shape=(...]
    ppermute x1, waiting for transfers between devices: 1.91 us -> 5.23 us  [shifted(): return lax.ppermute(value, axis, pairs)]
  transfers between devices with their start and end apart: 2 -> 2, of which waited for: 2 -> 2; matrix products, arithmetic and copies ran while one was open for 4% -> 4% of each run, Pallas kernels for 22% -> 15%
where the time goes in v3:
time: 42.6 us; the launch traced here: 42.3 us
  starting transfers between devices  11.5 us (27%)
  Pallas kernels  10.9 us (26%)
  waiting for transfers between devices  10.3 us (24%)
  local copies, waits for them, and re-layouts  6.69 us (16%)
  other arithmetic  2.22 us (5%)
  between operations  0.77 us (2%)
    pallas_call x2, Pallas kernels, local_math(): pl.pallas_call(make_kernel(images, first, dates, rows, cols), out_shape=(...  10.9 us
    all_to_all x1, starting transfers between devices, on_device(): lax.all_to_all(slotted, 'date', split_axis=0, concat_axis=0, tiled=True)  5.98 us
    ppermute x1, starting transfers between devices, shifted(): return lax.ppermute(value, axis, pairs)  5.5 us
    ppermute x1, waiting for transfers between devices, shifted(): return lax.ppermute(value, axis, pairs)  5.23 us
    all_to_all x1, waiting for transfers between devices, on_device(): lax.all_to_all(slotted, 'date', split_axis=0, concat_axis=0, tiled=True)  5.09 us
    unnamed x13, local copies, waits for them, and re-layouts  3.51 us
    slice x1, local copies, waits for them, and re-layouts, on_device(): rim = shifted(slc[:NB], 'date', -1)  1.4 us
    scatter x1, local copies, waits for them, and re-layouts, on_device(): slotted = jnp.zeros_like(tiles).at[owner].set(tiles)  1.04 us
  transfers between devices with their start and end apart: 2, of which 2 were waited for; matrix products, arithmetic and copies ran while one was open for 4% of the time, Pallas kernels for 15%

profile of v3, /device:TPU:0, one launch (start us, length us, event | category | flops | bytes accessed | tf_op | source)
XLA Modules:
  0.0 42.3 jit_solution(3419437108805042934)
XLA Ops:
  0.6 0.0 copy-start.2
  0.6 1.4 %slice.17 = bf16[3,2,256,384]{3,2,1,0:T(8,128)(2,1)S(1)} slice(bf16[8,2,256,384]{3,2,1,0:T(8,128)(2,1)} %refs_0_.3), slice={[0:3], [0:2], [0:256], [0:384]} | slice | bytes 2359296 | tf_op jit(solution)/shard_map/slice | solution.py:165
  2.0 5.5 %collective-permute-start = (bf16[3,2,256,384]{3,2,1,0:T(8,128)(2,1)S(1)}, bf16[3,2,256,384]{3,2,1,0:T(8,128)(2,1)S(1)}, u32[]{:S(2)}, u32[]{:S(2)}) collective-permute-start(bf16[3,2,256,384]{3,2,1,0:T(8,128)(2,1)S(1)} %slice.17), channel_id=1, source_target_pairs={{0,30},{2,0},{4,2},{6,4},{8,6},{10,8},{12,10},{14,12},{16,14},{18,... | collective-permute-start | bytes 3538952 | tf_op jit(solution)/shard_map/ppermute | solution.py:16
  7.5 0.0 copy-done.2
  7.5 0.1 slice.16
  7.6 0.1 copy.16.off_ref
  7.7 0.1 copy.15.off_ref
  7.8 0.0 copy-start
  7.8 1.9 %copy-done = bf16[8,2,256,384]{3,2,1,0:T(8,128)(2,1)S(1)} copy-done((bf16[8,2,256,384]{3,2,1,0:T(8,128)(2,1)S(1)}, bf16[8,2,256,384]{3,2,1,0:T(8,128)(2,1)}, u32[]{:S(2)}) %copy-start) | copy-done | bytes 3145752
  9.7 0.0 copy-start.3
  9.7 0.0 copy-start.1
  9.7 6.3 %shard_map.58 = (f32[5,3,2,16,96]{4,3,2,1,0:T(8,128)S(1)}, f32[5,3,16,96]{3,2,1,0:T(8,128)S(1)}, f32[3,16,96]{2,1,0:T(8,128)S(1)}) custom-call(s32[5,3]{1,0:T(8,128)S(1)} %copy.15.off_ref, bf16[8,2,256,384]{3,2,1,0:T(8,128)(2,1)S(1)} %copy-done), custom_call_target="tpu_custom_call" | custom-call | tf_op jit(solution)/shard_map/pallas_call | solution.py:136
  16.0 0.0 copy-done.3
  16.0 5.2 %collective-permute-done.refs_1_ = bf16[3,2,256,384]{3,2,1,0:T(8,128)(2,1)S(1)} collective-permute-done((bf16[3,2,256,384]{3,2,1,0:T(8,128)(2,1)S(1)}, bf16[3,2,256,384]{3,2,1,0:T(8,128)(2,1)S(1)}, u32[]{:S(2)}, u32[]{:S(2)}) %collective-permute-start) | collective-permute-done | bytes 1179680 | tf_op jit(solution)/shard_map/ppermute | solution.py:16
  21.3 0.0 copy-done.1
  21.3 4.6 %shard_map.59 = (f32[3,3,2,16,96]{4,3,2,1,0:T(8,128)S(1)}, f32[3,3,16,96]{3,2,1,0:T(8,128)S(1)}, f32[3,16,96]{2,1,0:T(8,128)S(1)}) custom-call(s32[3,3]{1,0:T(4,128)S(1)} %copy.16.off_ref, bf16[8,2,256,384]{3,2,1,0:T(8,128)(2,1)S(1)} %copy-done.1, bf16[3,2,256,384]{3,2,1,0:T(8,128)(2,1)S(1)} %collective-permute-done.refs_1_), custom_call_target="tpu_custom_call" | custom-call | tf_op jit(solution)/shard_map/pallas_call | solution.py:136
  25.8 0.1 copy.12
  26.0 1.0 %scatter_fusion = f32[16,3,16,6]{2,3,1,0:T(8,128)S(1)} fusion(f32[16,3,16,6]{2,3,1,0:T(8,128)S(1)} %broadcast_in_dim.9, s32[16]{0:T(128)S(1)} %compare_select_fusion, f32[16,3,16,6]{2,3,1,0:T(8,128)S(1)} %copy.13), kind=kCustom, calls=%fused_computation | custom fusion | bytes 55360 | tf_op jit(solution)/shard_map/scatter | solution.py:183
  27.1 0.7 %reshape.19 = f32[16,1,288]{2,1,0:T(1,128)} reshape(f32[16,3,6,16]{3,2,1,0:T(8,128)S(1)} %bitcast.11) | data formatting | bytes 36864
  27.8 6.0 %all-to-all-start = ((f32[16,1,288]{2,1,0:T(1,128)}), f32[16,1,288]{2,1,0:T(1,128)S(1)}, u32[]{:S(2)}, u32[]{:S(2)}) async-start(f32[16,1,288]{2,1,0:T(1,128)} %reshape.19), calls=%async_computation | async-start | bytes 49152 | tf_op jit(solution)/shard_map/all_to_all | solution.py:184
  33.8 0.8 %pad_maximum_fusion = f32[8,3,2,16,96]{4,3,2,1,0:T(8,128)} fusion(f32[3,3,2,16,96]{4,3,2,1,0:T(8,128)S(1)} %get-tuple-element.10, f32[5,3,2,16,96]{4,3,2,1,0:T(8,128)S(1)} %get-tuple-element.9), kind=kLoop, calls=%fused_computation.1 | loop fusion | flops 73728 | bytes 589824 | tf_op jit(solution)/shard_map/concatenate | solution.py:176
  34.6 0.7 %pad_maximum_fusion.1 = f32[8,3,16,96]{3,2,1,0:T(8,128)} fusion(f32[3,3,16,96]{3,2,1,0:T(8,128)S(1)} %get-tuple-element.12, f32[5,3,16,96]{3,2,1,0:T(8,128)S(1)} %get-tuple-element.11), kind=kLoop, calls=%fused_computation.2 | loop fusion | flops 36864 | bytes 294912 | tf_op jit(solution)/shard_map/concatenate | solution.py:177
  35.3 5.1 %all-to-all-done = f32[16,1,288]{2,1,0:T(1,128)S(1)} async-done(((f32[16,1,288]{2,1,0:T(1,128)}), f32[16,1,288]{2,1,0:T(1,128)S(1)}, u32[]{:S(2)}, u32[]{:S(2)}) %all-to-all-start) | async-done | bytes 18464 | tf_op jit(solution)/shard_map/all_to_all | solution.py:184
  40.4 0.5 %broadcast.10 = f32[]{:T(128)} broadcast(f32[]{:T(128)} %constant.17), dimensions={} | broadcast | bytes 8 | tf_op jit(solution)/shard_map/all_to_all | solution.py:184
  40.9 0.7 %reduce = f32[16,288]{1,0:T(8,128)S(1)} reduce(f32[16,1,288]{2,1,0:T(1,128)S(1)} %all-to-all-done, f32[]{:T(128)} %broadcast.10), dimensions={1}, to_apply=%all_to_all.3.reduce_sub_computation | reduce | bytes 36868 | tf_op jit(solution)/shard_map/all_to_all | solution.py:184
  41.6 0.1 reshape.20
  41.7 0.6 %copy.14 = f32[1,2,16,6]{2,1,3,0:T(2,128)} copy(f32[1,2,16,6]{2,3,1,0:T(8,128)S(1)} %fusion) | data formatting | bytes 1536
  (8 shorter events, 0.1 us)
Async XLA Ops:
  0.6 6.9 %copy-start.2 = (s32[8,3]{0,1:T(4,128)S(1)}, s32[8,3]{0,1:T(4,128)}, u32[]{:S(2)}) copy-start(s32[8,3]{0,1:T(4,128)} %param.4) | copy-start | bytes 292
  2.0 19.2 %collective-permute-start = (bf16[3,2,256,384]{3,2,1,0:T(8,128)(2,1)S(1)}, bf16[3,2,256,384]{3,2,1,0:T(8,128)(2,1)S(1)}, u32[]{:S(2)}, u32[]{:S(2)}) collective-permute-start(bf16[3,2,256,384]{3,2,1,0:T(8,128)(2,1)S(1)} %slice.17), channel_id=1, source_target_pairs={{0,30},{2,0},{4,2},{6,4},{8,6},{10,8},{12,10},{14,12},{16,14},{18,... | collective-permute-start | bytes 3538952 | tf_op jit(solution)/shard_map/ppermute | solution.py:16
  7.8 1.9 %copy-start = (bf16[8,2,256,384]{3,2,1,0:T(8,128)(2,1)S(1)}, bf16[8,2,256,384]{3,2,1,0:T(8,128)(2,1)}, u32[]{:S(2)}) copy-start(bf16[8,2,256,384]{3,2,1,0:T(8,128)(2,1)} %refs_0_.3) | copy-start | bytes 9437188
  9.7 6.3 %copy-start.3 = (s32[16]{0:T(128)S(1)}, s32[16]{0:T(128)}, u32[]{:S(2)}) copy-start(s32[16]{0:T(128)} %param.5) | copy-start | bytes 196
  9.7 11.6 %copy-start.1 = (bf16[8,2,256,384]{3,2,1,0:T(8,128)(2,1)S(1)}, bf16[8,2,256,384]{3,2,1,0:T(8,128)(2,1)}, u32[]{:S(2)}) copy-start(bf16[8,2,256,384]{3,2,1,0:T(8,128)(2,1)} %refs_0_.3) | copy-start | bytes 9437188
  27.8 12.6 %all-to-all-start = ((f32[16,1,288]{2,1,0:T(1,128)}), f32[16,1,288]{2,1,0:T(1,128)S(1)}, u32[]{:S(2)}, u32[]{:S(2)}) async-start(f32[16,1,288]{2,1,0:T(1,128)} %reshape.19), calls=%async_computation | async-start | bytes 49152 | tf_op jit(solution)/shard_map/all_to_all | solution.py:184

commit v4 on v3

--- a/solution.py
+++ b/solution.py
@@ -26,15 +26,29 @@
     return out + jnp.dot(lo, pool, preferred_element_type=jnp.float32)
 
 
-def make_kernel(images, first, dates, rows, cols):
+def make_kernel(images, first, dates, rows, cols, known, tiles):
     groups = rows // LR
     cells = cols // LA
     total = len(images)
     ctiles = cols // 128
-
-    def kernel(off_ref, *refs):
-        srcs = refs[:-9]
-        ifg_ref, coh_ref, ws_ref, raw, xf, pacc, racc, pw, sem = refs[-9:]
+    lanes = 128
+    nsrc = len(set(src for src, _ in images))
+
+    def kernel(*refs):
+        off_ref = refs[0]
+        if known:
+            owner_ref, pw_in, ws_in = refs[1:4]
+            srcs = refs[4 : 4 + nsrc]
+            rest = refs[4 + nsrc :]
+        else:
+            srcs = refs[1 : 1 + nsrc]
+            rest = refs[1 + nsrc :]
+        ifg_ref, coh_ref, last_ref = rest[:3]
+        if known:
+            raw, xf, pacc, racc, pw, racc_pooled, sem = rest[3:]
+        else:
+            pw_out = rest[3]
+            raw, xf, pacc, racc, pw, racc_pooled, sem = rest[4:]
         copies = []
         for t, (src, lead) in enumerate(images):
             cp = pltpu.make_async_copy(srcs[src].at[lead], raw.at[t], sem.at[t])
@@ -44,9 +58,9 @@
             copies[t].wait()
             xf[t] = raw[t].astype(jnp.float32)
 
-        lines = lax.broadcasted_iota(jnp.int32, (cols, cells), 0)
-        cell = lax.broadcasted_iota(jnp.int32, (cols, cells), 1)
-        pool = jnp.where(lines // LA == cell, 1.0 / (LR * LA), 0.0).astype(jnp.bfloat16)
+        line = lax.broadcasted_iota(jnp.int32, (cols, lanes), 0)
+        cell = lax.broadcasted_iota(jnp.int32, (cols, lanes), 1)
+        pool = jnp.where(line // LA == cell, 1.0 / (LR * LA), 0.0).astype(jnp.bfloat16)
         sub = lax.broadcasted_iota(jnp.int32, (8, 128), 0)
         masks = {k: (sub % (2 * k)) < k for k in (4, 2, 1)}
 
@@ -73,11 +87,18 @@
                         x0 = rows_of(j, 0, g, ct)
                         x1 = rows_of(j, 1, g, ct)
                         parts.append(half(x0 * x0 + x1 * x1))
-                    pacc[j, pl.ds(blk * 8, 8), pl.ds(ct * 128, 128)] = fold(parts)
+                    pacc[j - known, pl.ds(blk * 8, 8), pl.ds(ct * 128, 128)] = fold(parts)
             return c
 
-        lax.fori_loop(0, total, power, 0)
-        pw[...] = split_pool(pacc[...].reshape(total * groups, cols), pool).reshape(total, groups, cells)
+        lax.fori_loop(known, total, power, 0)
+        fresh = total - known
+        pw[pl.ds(known, fresh)] = split_pool(pacc[...].reshape(fresh * groups, cols), pool).reshape(
+            fresh, groups, lanes
+        )
+        if known:
+            pw[pl.ds(0, known)] = pw_in[...]
+        else:
+            pw_out[...] = pw[...]
 
         def partner(i, k):
             return jnp.clip(first + i + off_ref[i, k], 0, total - 1)
@@ -102,87 +123,123 @@
 
         lax.fori_loop(0, dates, pairs, 0)
         pooled = split_pool(racc[...].reshape(dates * NB * 2 * groups, cols), pool)
-        ifg_ref[...] = pooled.reshape(dates, NB, 2, groups, cells)
+        pooled = pooled.reshape(dates, NB, 2, groups, lanes)
+        ifg_ref[...] = pooled[..., :cells]
 
         def coher(i, ws):
             wr, wi, wc = ws
             pa = pw[first + i]
             for k in range(NB):
                 pb = pw[partner(i, k)]
-                re = ifg_ref[i, k, 0]
-                im = ifg_ref[i, k, 1]
+                re = pooled_at(i, k, 0)
+                im = pooled_at(i, k, 1)
                 co = jnp.sqrt(re * re + im * im) / jnp.sqrt(pa * pb + 1e-06)
-                coh_ref[i, k] = co
+                coh_ref[i, k] = co[:, :cells]
                 wr = wr + co * re
                 wi = wi + co * im
                 wc = wc + co
             return (wr, wi, wc)
 
-        zero = jnp.zeros((groups, cells), jnp.float32)
-        wr, wi, wc = lax.fori_loop(0, dates, coher, (zero, zero, zero))
-        ws_ref[0] = wr
-        ws_ref[1] = wi
-        ws_ref[2] = wc
+        racc_pooled[...] = pooled
+
+        def pooled_at(i, k, comp):
+            return racc_pooled[i, k, comp]
+
+        zero = jnp.zeros((groups, lanes), jnp.float32)
+        if known:
+            start = (ws_in[0], ws_in[1], ws_in[2])
+        else:
+            start = (zero, zero, zero)
+        wr, wi, wc = lax.fori_loop(0, dates, coher, start)
+        if not known:
+            last_ref[0] = wr
+            last_ref[1] = wi
+            last_ref[2] = wc
+            return
+        width = cells // tiles
+        lane = lax.broadcasted_iota(jnp.int32, (groups, lanes), 1)
+        for t in range(tiles):
+            base = t * width
+            block = jnp.where(
+                lane < width,
+                pltpu.roll(wr, (lanes - base) % lanes, 1),
+                jnp.where(
+                    lane < 2 * width,
+                    pltpu.roll(wi, (lanes + width - base) % lanes, 1),
+                    jnp.where(lane < 3 * width, pltpu.roll(wc, (lanes + 2 * width - base) % lanes, 1), 0.0),
+                ),
+            )
+            last_ref[owner_ref[t]] = block
 
     return kernel
 
 
-def local_math(offsets, sources, images, first, dates):
+def local_math(offsets, sources, images, first, dates, known=None):
     _, _, rows, cols = sources[0].shape
     groups = rows // LR
     cells = cols // LA
     total = len(images)
+    lanes = 128
     vmem = pltpu.VMEM
+    smem = pltpu.SMEM
+    if known is None:
+        nknown, tiles, extra = 0, 0, []
+        last = jax.ShapeDtypeStruct((3, groups, lanes), jnp.float32)
+        outs_extra = [jax.ShapeDtypeStruct((total, groups, lanes), jnp.float32)]
+    else:
+        owner, pw_in, ws_in = known
+        nknown, tiles, extra = pw_in.shape[0], owner.shape[0], [owner, pw_in, ws_in]
+        last = jax.ShapeDtypeStruct((tiles, groups, lanes), jnp.float32)
+        outs_extra = []
+    out_shape = [
+        jax.ShapeDtypeStruct((dates, NB, 2, groups, cells), jnp.float32),
+        jax.ShapeDtypeStruct((dates, NB, groups, cells), jnp.float32),
+        last,
+    ] + outs_extra
+    in_specs = [pl.BlockSpec(memory_space=smem)]
+    if known is not None:
+        in_specs += [pl.BlockSpec(memory_space=smem), pl.BlockSpec(memory_space=vmem), pl.BlockSpec(memory_space=vmem)]
+    in_specs += [pl.BlockSpec(memory_space=pl.ANY) for _ in sources]
     return pl.pallas_call(
-        make_kernel(images, first, dates, rows, cols),
-        out_shape=(
-            jax.ShapeDtypeStruct((dates, NB, 2, groups, cells), jnp.float32),
-            jax.ShapeDtypeStruct((dates, NB, groups, cells), jnp.float32),
-            jax.ShapeDtypeStruct((3, groups, cells), jnp.float32),
-        ),
-        in_specs=[pl.BlockSpec(memory_space=pltpu.SMEM)]
-        + [pl.BlockSpec(memory_space=pl.ANY) for _ in sources],
-        out_specs=(
-            pl.BlockSpec(memory_space=vmem),
-            pl.BlockSpec(memory_space=vmem),
-            pl.BlockSpec(memory_space=vmem),
-        ),
+        make_kernel(images, first, dates, rows, cols, nknown, tiles),
+        out_shape=tuple(out_shape),
+        in_specs=in_specs,
+        out_specs=tuple(pl.BlockSpec(memory_space=vmem) for _ in out_shape),
         scratch_shapes=[
             pltpu.VMEM((total, 2, rows, cols), jnp.bfloat16),
             pltpu.VMEM((total, 2, rows, cols), jnp.float32),
-            pltpu.VMEM((total, groups, cols), jnp.float32),
+            pltpu.VMEM((total - nknown, groups, cols), jnp.float32),
             pltpu.VMEM((dates, NB, 2, groups, cols), jnp.float32),
-            pltpu.VMEM((total, groups, cells), jnp.float32),
+            pltpu.VMEM((total, groups, lanes), jnp.float32),
+            pltpu.VMEM((dates, NB, 2, groups, lanes), jnp.float32),
             pltpu.SemaphoreType.DMA((total,)),
         ],
         compiler_params=pltpu.CompilerParams(vmem_limit_bytes=48 * 1024 * 1024),
-    )(offsets, *sources)
+    )(offsets, *extra, *sources)
 
 
 def on_device(slc, offsets, owner):
     count = slc.shape[0]
     inner = count - NB
     rim = shifted(slc[:NB], "date", -1)
-    ifg_a, coh_a, ws_a = local_math(
+    ifg_a, coh_a, ws_a, pw_a = local_math(
         offsets[:inner], [slc], [(0, t) for t in range(count)], 0, inner
     )
-    ifg_b, coh_b, ws_b = local_math(
+    ifg_b, coh_b, slotted = local_math(
         offsets[inner:],
         [slc, rim],
         [(0, inner + t) for t in range(NB)] + [(1, t) for t in range(NB)],
         0,
         NB,
+        known=(owner, pw_a[inner:], ws_a),
     )
     interferograms = jnp.concatenate([ifg_a, ifg_b], 0)
     coherence = jnp.concatenate([coh_a, coh_b], 0)
-    ws = ws_a + ws_b
-    tile_count = owner.shape[0]
-    rows_loc = ws.shape[1]
-    width = ws.shape[2] // tile_count
-    tiles = ws.reshape(3, rows_loc, tile_count, width).transpose(2, 0, 1, 3)
-    slotted = jnp.zeros_like(tiles).at[owner].set(tiles)
+    width = ifg_a.shape[-1] // owner.shape[0]
     sums = lax.all_to_all(slotted, "date", split_axis=0, concat_axis=0, tiled=True).sum(0)
-    network_mean = (sums[:2] / (1.0 + sums[2:3]))[None]
+    network_mean = (
+        jnp.stack([sums[:, :width], sums[:, width : 2 * width]], 0) / (1.0 + sums[:, 2 * width : 3 * width])
+    )[None]
     return (interferograms, coherence, network_mean)
 
 

time: 42.6 us -> 45.5 us (1.068)
  local copies, waits for them, and re-layouts: 6.69 us -> 9.5 us
  waiting for transfers between devices: 10.3 us -> 9.79 us
    unnamed x13 -> x24, local copies, waits for them, and re-layouts: 3.51 us -> 6.17 us
    scatter x1 -> x0, local copies, waits for them, and re-layouts: 1.04 us -> none  [on_device(): slotted = jnp.zeros_like(tiles).at[owner].set(tiles)]
    slice x1, local copies, waits for them, and re-layouts: 1.4 us -> 2.41 us  [on_device(): rim = shifted(slc[:NB], 'date', -1)]
    concatenate x1, other arithmetic: 0.7 us -> 1.63 us  [on_device(): coherence = jnp.concatenate([coh_a, coh_b], 0)]
    ppermute x1, waiting for transfers between devices: 5.23 us -> 4.3 us  [shifted(): return lax.ppermute(value, axis, pairs)]
    slice x0 -> x4, local copies, waits for them, and re-layouts: none -> 0.84 us  [the longest x1 0.61 us: on_device(): pw_a[inner:]]
    all_to_all x1 -> x0, other arithmetic: 0.7 us -> none  [on_device(): lax.all_to_all(slotted, 'date', split_axis=0, concat_axis=0, tiled=True)]
    all_to_all x1 -> x0, local copies, waits for them, and re-layouts: 0.51 us -> none  [on_device(): lax.all_to_all(slotted, 'date', split_axis=0, concat_axis=0, tiled=True)]
  transfers between devices with their start and end apart: 2 -> 2, of which waited for: 2 -> 2; matrix products, arithmetic and copies ran while one was open for 4% -> 7% of each run, Pallas kernels for 15% -> 14%
where the time goes in v4:
time: 45.5 us; the launch traced here: 45 us
  starting transfers between devices  11.4 us (25%)
  Pallas kernels  11.2 us (25%)
  waiting for transfers between devices  9.79 us (22%)
  local copies, waits for them, and re-layouts  9.5 us (21%)
  other arithmetic  2.44 us (5%)
  between operations  0.7 us (2%)
    pallas_call x2, Pallas kernels, local_math(): pl.pallas_call(make_kernel(images, first, dates, rows, cols, nknown, tile...  11.2 us
    unnamed x24, local copies, waits for them, and re-layouts  6.17 us
    all_to_all x1, starting transfers between devices, on_device(): lax.all_to_all(slotted, 'date', split_axis=0, concat_axis=0, tiled=True)  5.99 us
    all_to_all x1, waiting for transfers between devices, on_device(): lax.all_to_all(slotted, 'date', split_axis=0, concat_axis=0, tiled=True)  5.49 us
    ppermute x1, starting transfers between devices, shifted(): return lax.ppermute(value, axis, pairs)  5.44 us
    ppermute x1, waiting for transfers between devices, shifted(): return lax.ppermute(value, axis, pairs)  4.3 us
    slice x1, local copies, waits for them, and re-layouts, on_device(): rim = shifted(slc[:NB], 'date', -1)  2.41 us
    concatenate x1, other arithmetic, on_device(): coherence = jnp.concatenate([coh_a, coh_b], 0)  1.63 us
  transfers between devices with their start and end apart: 2, of which 2 were waited for; matrix products, arithmetic and copies ran while one was open for 7% of the time, Pallas kernels for 14%

profile of v4, /device:TPU:0, one launch (start us, length us, event | category | flops | bytes accessed | tf_op | source)
XLA Modules:
  0.0 45.0 jit_solution(14800851876321781375)
XLA Ops:
  0.6 0.0 copy-start.9
  0.6 2.4 %slice.24 = bf16[3,2,256,384]{3,2,1,0:T(8,128)(2,1)} slice(bf16[8,2,256,384]{3,2,1,0:T(8,128)(2,1)} %refs_4_.1), slice={[0:3], [0:2], [0:256], [0:384]} | slice | bytes 2359296 | tf_op jit(solution)/shard_map/slice | solution.py:224
  3.1 5.4 %collective-permute-start = (bf16[3,2,256,384]{3,2,1,0:T(8,128)(2,1)}, bf16[3,2,256,384]{3,2,1,0:T(8,128)(2,1)}, u32[]{:S(2)}, u32[]{:S(2)}) collective-permute-start(bf16[3,2,256,384]{3,2,1,0:T(8,128)(2,1)} %slice.24), channel_id=1, source_target_pairs={{0,30},{2,0},{4,2},{6,4},{8,6},{10,8},{12,10},{14,12},{16,14},{18,... | collective-permute-start | bytes 3538952 | tf_op jit(solution)/shard_map/ppermute | solution.py:16
  8.5 0.0 copy-done.9
  8.5 0.1 slice.22
  8.6 0.1 copy.21.refs_0_
  8.7 0.0 copy-start
  8.7 1.9 %copy-done = bf16[8,2,256,384]{3,2,1,0:T(8,128)(2,1)S(1)} copy-done((bf16[8,2,256,384]{3,2,1,0:T(8,128)(2,1)S(1)}, bf16[8,2,256,384]{3,2,1,0:T(8,128)(2,1)}, u32[]{:S(2)}) %copy-start) | copy-done | bytes 3145752
  10.6 0.0 copy-start.1
  10.6 0.0 copy-start.8
  10.6 6.3 %shard_map.58 = (f32[5,3,2,16,96]{4,3,2,1,0:T(8,128)S(1)}, f32[5,3,16,96]{3,2,1,0:T(8,128)S(1)}, f32[3,16,128]{2,1,0:T(8,128)S(1)}, f32[8,16,128]{2,1,0:T(8,128)S(1)}) custom-call(s32[5,3]{1,0:T(8,128)S(1)} %copy.21.refs_0_, bf16[8,2,256,384]{3,2,1,0:T(8,128)(2,1)S(1)} %copy-done), custom_call_target="tpu_custom_call" | custom-call | tf_op jit(solution)/shard_map/pallas_call | solution.py:203
  16.9 0.0 copy-start.3
  16.9 0.6 %copy-done.3 = f32[5,3,16,96]{3,2,1,0:T(8,128)} copy-done((f32[5,3,16,96]{3,2,1,0:T(8,128)}, f32[5,3,16,96]{3,2,1,0:T(8,128)S(1)}, u32[]{:S(2)}) %copy-start.3) | copy-done | bytes 92184
  17.5 0.0 copy-start.6
  17.5 0.6 %slice.23.refs_2_ = f32[3,16,128]{2,1,0:T(8,128)} slice(f32[8,16,128]{2,1,0:T(8,128)S(1)} %get-tuple-element.11), slice={[5:8], [0:16], [0:128]} | slice | bytes 49152 | tf_op jit(solution)/shard_map/slice | solution.py:234
  18.1 0.1 copy.22.refs_0_
  18.2 4.3 %collective-permute-done.refs_5_ = bf16[3,2,256,384]{3,2,1,0:T(8,128)(2,1)} collective-permute-done((bf16[3,2,256,384]{3,2,1,0:T(8,128)(2,1)}, bf16[3,2,256,384]{3,2,1,0:T(8,128)(2,1)}, u32[]{:S(2)}, u32[]{:S(2)}) %collective-permute-start) | collective-permute-done | bytes 1179680 | tf_op jit(solution)/shard_map/ppermute | solution.py:16
  22.5 0.0 copy-done.6
  22.5 0.0 copy-done.1
  22.5 0.0 copy-done.8
  22.5 0.0 copy-start.4
  22.6 0.7 %copy-done.4 = f32[3,16,128]{2,1,0:T(8,128)S(1)} copy-done((f32[3,16,128]{2,1,0:T(8,128)S(1)}, f32[3,16,128]{2,1,0:T(8,128)}, u32[]{:S(2)}) %copy-start.4) | copy-done | bytes 24600
  23.3 0.0 copy-start.7
  23.3 0.7 %copy-done.7 = f32[3,16,128]{2,1,0:T(8,128)S(1)} copy-done((f32[3,16,128]{2,1,0:T(8,128)S(1)}, f32[3,16,128]{2,1,0:T(8,128)}, u32[]{:S(2)}) %copy-start.7) | copy-done | bytes 24600
  24.0 4.9 %shard_map.59 = (f32[3,3,2,16,96]{4,3,2,1,0:T(8,128)S(1)}, f32[3,3,16,96]{3,2,1,0:T(8,128)S(1)}, f32[16,16,128]{2,1,0:T(8,128)S(1)}) custom-call(s32[3,3]{1,0:T(4,128)S(1)} %copy.22.refs_0_, s32[16]{0:T(128)S(1)} %copy-done.8, f32[3,16,128]{2,1,0:T(8,128)S(1)} %copy-done.4, f32[3,16,128]{2,1,0:T(8,128)S(1)} %copy-done.7, ...), custom_call_target="tpu_custom_call" | custom-call | tf_op jit(solution)/shard_map/pallas_call | solution.py:203
  28.9 0.0 copy-start.2
  28.9 0.6 %copy-done.2 = f32[16,16,128]{2,1,0:T(8,128)} copy-done((f32[16,16,128]{2,1,0:T(8,128)}, f32[16,16,128]{2,1,0:T(8,128)S(1)}, u32[]{:S(2)}) %copy-start.2) | copy-done | bytes 131096
  29.5 0.0 copy-start.5
  29.5 0.6 %copy-done.5 = f32[3,3,16,96]{3,2,1,0:T(8,128)} copy-done((f32[3,3,16,96]{3,2,1,0:T(8,128)}, f32[3,3,16,96]{3,2,1,0:T(8,128)S(1)}, u32[]{:S(2)}) %copy-start.5) | copy-done | bytes 55320
  30.2 6.0 %all-to-all-start = ((f32[16,16,128]{2,1,0:T(8,128)}), f32[16,16,128]{2,1,0:T(8,128)S(1)}, u32[]{:S(2)}, u32[]{:S(2)}) async-start(f32[16,16,128]{2,1,0:T(8,128)} %copy-done.2), calls=%async_computation | async-start | bytes 262144 | tf_op jit(solution)/shard_map/all_to_all | solution.py:239
  36.2 1.6 %pad_maximum_fusion.1 = f32[8,3,16,96]{3,2,1,0:T(8,128)} fusion(f32[3,3,16,96]{3,2,1,0:T(8,128)} %copy-done.5, f32[5,3,16,96]{3,2,1,0:T(8,128)} %copy-done.3), kind=kLoop, calls=%fused_computation.1 | loop fusion | flops 36864 | bytes 294912 | tf_op jit(solution)/shard_map/concatenate | solution.py:237
  37.8 0.8 %pad_maximum_fusion = f32[8,3,2,16,96]{4,3,2,1,0:T(8,128)} fusion(f32[3,3,2,16,96]{4,3,2,1,0:T(8,128)S(1)} %get-tuple-element.13, f32[5,3,2,16,96]{4,3,2,1,0:T(8,128)S(1)} %get-tuple-element.10), kind=kLoop, calls=%fused_computation | loop fusion | flops 73728 | bytes 589824 | tf_op jit(solution)/shard_map/concatenate | solution.py:236
  38.6 5.5 %all-to-all-done = f32[16,16,128]{2,1,0:T(8,128)S(1)} async-done(((f32[16,16,128]{2,1,0:T(8,128)}), f32[16,16,128]{2,1,0:T(8,128)S(1)}, u32[]{:S(2)}, u32[]{:S(2)}) %all-to-all-start) | async-done | bytes 131104 | tf_op jit(solution)/shard_map/all_to_all | solution.py:239
  44.1 0.1 fusion
  44.2 0.1 copy.23
  44.3 0.1 copy.17
  44.3 0.1 copy.18
  44.4 0.6 %copy.20 = f32[1,2,16,6]{2,1,3,0:T(2,128)} copy(f32[1,2,16,6]{2,3,1,0:T(8,128)S(1)} %maximum_divide_fusion) | data formatting | bytes 1536
  (3 shorter events, 0.0 us)
Async XLA Ops:
  0.6 7.9 %copy-start.9 = (s32[8,3]{0,1:T(4,128)S(1)}, s32[8,3]{0,1:T(4,128)}, u32[]{:S(2)}) copy-start(s32[8,3]{0,1:T(4,128)} %param.4) | copy-start | bytes 292
  3.1 19.5 %collective-permute-start = (bf16[3,2,256,384]{3,2,1,0:T(8,128)(2,1)}, bf16[3,2,256,384]{3,2,1,0:T(8,128)(2,1)}, u32[]{:S(2)}, u32[]{:S(2)}) collective-permute-start(bf16[3,2,256,384]{3,2,1,0:T(8,128)(2,1)} %slice.24), channel_id=1, source_target_pairs={{0,30},{2,0},{4,2},{6,4},{8,6},{10,8},{12,10},{14,12},{16,14},{18,... | collective-permute-start | bytes 3538952 | tf_op jit(solution)/shard_map/ppermute | solution.py:16
  8.7 1.9 %copy-start = (bf16[8,2,256,384]{3,2,1,0:T(8,128)(2,1)S(1)}, bf16[8,2,256,384]{3,2,1,0:T(8,128)(2,1)}, u32[]{:S(2)}) copy-start(bf16[8,2,256,384]{3,2,1,0:T(8,128)(2,1)} %refs_4_.1) | copy-start | bytes 9437188
  10.6 12.0 %copy-start.1 = (bf16[8,2,256,384]{3,2,1,0:T(8,128)(2,1)S(1)}, bf16[8,2,256,384]{3,2,1,0:T(8,128)(2,1)}, u32[]{:S(2)}) copy-start(bf16[8,2,256,384]{3,2,1,0:T(8,128)(2,1)} %refs_4_.1) | copy-start | bytes 9437188
  10.6 12.0 %copy-start.8 = (s32[16]{0:T(128)S(1)}, s32[16]{0:T(128)}, u32[]{:S(2)}) copy-start(s32[16]{0:T(128)} %refs_1_.3) | copy-start | bytes 196
  16.9 0.7 %copy-start.3 = (f32[5,3,16,96]{3,2,1,0:T(8,128)}, f32[5,3,16,96]{3,2,1,0:T(8,128)S(1)}, u32[]{:S(2)}) copy-start(f32[5,3,16,96]{3,2,1,0:T(8,128)S(1)} %get-tuple-element.14) | copy-start | bytes 276484
  17.5 5.0 %copy-start.6 = (f32[3,16,128]{2,1,0:T(8,128)}, f32[3,16,128]{2,1,0:T(8,128)S(1)}, u32[]{:S(2)}) copy-start(f32[3,16,128]{2,1,0:T(8,128)S(1)} %get-tuple-element.12.refs_3_) | copy-start | bytes 73732
  22.5 0.7 %copy-start.4 = (f32[3,16,128]{2,1,0:T(8,128)S(1)}, f32[3,16,128]{2,1,0:T(8,128)}, u32[]{:S(2)}) copy-start(f32[3,16,128]{2,1,0:T(8,128)} %slice.23.refs_2_) | copy-start | bytes 73732
  23.3 0.7 %copy-start.7 = (f32[3,16,128]{2,1,0:T(8,128)S(1)}, f32[3,16,128]{2,1,0:T(8,128)}, u32[]{:S(2)}) copy-start(f32[3,16,128]{2,1,0:T(8,128)} %copy-done.6) | copy-start | bytes 73732
  28.9 0.7 %copy-start.2 = (f32[16,16,128]{2,1,0:T(8,128)}, f32[16,16,128]{2,1,0:T(8,128)S(1)}, u32[]{:S(2)}) copy-start(f32[16,16,128]{2,1,0:T(8,128)S(1)} %get-tuple-element.16) | copy-start | bytes 393220
  29.5 0.6 %copy-start.5 = (f32[3,3,16,96]{3,2,1,0:T(8,128)}, f32[3,3,16,96]{3,2,1,0:T(8,128)S(1)}, u32[]{:S(2)}) copy-start(f32[3,3,16,96]{3,2,1,0:T(8,128)S(1)} %get-tuple-element.15) | copy-start | bytes 165892
  30.2 13.9 %all-to-all-start = ((f32[16,16,128]{2,1,0:T(8,128)}), f32[16,16,128]{2,1,0:T(8,128)S(1)}, u32[]{:S(2)}, u32[]{:S(2)}) async-start(f32[16,16,128]{2,1,0:T(8,128)} %copy-done.2), calls=%async_computation | async-start | bytes 262144 | tf_op jit(solution)/shard_map/all_to_all | solution.py:239

commit v5 on v4

--- a/solution.py
+++ b/solution.py
@@ -26,7 +26,7 @@
     return out + jnp.dot(lo, pool, preferred_element_type=jnp.float32)
 
 
-def make_kernel(images, first, dates, rows, cols, known, tiles):
+def make_kernel(images, first, dates, rows, cols, known, tiles, date0, pw_base):
     groups = rows // LR
     cells = cols // LA
     total = len(images)
@@ -38,17 +38,20 @@
         off_ref = refs[0]
         if known:
             owner_ref, pw_in, ws_in = refs[1:4]
-            srcs = refs[4 : 4 + nsrc]
-            rest = refs[4 + nsrc :]
+            srcs = refs[6 : 6 + nsrc]
+            rest = refs[6 + nsrc :]
+            ifg_ref, coh_ref, last_ref = rest[:3]
+            raw, xf, pacc, racc, pw, racc_pooled, ifg_s, coh_s, pay, ws_s, sem, osem = rest[3:]
         else:
             srcs = refs[1 : 1 + nsrc]
             rest = refs[1 + nsrc :]
-        ifg_ref, coh_ref, last_ref = rest[:3]
-        if known:
-            raw, xf, pacc, racc, pw, racc_pooled, sem = rest[3:]
-        else:
-            pw_out = rest[3]
-            raw, xf, pacc, racc, pw, racc_pooled, sem = rest[4:]
+            ifg_ref, coh_ref, last_ref, pw_out = rest[:4]
+            raw, xf, pacc, racc, pw, racc_pooled, ifg_s, coh_s, sem, osem = rest[4:]
+        if known:
+            pw_cp = pltpu.make_async_copy(pw_in.at[pl.ds(pw_base, known)], pw.at[pl.ds(0, known)], osem.at[0])
+            ws_cp = pltpu.make_async_copy(ws_in, ws_s, osem.at[1])
+            pw_cp.start()
+            ws_cp.start()
         copies = []
         for t, (src, lead) in enumerate(images):
             cp = pltpu.make_async_copy(srcs[src].at[lead], raw.at[t], sem.at[t])
@@ -96,7 +99,7 @@
             fresh, groups, lanes
         )
         if known:
-            pw[pl.ds(0, known)] = pw_in[...]
+            pw_cp.wait()
         else:
             pw_out[...] = pw[...]
 
@@ -124,7 +127,7 @@
         lax.fori_loop(0, dates, pairs, 0)
         pooled = split_pool(racc[...].reshape(dates * NB * 2 * groups, cols), pool)
         pooled = pooled.reshape(dates, NB, 2, groups, lanes)
-        ifg_ref[...] = pooled[..., :cells]
+        ifg_s[...] = pooled[..., :cells]
 
         def coher(i, ws):
             wr, wi, wc = ws
@@ -134,7 +137,7 @@
                 re = pooled_at(i, k, 0)
                 im = pooled_at(i, k, 1)
                 co = jnp.sqrt(re * re + im * im) / jnp.sqrt(pa * pb + 1e-06)
-                coh_ref[i, k] = co[:, :cells]
+                coh_s[i, k] = co[:, :cells]
                 wr = wr + co * re
                 wi = wi + co * im
                 wc = wc + co
@@ -147,14 +150,23 @@
 
         zero = jnp.zeros((groups, lanes), jnp.float32)
         if known:
-            start = (ws_in[0], ws_in[1], ws_in[2])
+            ws_cp.wait()
+            start = (ws_s[0], ws_s[1], ws_s[2])
         else:
             start = (zero, zero, zero)
         wr, wi, wc = lax.fori_loop(0, dates, coher, start)
+        outs = [
+            pltpu.make_async_copy(ifg_s, ifg_ref.at[pl.ds(date0, dates)], osem.at[2]),
+            pltpu.make_async_copy(coh_s, coh_ref.at[pl.ds(date0, dates)], osem.at[3]),
+        ]
+        for cp in outs:
+            cp.start()
         if not known:
             last_ref[0] = wr
             last_ref[1] = wi
             last_ref[2] = wc
+            for cp in outs:
+                cp.wait()
             return
         width = cells // tiles
         lane = lax.broadcasted_iota(jnp.int32, (groups, lanes), 1)
@@ -169,12 +181,17 @@
                     jnp.where(lane < 3 * width, pltpu.roll(wc, (lanes + 2 * width - base) % lanes, 1), 0.0),
                 ),
             )
-            last_ref[owner_ref[t]] = block
+            pay[owner_ref[t]] = block
+        pay_cp = pltpu.make_async_copy(pay, last_ref, osem.at[4])
+        pay_cp.start()
+        for cp in outs:
+            cp.wait()
+        pay_cp.wait()
 
     return kernel
 
 
-def local_math(offsets, sources, images, first, dates, known=None):
+def local_math(offsets, sources, images, first, dates, count, date0, known=None):
     _, _, rows, cols = sources[0].shape
     groups = rows // LR
     cells = cols // LA
@@ -182,38 +199,52 @@
     lanes = 128
     vmem = pltpu.VMEM
     smem = pltpu.SMEM
+    anyspace = pl.BlockSpec(memory_space=pl.ANY)
+    hbm = pl.BlockSpec(memory_space=pltpu.HBM)
+    full = [
+        jax.ShapeDtypeStruct((count, NB, 2, groups, cells), jnp.float32),
+        jax.ShapeDtypeStruct((count, NB, groups, cells), jnp.float32),
+    ]
+    scratch = [
+        pltpu.VMEM((total, 2, rows, cols), jnp.bfloat16),
+        pltpu.VMEM((total, 2, rows, cols), jnp.float32),
+        None,
+        pltpu.VMEM((dates, NB, 2, groups, cols), jnp.float32),
+        pltpu.VMEM((total, groups, lanes), jnp.float32),
+        pltpu.VMEM((dates, NB, 2, groups, lanes), jnp.float32),
+        pltpu.VMEM((dates, NB, 2, groups, cells), jnp.float32),
+        pltpu.VMEM((dates, NB, groups, cells), jnp.float32),
+    ]
     if known is None:
-        nknown, tiles, extra = 0, 0, []
-        last = jax.ShapeDtypeStruct((3, groups, lanes), jnp.float32)
-        outs_extra = [jax.ShapeDtypeStruct((total, groups, lanes), jnp.float32)]
+        nknown, tiles, pw_base = 0, 0, 0
+        out_shape = full + [
+            jax.ShapeDtypeStruct((3, groups, lanes), jnp.float32),
+            jax.ShapeDtypeStruct((total, groups, lanes), jnp.float32),
+        ]
+        out_specs = [anyspace, anyspace, pl.BlockSpec(memory_space=vmem), pl.BlockSpec(memory_space=vmem)]
+        in_specs = [pl.BlockSpec(memory_space=smem)] + [hbm for _ in sources]
+        extra = []
+        aliases = {}
     else:
-        owner, pw_in, ws_in = known
-        nknown, tiles, extra = pw_in.shape[0], owner.shape[0], [owner, pw_in, ws_in]
-        last = jax.ShapeDtypeStruct((tiles, groups, lanes), jnp.float32)
-        outs_extra = []
-    out_shape = [
-        jax.ShapeDtypeStruct((dates, NB, 2, groups, cells), jnp.float32),
-        jax.ShapeDtypeStruct((dates, NB, groups, cells), jnp.float32),
-        last,
-    ] + outs_extra
-    in_specs = [pl.BlockSpec(memory_space=smem)]
-    if known is not None:
-        in_specs += [pl.BlockSpec(memory_space=smem), pl.BlockSpec(memory_space=vmem), pl.BlockSpec(memory_space=vmem)]
-    in_specs += [pl.BlockSpec(memory_space=pl.ANY) for _ in sources]
+        owner, pw_in, ws_in, ifg_in, coh_in, pw_base = known
+        nknown, tiles = NB, owner.shape[0]
+        out_shape = full + [jax.ShapeDtypeStruct((tiles, groups, lanes), jnp.float32)]
+        out_specs = [anyspace, anyspace, anyspace]
+        in_specs = [pl.BlockSpec(memory_space=smem), pl.BlockSpec(memory_space=smem)] + [
+            anyspace for _ in range(4)
+        ] + [hbm for _ in sources]
+        extra = [owner, pw_in, ws_in, ifg_in, coh_in]
+        aliases = {4: 0, 5: 1}
+        scratch += [pltpu.VMEM((tiles, groups, lanes), jnp.float32), pltpu.VMEM((3, groups, lanes), jnp.float32)]
+    scratch[2] = pltpu.VMEM((total - nknown, groups, cols), jnp.float32)
+    scratch += [pltpu.SemaphoreType.DMA((total,)), pltpu.SemaphoreType.DMA((5,))]
     return pl.pallas_call(
-        make_kernel(images, first, dates, rows, cols, nknown, tiles),
+        make_kernel(images, first, dates, rows, cols, nknown, tiles, date0, pw_base),
         out_shape=tuple(out_shape),
         in_specs=in_specs,
-        out_specs=tuple(pl.BlockSpec(memory_space=vmem) for _ in out_shape),
-        scratch_shapes=[
-            pltpu.VMEM((total, 2, rows, cols), jnp.bfloat16),
-            pltpu.VMEM((total, 2, rows, cols), jnp.float32),
-            pltpu.VMEM((total - nknown, groups, cols), jnp.float32),
-            pltpu.VMEM((dates, NB, 2, groups, cols), jnp.float32),
-            pltpu.VMEM((total, groups, lanes), jnp.float32),
-            pltpu.VMEM((dates, NB, 2, groups, lanes), jnp.float32),
-            pltpu.SemaphoreType.DMA((total,)),
-        ],
+        out_specs=tuple(out_specs),
+        scratch_shapes=scratch,
+        input_output_aliases=aliases,
         compiler_params=pltpu.CompilerParams(vmem_limit_bytes=48 * 1024 * 1024),
     )(offsets, *extra, *sources)
 
@@ -223,18 +254,18 @@
     inner = count - NB
     rim = shifted(slc[:NB], "date", -1)
     ifg_a, coh_a, ws_a, pw_a = local_math(
-        offsets[:inner], [slc], [(0, t) for t in range(count)], 0, inner
+        offsets[:inner], [slc], [(0, t) for t in range(count)], 0, inner, count, 0
     )
-    ifg_b, coh_b, slotted = local_math(
+    interferograms, coherence, slotted = local_math(
         offsets[inner:],
         [slc, rim],
         [(0, inner + t) for t in range(NB)] + [(1, t) for t in range(NB)],
         0,
         NB,
-        known=(owner, pw_a[inner:], ws_a),
+        count,
+        inner,
+        known=(owner, pw_a, ws_a, ifg_a, coh_a, inner),
     )
-    interferograms = jnp.concatenate([ifg_a, ifg_b], 0)
-    coherence = jnp.concatenate([coh_a, coh_b], 0)
     width = ifg_a.shape[-1] // owner.shape[0]
     sums = lax.all_to_all(slotted, "date", split_axis=0, concat_axis=0, tiled=True).sum(0)
     network_mean = (

time: 45.5 us -> 43 us (0.945)
  blocking collectives: 0 us -> 13.7 us
  starting transfers between devices: 11.4 us -> 5.44 us
  waiting for transfers between devices: 9.79 us -> 4.82 us
  local copies, waits for them, and re-layouts: 9.5 us -> 5.48 us
  other arithmetic: 2.44 us -> 0.03 us
  Pallas kernels: 11.2 us -> 12.6 us
    all_to_all x0 -> x1, blocking collectives: none -> 13.7 us  [on_device(): lax.all_to_all(slotted, 'date', split_axis=0, concat_axis=0, tiled=True)]
    all_to_all x1 -> x0, starting transfers between devices: 5.99 us -> none  [on_device(): lax.all_to_all(slotted, 'date', split_axis=0, concat_axis=0, tiled=True)]
    all_to_all x1 -> x0, waiting for transfers between devices: 5.49 us -> none  [on_device(): lax.all_to_all(slotted, 'date', split_axis=0, concat_axis=0, tiled=True)]
    unnamed x24 -> x12, local copies, waits for them, and re-layouts: 6.17 us -> 2.77 us
    concatenate x2 -> x0, other arithmetic: 2.41 us -> none  [the longest x1 1.63 us: on_device(): coherence = jnp.concatenate([coh_a, coh_b], 0)]
    pallas_call x2, Pallas kernels: 11.2 us -> 12.6 us  [local_math(): pl.pallas_call(make_kernel(images, first, dates, rows, cols, nknown, tile...]
    slice x1 -> x0, local copies, waits for them, and re-layouts: 0.61 us -> none  [on_device(): pw_a[inner:]]
    ppermute x1, waiting for transfers between devices: 4.3 us -> 4.82 us  [shifted(): return lax.ppermute(value, axis, pairs)]
  transfers between devices with their start and end apart: 2 -> 1, of which waited for: 2 -> 1; matrix products, arithmetic and copies ran while one was open for 7% -> 1% of each run, Pallas kernels for 14% -> 17%
where the time goes in v5:
time: 43 us; the launch traced here: 42.7 us
  blocking collectives  13.7 us (32%)
  Pallas kernels  12.6 us (29%)
  local copies, waits for them, and re-layouts  5.48 us (13%)
  starting transfers between devices  5.44 us (13%)
  waiting for transfers between devices  4.82 us (11%)
  between operations  0.67 us (2%)
    all_to_all x1, blocking collectives, on_device(): lax.all_to_all(slotted, 'date', split_axis=0, concat_axis=0, tiled=True)  13.7 us
    pallas_call x2, Pallas kernels, local_math(): pl.pallas_call(make_kernel(images, first, dates, rows, cols, nknown, tile...  12.6 us
    ppermute x1, starting transfers between devices, shifted(): return lax.ppermute(value, axis, pairs)  5.44 us
    ppermute x1, waiting for transfers between devices, shifted(): return lax.ppermute(value, axis, pairs)  4.82 us
    unnamed x12, local copies, waits for them, and re-layouts  2.77 us
    slice x1, local copies, waits for them, and re-layouts, on_device(): rim = shifted(slc[:NB], 'date', -1)  2.41 us
  transfers between devices with their start and end apart: 1, of which 1 were waited for; matrix products, arithmetic and copies ran while one was open for 1% of the time, Pallas kernels for 17%

profile of v5, /device:TPU:0, one launch (start us, length us, event | category | flops | bytes accessed | tf_op | source)
XLA Modules:
  0.0 42.7 jit_solution(6199436302657811402)
XLA Ops:
  0.6 0.0 copy-start.3
  0.6 2.4 %slice.20 = bf16[3,2,256,384]{3,2,1,0:T(8,128)(2,1)} slice(bf16[8,2,256,384]{3,2,1,0:T(8,128)(2,1)} %refs_6_.1), slice={[0:3], [0:2], [0:256], [0:384]} | slice | bytes 2359296 | tf_op jit(solution)/shard_map/slice | solution.py:255
  3.0 5.4 %collective-permute-start = (bf16[3,2,256,384]{3,2,1,0:T(8,128)(2,1)}, bf16[3,2,256,384]{3,2,1,0:T(8,128)(2,1)}, u32[]{:S(2)}, u32[]{:S(2)}) collective-permute-start(bf16[3,2,256,384]{3,2,1,0:T(8,128)(2,1)} %slice.20), channel_id=1, source_target_pairs={{0,30},{2,0},{4,2},{6,4},{8,6},{10,8},{12,10},{14,12},{16,14},{18,... | collective-permute-start | bytes 3538952 | tf_op jit(solution)/shard_map/ppermute | solution.py:16
  8.5 0.0 copy-done.3
  8.5 0.1 slice.18
  8.6 0.1 copy.24.refs_0_
  8.7 0.0 copy-start
  8.7 1.9 %copy-done = bf16[8,2,256,384]{3,2,1,0:T(8,128)(2,1)S(1)} copy-done((bf16[8,2,256,384]{3,2,1,0:T(8,128)(2,1)S(1)}, bf16[8,2,256,384]{3,2,1,0:T(8,128)(2,1)}, u32[]{:S(2)}) %copy-start) | copy-done | bytes 3145752
  10.5 0.0 copy-start.1
  10.6 0.0 copy-start.2
  10.6 7.1 %shard_map.58 = (f32[8,3,2,16,96]{4,3,2,1,0:T(8,128)}, f32[8,3,16,96]{3,2,1,0:T(8,128)}, f32[3,16,128]{2,1,0:T(8,128)S(1)}, f32[8,16,128]{2,1,0:T(8,128)S(1)}) custom-call(s32[5,3]{1,0:T(8,128)S(1)} %copy.24.refs_0_, bf16[8,2,256,384]{3,2,1,0:T(8,128)(2,1)S(1)} %copy-done), custom_call_target="tpu_custom_call" | custom-call | tf_op jit(solution)/shard_map/pallas_call | solution.py:241
  17.6 0.1 copy.23.refs_0_
  17.7 4.8 %collective-permute-done.refs_7_ = bf16[3,2,256,384]{3,2,1,0:T(8,128)(2,1)} collective-permute-done((bf16[3,2,256,384]{3,2,1,0:T(8,128)(2,1)}, bf16[3,2,256,384]{3,2,1,0:T(8,128)(2,1)}, u32[]{:S(2)}, u32[]{:S(2)}) %collective-permute-start) | collective-permute-done | bytes 1179680 | tf_op jit(solution)/shard_map/ppermute | solution.py:16
  22.5 0.0 copy-done.1
  22.5 0.0 copy-done.2
  22.5 5.5 %shard_map.59 = (f32[8,3,2,16,96]{4,3,2,1,0:T(8,128)}, f32[8,3,16,96]{3,2,1,0:T(8,128)}, f32[16,16,128]{2,1,0:T(8,128)S(1)}) custom-call(s32[3,3]{1,0:T(4,128)S(1)} %copy.23.refs_0_, s32[16]{0:T(128)S(1)} %copy-done.2, f32[8,16,128]{2,1,0:T(8,128)S(1)} %get-tuple-element.10.refs_2_, ...), custom_call_target="tpu_custom_call", output_to_operand_aliasing={{0}: (4, {}), {1}: (5, {})} | custom-call | tf_op jit(solution)/shard_map/pallas_call | solution.py:241
  28.1 13.7 %all_to_all.5 = f32[16,16,128]{2,1,0:T(8,128)S(1)} all-to-all(f32[16,16,128]{2,1,0:T(8,128)S(1)} %get-tuple-element.16), channel_id=1, replica_groups=mesh['date'=16,'strip'=2] {'date'}, dimensions={0} | all-to-all | bytes 262144 | tf_op jit(solution)/shard_map/all_to_all | solution.py:270
  41.8 0.1 fusion
  41.9 0.1 copy.25
  42.0 0.1 copy.19
  42.0 0.1 copy.20
  42.1 0.6 %copy.22 = f32[1,2,16,6]{2,1,3,0:T(2,128)} copy(f32[1,2,16,6]{2,3,1,0:T(8,128)S(1)} %maximum_divide_fusion) | data formatting | bytes 1536
  (3 shorter events, 0.0 us)
Async XLA Ops:
  0.6 7.9 %copy-start.3 = (s32[8,3]{0,1:T(4,128)S(1)}, s32[8,3]{0,1:T(4,128)}, u32[]{:S(2)}) copy-start(s32[8,3]{0,1:T(4,128)} %param.4) | copy-start | bytes 292
  3.0 19.5 %collective-permute-start = (bf16[3,2,256,384]{3,2,1,0:T(8,128)(2,1)}, bf16[3,2,256,384]{3,2,1,0:T(8,128)(2,1)}, u32[]{:S(2)}, u32[]{:S(2)}) collective-permute-start(bf16[3,2,256,384]{3,2,1,0:T(8,128)(2,1)} %slice.20), channel_id=1, source_target_pairs={{0,30},{2,0},{4,2},{6,4},{8,6},{10,8},{12,10},{14,12},{16,14},{18,... | collective-permute-start | bytes 3538952 | tf_op jit(solution)/shard_map/ppermute | solution.py:16
  8.7 1.9 %copy-start = (bf16[8,2,256,384]{3,2,1,0:T(8,128)(2,1)S(1)}, bf16[8,2,256,384]{3,2,1,0:T(8,128)(2,1)}, u32[]{:S(2)}) copy-start(bf16[8,2,256,384]{3,2,1,0:T(8,128)(2,1)} %refs_6_.1) | copy-start | bytes 9437188
  10.5 12.0 %copy-start.1 = (bf16[8,2,256,384]{3,2,1,0:T(8,128)(2,1)S(1)}, bf16[8,2,256,384]{3,2,1,0:T(8,128)(2,1)}, u32[]{:S(2)}) copy-start(bf16[8,2,256,384]{3,2,1,0:T(8,128)(2,1)} %refs_6_.1) | copy-start | bytes 9437188
  10.6 12.0 %copy-start.2 = (s32[16]{0:T(128)S(1)}, s32[16]{0:T(128)}, u32[]{:S(2)}) copy-start(s32[16]{0:T(128)} %refs_1_.3) | copy-start | bytes 196

commit v6 on v5

--- a/solution.py
+++ b/solution.py
@@ -249,10 +249,25 @@
     )(offsets, *extra, *sources)
 
 
+def head_of(slc):
+    def kernel(src, out, sem):
+        cp = pltpu.make_async_copy(src.at[pl.ds(0, NB)], out, sem.at[0])
+        cp.start()
+        cp.wait()
+
+    return pl.pallas_call(
+        kernel,
+        out_shape=jax.ShapeDtypeStruct((NB,) + slc.shape[1:], slc.dtype),
+        in_specs=[pl.BlockSpec(memory_space=pltpu.HBM)],
+        out_specs=pl.BlockSpec(memory_space=pl.ANY),
+        scratch_shapes=[pltpu.SemaphoreType.DMA((1,))],
+    )(slc)
+
+
 def on_device(slc, offsets, owner):
     count = slc.shape[0]
     inner = count - NB
-    rim = shifted(slc[:NB], "date", -1)
+    rim = shifted(head_of(slc), "date", -1)
     ifg_a, coh_a, ws_a, pw_a = local_math(
         offsets[:inner], [slc], [(0, t) for t in range(count)], 0, inner, count, 0
     )

time: 43 us -> 77.4 us (1.80)
  Pallas kernels: 12.6 us -> 49.4 us
  local copies, waits for them, and re-layouts: 5.48 us -> 1.19 us
  waiting for transfers between devices: 4.82 us -> 6.7 us
    pallas_call x0 -> x1, Pallas kernels: none -> 36.8 us  [head_of(): pl.pallas_call(kernel, out_shape=jax.ShapeDtypeStruct((NB,) + slc.shape[1...]
    slice x1 -> x0, local copies, waits for them, and re-layouts: 2.41 us -> none  [on_device(): rim = shifted(slc[:NB], 'date', -1)]
    unnamed x12 -> x10, local copies, waits for them, and re-layouts: 2.77 us -> 0.88 us
    ppermute x1, waiting for transfers between devices: 4.82 us -> 6.7 us  [shifted(): return lax.ppermute(value, axis, pairs)]
  transfers between devices with their start and end apart: 1 -> 1, of which waited for: 1 -> 1; matrix products, arithmetic and copies ran while one was open for 1% -> 0% of each run, Pallas kernels for 17% -> 9%
where the time goes in v6:
time: 77.4 us; the launch traced here: 77.2 us
  Pallas kernels  49.4 us (64%)
  blocking collectives  13.7 us (18%)
  waiting for transfers between devices  6.7 us (9%)
  starting transfers between devices  5.5 us (7%)
  local copies, waits for them, and re-layouts  1.19 us (2%)
    pallas_call x1, Pallas kernels, head_of(): pl.pallas_call(kernel, out_shape=jax.ShapeDtypeStruct((NB,) + slc.shape[1...  36.8 us
    all_to_all x1, blocking collectives, on_device(): lax.all_to_all(slotted, 'date', split_axis=0, concat_axis=0, tiled=True)  13.7 us
    pallas_call x2, Pallas kernels, local_math(): pl.pallas_call(make_kernel(images, first, dates, rows, cols, nknown, tile...  12.6 us
    ppermute x1, waiting for transfers between devices, shifted(): return lax.ppermute(value, axis, pairs)  6.7 us
    ppermute x1, starting transfers between devices, shifted(): return lax.ppermute(value, axis, pairs)  5.5 us
  transfers between devices with their start and end apart: 1, of which 1 were waited for; matrix products, arithmetic and copies ran while one was open for 0% of the time, Pallas kernels for 9%

profile of v6, /device:TPU:0, one launch (start us, length us, event | category | flops | bytes accessed | tf_op | source)
XLA Modules:
  0.0 77.2 jit_solution(11374360974825291962)
XLA Ops:
  0.6 0.0 copy-start
  0.6 0.0 copy-start.2
  0.6 36.8 %shard_map.59 = bf16[3,2,256,384]{3,2,1,0:T(8,128)(2,1)} custom-call(bf16[8,2,256,384]{3,2,1,0:T(8,128)(2,1)} %refs_6_.1), custom_call_target="tpu_custom_call" | custom-call | tf_op jit(solution)/shard_map/pallas_call | solution.py:258
  37.5 5.5 %collective-permute-start = (bf16[3,2,256,384]{3,2,1,0:T(8,128)(2,1)}, bf16[3,2,256,384]{3,2,1,0:T(8,128)(2,1)}, u32[]{:S(2)}, u32[]{:S(2)}) collective-permute-start(bf16[3,2,256,384]{3,2,1,0:T(8,128)(2,1)} %shard_map.59), channel_id=1, source_target_pairs={{0,30},{2,0},{4,2},{6,4},{8,6},{10,8},{12,10},{14,12},{16,14},{18,... | collective-permute-start | bytes 3538952 | tf_op jit(solution)/shard_map/ppermute | solution.py:16
  43.0 0.0 copy-done.2
  43.0 0.1 slice.15
  43.1 0.1 copy.24.refs_0_
  43.2 0.0 copy-done
  43.2 0.0 copy-start.1
  43.2 7.1 %shard_map.58 = (f32[8,3,2,16,96]{4,3,2,1,0:T(8,128)}, f32[8,3,16,96]{3,2,1,0:T(8,128)}, f32[3,16,128]{2,1,0:T(8,128)S(1)}, f32[8,16,128]{2,1,0:T(8,128)S(1)}) custom-call(s32[5,3]{1,0:T(8,128)S(1)} %copy.24.refs_0_, bf16[8,2,256,384]{3,2,1,0:T(8,128)(2,1)S(1)} %copy-done), custom_call_target="tpu_custom_call" | custom-call | tf_op jit(solution)/shard_map/pallas_call | solution.py:241
  50.2 0.1 copy.23.refs_0_
  50.3 6.7 %collective-permute-done.refs_7_ = bf16[3,2,256,384]{3,2,1,0:T(8,128)(2,1)} collective-permute-done((bf16[3,2,256,384]{3,2,1,0:T(8,128)(2,1)}, bf16[3,2,256,384]{3,2,1,0:T(8,128)(2,1)}, u32[]{:S(2)}, u32[]{:S(2)}) %collective-permute-start) | collective-permute-done | bytes 1179680 | tf_op jit(solution)/shard_map/ppermute | solution.py:16
  57.0 0.0 copy-done.1
  57.0 5.5 %shard_map.60 = (f32[8,3,2,16,96]{4,3,2,1,0:T(8,128)}, f32[8,3,16,96]{3,2,1,0:T(8,128)}, f32[16,16,128]{2,1,0:T(8,128)S(1)}) custom-call(s32[3,3]{1,0:T(4,128)S(1)} %copy.23.refs_0_, s32[16]{0:T(128)S(1)} %copy-done.1, f32[8,16,128]{2,1,0:T(8,128)S(1)} %get-tuple-element.10.refs_2_, ...), custom_call_target="tpu_custom_call", output_to_operand_aliasing={{0}: (4, {}), {1}: (5, {})} | custom-call | tf_op jit(solution)/shard_map/pallas_call | solution.py:241
  62.6 13.7 %all_to_all.5 = f32[16,16,128]{2,1,0:T(8,128)S(1)} all-to-all(f32[16,16,128]{2,1,0:T(8,128)S(1)} %get-tuple-element.16), channel_id=1, replica_groups=mesh['date'=16,'strip'=2] {'date'}, dimensions={0} | all-to-all | bytes 262144 | tf_op jit(solution)/shard_map/all_to_all | solution.py:285
  76.3 0.1 fusion
  76.4 0.1 copy.25
  76.5 0.1 copy.19
  76.5 0.1 copy.20
  76.6 0.6 copy.22
  (3 shorter events, 0.0 us)
Async XLA Ops:
  0.6 42.5 %copy-start = (bf16[8,2,256,384]{3,2,1,0:T(8,128)(2,1)S(1)}, bf16[8,2,256,384]{3,2,1,0:T(8,128)(2,1)}, u32[]{:S(2)}) copy-start(bf16[8,2,256,384]{3,2,1,0:T(8,128)(2,1)} %refs_6_.1) | copy-start | bytes 9437188
  0.6 42.4 %copy-start.2 = (s32[8,3]{0,1:T(4,128)S(1)}, s32[8,3]{0,1:T(4,128)}, u32[]{:S(2)}) copy-start(s32[8,3]{0,1:T(4,128)} %param.4) | copy-start | bytes 292
  37.5 19.5 %collective-permute-start = (bf16[3,2,256,384]{3,2,1,0:T(8,128)(2,1)}, bf16[3,2,256,384]{3,2,1,0:T(8,128)(2,1)}, u32[]{:S(2)}, u32[]{:S(2)}) collective-permute-start(bf16[3,2,256,384]{3,2,1,0:T(8,128)(2,1)} %shard_map.59), channel_id=1, source_target_pairs={{0,30},{2,0},{4,2},{6,4},{8,6},{10,8},{12,10},{14,12},{16,14},{18,... | collective-permute-start | bytes 3538952 | tf_op jit(solution)/shard_map/ppermute | solution.py:16
  43.2 13.9 %copy-start.1 = (s32[16]{0:T(128)S(1)}, s32[16]{0:T(128)}, u32[]{:S(2)}) copy-start(s32[16]{0:T(128)} %refs_1_.3) | copy-start | bytes 196

commit v7 on v5

--- a/solution.py
+++ b/solution.py
@@ -37,21 +37,23 @@
     def kernel(*refs):
         off_ref = refs[0]
         if known:
-            owner_ref, pw_in, ws_in = refs[1:4]
-            srcs = refs[6 : 6 + nsrc]
-            rest = refs[6 + nsrc :]
+            owner_ref, pw_in, ws_in, rx_in = refs[1:5]
+            srcs = refs[7 : 7 + nsrc]
+            rest = refs[7 + nsrc :]
             ifg_ref, coh_ref, last_ref = rest[:3]
             raw, xf, pacc, racc, pw, racc_pooled, ifg_s, coh_s, pay, ws_s, sem, osem = rest[3:]
         else:
             srcs = refs[1 : 1 + nsrc]
             rest = refs[1 + nsrc :]
-            ifg_ref, coh_ref, last_ref, pw_out = rest[:4]
-            raw, xf, pacc, racc, pw, racc_pooled, ifg_s, coh_s, sem, osem = rest[4:]
+            ifg_ref, coh_ref, last_ref, pw_out, racc_x = rest[:5]
+            raw, xf, pacc, racc, pw, racc_pooled, ifg_s, coh_s, sem, osem = rest[5:]
         if known:
             pw_cp = pltpu.make_async_copy(pw_in.at[pl.ds(pw_base, known)], pw.at[pl.ds(0, known)], osem.at[0])
             ws_cp = pltpu.make_async_copy(ws_in, ws_s, osem.at[1])
+            rx_cp = pltpu.make_async_copy(rx_in, racc, osem.at[2])
             pw_cp.start()
             ws_cp.start()
+            rx_cp.start()
         copies = []
         for t, (src, lead) in enumerate(images):
             cp = pltpu.make_async_copy(srcs[src].at[lead], raw.at[t], sem.at[t])
@@ -106,26 +108,40 @@
         def partner(i, k):
             return jnp.clip(first + i + off_ref[i, k], 0, total - 1)
 
+        def wanted(i, k):
+            reach = first + i + off_ref[i, k]
+            if known:
+                return reach >= known
+            return jnp.logical_or(i < dates, reach <= total - 1)
+
         def pairs(i, c):
             for k in range(NB):
                 j = partner(i, k)
-                for ct in range(ctiles):
-                    for blk in range(groups // 8):
-                        re = []
-                        im = []
-                        for g in range(blk * 8, blk * 8 + 8):
-                            a0 = rows_of(first + i, 0, g, ct)
-                            a1 = rows_of(first + i, 1, g, ct)
-                            b0 = rows_of(j, 0, g, ct)
-                            b1 = rows_of(j, 1, g, ct)
-                            re.append(half(a0 * b0 + a1 * b1))
-                            im.append(half(a1 * b0 - a0 * b1))
-                        racc[i, k, 0, pl.ds(blk * 8, 8), pl.ds(ct * 128, 128)] = fold(re)
-                        racc[i, k, 1, pl.ds(blk * 8, 8), pl.ds(ct * 128, 128)] = fold(im)
+
+                @pl.when(wanted(i, k))
+                def _():
+                    for ct in range(ctiles):
+                        for blk in range(groups // 8):
+                            re = []
+                            im = []
+                            for g in range(blk * 8, blk * 8 + 8):
+                                a0 = rows_of(first + i, 0, g, ct)
+                                a1 = rows_of(first + i, 1, g, ct)
+                                b0 = rows_of(j, 0, g, ct)
+                                b1 = rows_of(j, 1, g, ct)
+                                re.append(half(a0 * b0 + a1 * b1))
+                                im.append(half(a1 * b0 - a0 * b1))
+                            racc[i, k, 0, pl.ds(blk * 8, 8), pl.ds(ct * 128, 128)] = fold(re)
+                            racc[i, k, 1, pl.ds(blk * 8, 8), pl.ds(ct * 128, 128)] = fold(im)
+
             return c
 
-        lax.fori_loop(0, dates, pairs, 0)
-        pooled = split_pool(racc[...].reshape(dates * NB * 2 * groups, cols), pool)
+        if known:
+            rx_cp.wait()
+        lax.fori_loop(0, racc.shape[0], pairs, 0)
+        if not known:
+            racc_x[...] = racc[pl.ds(dates, racc.shape[0] - dates)]
+        pooled = split_pool(racc[pl.ds(0, dates)].reshape(dates * NB * 2 * groups, cols), pool)
         pooled = pooled.reshape(dates, NB, 2, groups, lanes)
         ifg_s[...] = pooled[..., :cells]
 
@@ -156,8 +172,8 @@
             start = (zero, zero, zero)
         wr, wi, wc = lax.fori_loop(0, dates, coher, start)
         outs = [
-            pltpu.make_async_copy(ifg_s, ifg_ref.at[pl.ds(date0, dates)], osem.at[2]),
-            pltpu.make_async_copy(coh_s, coh_ref.at[pl.ds(date0, dates)], osem.at[3]),
+            pltpu.make_async_copy(ifg_s, ifg_ref.at[pl.ds(date0, dates)], osem.at[3]),
+            pltpu.make_async_copy(coh_s, coh_ref.at[pl.ds(date0, dates)], osem.at[4]),
         ]
         for cp in outs:
             cp.start()
@@ -182,7 +198,7 @@
                 ),
             )
             pay[owner_ref[t]] = block
-        pay_cp = pltpu.make_async_copy(pay, last_ref, osem.at[4])
+        pay_cp = pltpu.make_async_copy(pay, last_ref, osem.at[5])
         pay_cp.start()
         for cp in outs:
             cp.wait()
@@ -192,6 +208,7 @@
 
 
 def local_math(offsets, sources, images, first, dates, count, date0, known=None):
+    pair_dates = offsets.shape[0]
     _, _, rows, cols = sources[0].shape
     groups = rows // LR
     cells = cols // LA
@@ -209,7 +226,7 @@
         pltpu.VMEM((total, 2, rows, cols), jnp.bfloat16),
         pltpu.VMEM((total, 2, rows, cols), jnp.float32),
         None,
-        pltpu.VMEM((dates, NB, 2, groups, cols), jnp.float32),
+        pltpu.VMEM((pair_dates, NB, 2, groups, cols), jnp.float32),
         pltpu.VMEM((total, groups, lanes), jnp.float32),
         pltpu.VMEM((dates, NB, 2, groups, lanes), jnp.float32),
         pltpu.VMEM((dates, NB, 2, groups, cells), jnp.float32),
@@ -220,24 +237,25 @@
         out_shape = full + [
             jax.ShapeDtypeStruct((3, groups, lanes), jnp.float32),
             jax.ShapeDtypeStruct((total, groups, lanes), jnp.float32),
+            jax.ShapeDtypeStruct((pair_dates - dates, NB, 2, groups, cols), jnp.float32),
         ]
-        out_specs = [anyspace, anyspace, pl.BlockSpec(memory_space=vmem), pl.BlockSpec(memory_space=vmem)]
+        out_specs = [anyspace, anyspace] + [pl.BlockSpec(memory_space=vmem) for _ in range(3)]
         in_specs = [pl.BlockSpec(memory_space=smem)] + [hbm for _ in sources]
         extra = []
         aliases = {}
     else:
-        owner, pw_in, ws_in, ifg_in, coh_in, pw_base = known
+        owner, pw_in, ws_in, rx_in, ifg_in, coh_in, pw_base = known
         nknown, tiles = NB, owner.shape[0]
         out_shape = full + [jax.ShapeDtypeStruct((tiles, groups, lanes), jnp.float32)]
         out_specs = [anyspace, anyspace, anyspace]
         in_specs = [pl.BlockSpec(memory_space=smem), pl.BlockSpec(memory_space=smem)] + [
-            anyspace for _ in range(4)
+            anyspace for _ in range(5)
         ] + [hbm for _ in sources]
-        extra = [owner, pw_in, ws_in, ifg_in, coh_in]
-        aliases = {4: 0, 5: 1}
+        extra = [owner, pw_in, ws_in, rx_in, ifg_in, coh_in]
+        aliases = {5: 0, 6: 1}
         scratch += [pltpu.VMEM((tiles, groups, lanes), jnp.float32), pltpu.VMEM((3, groups, lanes), jnp.float32)]
     scratch[2] = pltpu.VMEM((total - nknown, groups, cols), jnp.float32)
-    scratch += [pltpu.SemaphoreType.DMA((total,)), pltpu.SemaphoreType.DMA((5,))]
+    scratch += [pltpu.SemaphoreType.DMA((total,)), pltpu.SemaphoreType.DMA((6,))]
     return pl.pallas_call(
         make_kernel(images, first, dates, rows, cols, nknown, tiles, date0, pw_base),
         out_shape=tuple(out_shape),
@@ -253,8 +271,8 @@
     count = slc.shape[0]
     inner = count - NB
     rim = shifted(slc[:NB], "date", -1)
-    ifg_a, coh_a, ws_a, pw_a = local_math(
-        offsets[:inner], [slc], [(0, t) for t in range(count)], 0, inner, count, 0
+    ifg_a, coh_a, ws_a, pw_a, rx_a = local_math(
+        offsets, [slc], [(0, t) for t in range(count)], 0, inner, count, 0
     )
     interferograms, coherence, slotted = local_math(
         offsets[inner:],
@@ -264,7 +282,7 @@
         NB,
         count,
         inner,
-        known=(owner, pw_a, ws_a, ifg_a, coh_a, inner),
+        known=(owner, pw_a, ws_a, rx_a, ifg_a, coh_a, inner),
     )
     width = ifg_a.shape[-1] // owner.shape[0]
     sums = lax.all_to_all(slotted, "date", split_axis=0, concat_axis=0, tiled=True).sum(0)

time: 43 us -> 41.1 us (0.956)
  local copies, waits for them, and re-layouts: 5.48 us -> 4.3 us
  waiting for transfers between devices: 4.82 us -> 4.04 us
    slice x1, local copies, waits for them, and re-layouts: 2.41 us -> 1.4 us  [on_device(): rim = shifted(slc[:NB], 'date', -1)]
    ppermute x1, waiting for transfers between devices: 4.82 us -> 4.04 us  [shifted(): return lax.ppermute(value, axis, pairs)]
    unnamed x12 -> x11, local copies, waits for them, and re-layouts: 2.77 us -> 2.67 us
  transfers between devices with their start and end apart: 1 -> 1, of which waited for: 1 -> 1; matrix products, arithmetic and copies ran while one was open for 1% -> 0% of each run, Pallas kernels for 17% -> 19%
where the time goes in v7:
time: 41.1 us
  blocking collectives  13.7 us (33%)
  Pallas kernels  12.9 us (31%)
  starting transfers between devices  5.5 us (13%)
  local copies, waits for them, and re-layouts  4.3 us (10%)
  waiting for transfers between devices  4.04 us (10%)
  between operations  0.67 us (2%)
    all_to_all x1, blocking collectives, on_device(): lax.all_to_all(slotted, 'date', split_axis=0, concat_axis=0, tiled=True)  13.7 us
    pallas_call x2, Pallas kernels, local_math(): pl.pallas_call(make_kernel(images, first, dates, rows, cols, nknown, tile...  12.9 us
    ppermute x1, starting transfers between devices, shifted(): return lax.ppermute(value, axis, pairs)  5.5 us
    ppermute x1, waiting for transfers between devices, shifted(): return lax.ppermute(value, axis, pairs)  4.04 us
    unnamed x11, local copies, waits for them, and re-layouts  2.67 us
    slice x1, local copies, waits for them, and re-layouts, on_device(): rim = shifted(slc[:NB], 'date', -1)  1.4 us
  transfers between devices with their start and end apart: 1, of which 1 were waited for; matrix products, arithmetic and copies ran while one was open for 0% of the time, Pallas kernels for 19%

profile of v7, /device:TPU:0, one launch (start us, length us, event | category | flops | bytes accessed | tf_op | source)
XLA Modules:
  0.0 41.1 jit_solution(11333438671097681288)
XLA Ops:
  0.6 0.0 copy-start.3
  0.6 1.4 %slice.16 = bf16[3,2,256,384]{3,2,1,0:T(8,128)(2,1)S(1)} slice(bf16[8,2,256,384]{3,2,1,0:T(8,128)(2,1)} %refs_7_.1), slice={[0:3], [0:2], [0:256], [0:384]} | slice | bytes 2359296 | tf_op jit(solution)/shard_map/slice | solution.py:273
  2.0 5.5 %collective-permute-start = (bf16[3,2,256,384]{3,2,1,0:T(8,128)(2,1)S(1)}, bf16[3,2,256,384]{3,2,1,0:T(8,128)(2,1)S(1)}, u32[]{:S(2)}, u32[]{:S(2)}) collective-permute-start(bf16[3,2,256,384]{3,2,1,0:T(8,128)(2,1)S(1)} %slice.16), channel_id=1, source_target_pairs={{0,30},{2,0},{4,2},{6,4},{8,6},{10,8},{12,10},{14,12},{16,14},{18,... | collective-permute-start | bytes 3538952 | tf_op jit(solution)/shard_map/ppermute | solution.py:16
  7.5 0.0 copy-done.3
  7.5 0.1 copy.17.refs_0_
  7.6 0.0 copy-start
  7.6 1.9 %copy-done = bf16[8,2,256,384]{3,2,1,0:T(8,128)(2,1)S(1)} copy-done((bf16[8,2,256,384]{3,2,1,0:T(8,128)(2,1)S(1)}, bf16[8,2,256,384]{3,2,1,0:T(8,128)(2,1)}, u32[]{:S(2)}) %copy-start) | copy-done | bytes 3145752
  9.5 0.0 copy-start.1
  9.5 0.0 copy-start.2
  9.5 7.7 %shard_map.58 = (f32[8,3,2,16,96]{4,3,2,1,0:T(8,128)}, f32[8,3,16,96]{3,2,1,0:T(8,128)}, f32[3,16,128]{2,1,0:T(8,128)S(1)}, f32[8,16,128]{2,1,0:T(8,128)S(1)}, f32[3,3,2,16,384]{4,3,2,1,0:T(8,128)S(1)}) custom-call(s32[8,3]{1,0:T(8,128)S(1)} %copy.17.refs_0_, bf16[8,2,256,384]{3,2,1,0:T(8,128)(2,1)S(1)} %copy-done), custom_call_target="tpu_custom_call" | custom-call | tf_op jit(solution)/shard_map/pallas_call | solution.py:259
  17.2 4.0 %collective-permute-done.refs_8_ = bf16[3,2,256,384]{3,2,1,0:T(8,128)(2,1)S(1)} collective-permute-done((bf16[3,2,256,384]{3,2,1,0:T(8,128)(2,1)S(1)}, bf16[3,2,256,384]{3,2,1,0:T(8,128)(2,1)S(1)}, u32[]{:S(2)}, u32[]{:S(2)}) %collective-permute-start) | collective-permute-done | bytes 1179680 | tf_op jit(solution)/shard_map/ppermute | solution.py:16
  21.3 0.0 copy-done.1
  21.3 0.0 copy-done.2
  21.3 5.2 %shard_map.59 = (f32[8,3,2,16,96]{4,3,2,1,0:T(8,128)}, f32[8,3,16,96]{3,2,1,0:T(8,128)}, f32[16,16,128]{2,1,0:T(8,128)S(1)}) custom-call(s32[3,3]{1,0:T(4,128)S(1)} %slice.15.refs_0_, s32[16]{0:T(128)S(1)} %copy-done.2, f32[8,16,128]{2,1,0:T(8,128)S(1)} %get-tuple-element.11.refs_2_, ...), custom_call_target="tpu_custom_call", output_to_operand_aliasing={{0}: (5, {}), {1}: (6, {})} | custom-call | tf_op jit(solution)/shard_map/pallas_call | solution.py:259
  26.5 13.7 %all_to_all.5 = f32[16,16,128]{2,1,0:T(8,128)S(1)} all-to-all(f32[16,16,128]{2,1,0:T(8,128)S(1)} %get-tuple-element.18), channel_id=1, replica_groups=mesh['date'=16,'strip'=2] {'date'}, dimensions={0} | all-to-all | bytes 262144 | tf_op jit(solution)/shard_map/all_to_all | solution.py:288
  40.2 0.1 fusion
  40.3 0.1 copy.23
  40.3 0.1 copy.20
  40.4 0.1 copy.19
  40.5 0.6 %copy.22 = f32[1,2,16,6]{2,1,3,0:T(2,128)} copy(f32[1,2,16,6]{2,3,1,0:T(8,128)S(1)} %maximum_divide_fusion) | data formatting | bytes 1536
  (4 shorter events, 0.0 us)
Async XLA Ops:
  0.6 6.9 %copy-start.3 = (s32[8,3]{0,1:T(4,128)S(1)}, s32[8,3]{0,1:T(4,128)}, u32[]{:S(2)}) copy-start(s32[8,3]{0,1:T(4,128)} %param.4) | copy-start | bytes 292
  2.0 19.2 %collective-permute-start = (bf16[3,2,256,384]{3,2,1,0:T(8,128)(2,1)S(1)}, bf16[3,2,256,384]{3,2,1,0:T(8,128)(2,1)S(1)}, u32[]{:S(2)}, u32[]{:S(2)}) collective-permute-start(bf16[3,2,256,384]{3,2,1,0:T(8,128)(2,1)S(1)} %slice.16), channel_id=1, source_target_pairs={{0,30},{2,0},{4,2},{6,4},{8,6},{10,8},{12,10},{14,12},{16,14},{18,... | collective-permute-start | bytes 3538952 | tf_op jit(solution)/shard_map/ppermute | solution.py:16
  7.6 1.9 %copy-start = (bf16[8,2,256,384]{3,2,1,0:T(8,128)(2,1)S(1)}, bf16[8,2,256,384]{3,2,1,0:T(8,128)(2,1)}, u32[]{:S(2)}) copy-start(bf16[8,2,256,384]{3,2,1,0:T(8,128)(2,1)} %refs_7_.1) | copy-start | bytes 9437188
  9.5 11.7 %copy-start.1 = (bf16[8,2,256,384]{3,2,1,0:T(8,128)(2,1)S(1)}, bf16[8,2,256,384]{3,2,1,0:T(8,128)(2,1)}, u32[]{:S(2)}) copy-start(bf16[8,2,256,384]{3,2,1,0:T(8,128)(2,1)} %refs_7_.1) | copy-start | bytes 9437188
  9.5 11.7 %copy-start.2 = (s32[16]{0:T(128)S(1)}, s32[16]{0:T(128)}, u32[]{:S(2)}) copy-start(s32[16]{0:T(128)} %refs_1_.3) | copy-start | bytes 196

commit v8 on v7

--- a/solution.py
+++ b/solution.py
@@ -41,12 +41,12 @@
             srcs = refs[7 : 7 + nsrc]
             rest = refs[7 + nsrc :]
             ifg_ref, coh_ref, last_ref = rest[:3]
-            raw, xf, pacc, racc, pw, racc_pooled, ifg_s, coh_s, pay, ws_s, sem, osem = rest[3:]
+            xf, pacc, racc, pw, racc_pooled, ifg_s, coh_s, pay, ws_s, osem = rest[3:]
         else:
             srcs = refs[1 : 1 + nsrc]
             rest = refs[1 + nsrc :]
             ifg_ref, coh_ref, last_ref, pw_out, racc_x = rest[:5]
-            raw, xf, pacc, racc, pw, racc_pooled, ifg_s, coh_s, sem, osem = rest[5:]
+            xf, pacc, racc, pw, racc_pooled, ifg_s, coh_s, osem = rest[5:]
         if known:
             pw_cp = pltpu.make_async_copy(pw_in.at[pl.ds(pw_base, known)], pw.at[pl.ds(0, known)], osem.at[0])
             ws_cp = pltpu.make_async_copy(ws_in, ws_s, osem.at[1])
@@ -54,14 +54,8 @@
             pw_cp.start()
             ws_cp.start()
             rx_cp.start()
-        copies = []
         for t, (src, lead) in enumerate(images):
-            cp = pltpu.make_async_copy(srcs[src].at[lead], raw.at[t], sem.at[t])
-            cp.start()
-            copies.append(cp)
-        for t in range(total):
-            copies[t].wait()
-            xf[t] = raw[t].astype(jnp.float32)
+            xf[t] = srcs[src][lead].astype(jnp.float32)
 
         line = lax.broadcasted_iota(jnp.int32, (cols, lanes), 0)
         cell = lax.broadcasted_iota(jnp.int32, (cols, lanes), 1)
@@ -217,13 +211,12 @@
     vmem = pltpu.VMEM
     smem = pltpu.SMEM
     anyspace = pl.BlockSpec(memory_space=pl.ANY)
-    hbm = pl.BlockSpec(memory_space=pltpu.HBM)
+    hbm = pl.BlockSpec(memory_space=vmem)
     full = [
         jax.ShapeDtypeStruct((count, NB, 2, groups, cells), jnp.float32),
         jax.ShapeDtypeStruct((count, NB, groups, cells), jnp.float32),
     ]
     scratch = [
-        pltpu.VMEM((total, 2, rows, cols), jnp.bfloat16),
         pltpu.VMEM((total, 2, rows, cols), jnp.float32),
         None,
         pltpu.VMEM((pair_dates, NB, 2, groups, cols), jnp.float32),
@@ -254,8 +247,8 @@
         extra = [owner, pw_in, ws_in, rx_in, ifg_in, coh_in]
         aliases = {5: 0, 6: 1}
         scratch += [pltpu.VMEM((tiles, groups, lanes), jnp.float32), pltpu.VMEM((3, groups, lanes), jnp.float32)]
-    scratch[2] = pltpu.VMEM((total - nknown, groups, cols), jnp.float32)
-    scratch += [pltpu.SemaphoreType.DMA((total,)), pltpu.SemaphoreType.DMA((6,))]
+    scratch[1] = pltpu.VMEM((total - nknown, groups, cols), jnp.float32)
+    scratch += [pltpu.SemaphoreType.DMA((6,))]
     return pl.pallas_call(
         make_kernel(images, first, dates, rows, cols, nknown, tiles, date0, pw_base),
         out_shape=tuple(out_shape),

time: 41.1 us -> 40.1 us (0.976)
  Pallas kernels: 12.9 us -> 10.1 us
  waiting for transfers between devices: 4.04 us -> 5.47 us
    pallas_call x2, Pallas kernels: 12.9 us -> 10.1 us  [local_math(): pl.pallas_call(make_kernel(images, first, dates, rows, cols, nknown, tile...]
    ppermute x1, waiting for transfers between devices: 4.04 us -> 5.47 us  [shifted(): return lax.ppermute(value, axis, pairs)]
  transfers between devices with their start and end apart: 1 -> 1, of which waited for: 1 -> 1; matrix products, arithmetic and copies ran while one was open for 0% -> 0% of each run, Pallas kernels for 19% -> 16%
where the time goes in v8:
time: 40.1 us; the launch traced here: 39.9 us
  blocking collectives  13.8 us (34%)
  Pallas kernels  10.1 us (25%)
  starting transfers between devices  5.5 us (14%)
  waiting for transfers between devices  5.47 us (14%)
  local copies, waits for them, and re-layouts  4.3 us (11%)
  between operations  0.67 us (2%)
    all_to_all x1, blocking collectives, on_device(): lax.all_to_all(slotted, 'date', split_axis=0, concat_axis=0, tiled=True)  13.8 us
    pallas_call x2, Pallas kernels, local_math(): pl.pallas_call(make_kernel(images, first, dates, rows, cols, nknown, tile...  10.1 us
    ppermute x1, starting transfers between devices, shifted(): return lax.ppermute(value, axis, pairs)  5.5 us
    ppermute x1, waiting for transfers between devices, shifted(): return lax.ppermute(value, axis, pairs)  5.47 us
    unnamed x11, local copies, waits for them, and re-layouts  2.67 us
    slice x1, local copies, waits for them, and re-layouts, on_device(): rim = shifted(slc[:NB], 'date', -1)  1.4 us
  transfers between devices with their start and end apart: 1, of which 1 were waited for; matrix products, arithmetic and copies ran while one was open for 0% of the time, Pallas kernels for 16%

profile of v8, /device:TPU:0, one launch (start us, length us, event | category | flops | bytes accessed | tf_op | source)
XLA Modules:
  0.0 39.9 jit_solution(10181788008930199002)
XLA Ops:
  0.6 0.0 copy-start.3
  0.6 1.4 %slice.16 = bf16[3,2,256,384]{3,2,1,0:T(8,128)(2,1)S(1)} slice(bf16[8,2,256,384]{3,2,1,0:T(8,128)(2,1)} %refs_7_.1), slice={[0:3], [0:2], [0:256], [0:384]} | slice | bytes 2359296 | tf_op jit(solution)/shard_map/slice | solution.py:266
  2.0 5.5 %collective-permute-start = (bf16[3,2,256,384]{3,2,1,0:T(8,128)(2,1)S(1)}, bf16[3,2,256,384]{3,2,1,0:T(8,128)(2,1)S(1)}, u32[]{:S(2)}, u32[]{:S(2)}) collective-permute-start(bf16[3,2,256,384]{3,2,1,0:T(8,128)(2,1)S(1)} %slice.16), channel_id=1, source_target_pairs={{0,30},{2,0},{4,2},{6,4},{8,6},{10,8},{12,10},{14,12},{16,14},{18,... | collective-permute-start | bytes 3538952 | tf_op jit(solution)/shard_map/ppermute | solution.py:16
  7.5 0.0 copy-done.3
  7.5 0.1 copy.17.refs_0_
  7.6 0.0 copy-start
  7.6 1.9 %copy-done = bf16[8,2,256,384]{3,2,1,0:T(8,128)(2,1)S(1)} copy-done((bf16[8,2,256,384]{3,2,1,0:T(8,128)(2,1)S(1)}, bf16[8,2,256,384]{3,2,1,0:T(8,128)(2,1)}, u32[]{:S(2)}) %copy-start) | copy-done | bytes 3145752
  9.5 0.0 copy-start.1
  9.5 0.0 copy-start.2
  9.5 6.3 %shard_map.58 = (f32[8,3,2,16,96]{4,3,2,1,0:T(8,128)}, f32[8,3,16,96]{3,2,1,0:T(8,128)}, f32[3,16,128]{2,1,0:T(8,128)S(1)}, f32[8,16,128]{2,1,0:T(8,128)S(1)}, f32[3,3,2,16,384]{4,3,2,1,0:T(8,128)S(1)}) custom-call(s32[8,3]{1,0:T(8,128)S(1)} %copy.17.refs_0_, bf16[8,2,256,384]{3,2,1,0:T(8,128)(2,1)S(1)} %copy-done), custom_call_target="tpu_custom_call" | custom-call | tf_op jit(solution)/shard_map/pallas_call | solution.py:252
  15.8 5.5 %collective-permute-done.refs_8_ = bf16[3,2,256,384]{3,2,1,0:T(8,128)(2,1)S(1)} collective-permute-done((bf16[3,2,256,384]{3,2,1,0:T(8,128)(2,1)S(1)}, bf16[3,2,256,384]{3,2,1,0:T(8,128)(2,1)S(1)}, u32[]{:S(2)}, u32[]{:S(2)}) %collective-permute-start) | collective-permute-done | bytes 1179680 | tf_op jit(solution)/shard_map/ppermute | solution.py:16
  21.3 0.0 copy-done.1
  21.3 0.0 copy-done.2
  21.3 3.9 %shard_map.59 = (f32[8,3,2,16,96]{4,3,2,1,0:T(8,128)}, f32[8,3,16,96]{3,2,1,0:T(8,128)}, f32[16,16,128]{2,1,0:T(8,128)S(1)}) custom-call(s32[3,3]{1,0:T(4,128)S(1)} %slice.15.refs_0_, s32[16]{0:T(128)S(1)} %copy-done.2, f32[8,16,128]{2,1,0:T(8,128)S(1)} %get-tuple-element.11.refs_2_, ...), custom_call_target="tpu_custom_call", output_to_operand_aliasing={{0}: (5, {}), {1}: (6, {})} | custom-call | tf_op jit(solution)/shard_map/pallas_call | solution.py:252
  25.1 13.8 %all_to_all.5 = f32[16,16,128]{2,1,0:T(8,128)S(1)} all-to-all(f32[16,16,128]{2,1,0:T(8,128)S(1)} %get-tuple-element.18), channel_id=1, replica_groups=mesh['date'=16,'strip'=2] {'date'}, dimensions={0} | all-to-all | bytes 262144 | tf_op jit(solution)/shard_map/all_to_all | solution.py:281
  39.0 0.1 fusion
  39.1 0.1 copy.23
  39.2 0.1 copy.20
  39.2 0.1 copy.19
  39.3 0.6 %copy.22 = f32[1,2,16,6]{2,1,3,0:T(2,128)} copy(f32[1,2,16,6]{2,3,1,0:T(8,128)S(1)} %maximum_divide_fusion) | data formatting | bytes 1536
  (4 shorter events, 0.0 us)
Async XLA Ops:
  0.6 6.9 %copy-start.3 = (s32[8,3]{0,1:T(4,128)S(1)}, s32[8,3]{0,1:T(4,128)}, u32[]{:S(2)}) copy-start(s32[8,3]{0,1:T(4,128)} %param.4) | copy-start | bytes 292
  2.0 19.2 %collective-permute-start = (bf16[3,2,256,384]{3,2,1,0:T(8,128)(2,1)S(1)}, bf16[3,2,256,384]{3,2,1,0:T(8,128)(2,1)S(1)}, u32[]{:S(2)}, u32[]{:S(2)}) collective-permute-start(bf16[3,2,256,384]{3,2,1,0:T(8,128)(2,1)S(1)} %slice.16), channel_id=1, source_target_pairs={{0,30},{2,0},{4,2},{6,4},{8,6},{10,8},{12,10},{14,12},{16,14},{18,... | collective-permute-start | bytes 3538952 | tf_op jit(solution)/shard_map/ppermute | solution.py:16
  7.6 1.9 %copy-start = (bf16[8,2,256,384]{3,2,1,0:T(8,128)(2,1)S(1)}, bf16[8,2,256,384]{3,2,1,0:T(8,128)(2,1)}, u32[]{:S(2)}) copy-start(bf16[8,2,256,384]{3,2,1,0:T(8,128)(2,1)} %refs_7_.1) | copy-start | bytes 9437188
  9.5 11.7 %copy-start.1 = (bf16[8,2,256,384]{3,2,1,0:T(8,128)(2,1)S(1)}, bf16[8,2,256,384]{3,2,1,0:T(8,128)(2,1)}, u32[]{:S(2)}) copy-start(bf16[8,2,256,384]{3,2,1,0:T(8,128)(2,1)} %refs_7_.1) | copy-start | bytes 9437188
  9.5 11.7 %copy-start.2 = (s32[16]{0:T(128)S(1)}, s32[16]{0:T(128)}, u32[]{:S(2)}) copy-start(s32[16]{0:T(128)} %refs_1_.3) | copy-start | bytes 196

commit v9 on v8

--- a/solution.py
+++ b/solution.py
@@ -179,18 +179,16 @@
                 cp.wait()
             return
         width = cells // tiles
-        lane = lax.broadcasted_iota(jnp.int32, (groups, lanes), 1)
+        lane = lax.broadcasted_iota(jnp.int32, (8, lanes), 1)
+        sums = (wr, wi, wc)
         for t in range(tiles):
             base = t * width
-            block = jnp.where(
-                lane < width,
-                pltpu.roll(wr, (lanes - base) % lanes, 1),
-                jnp.where(
-                    lane < 2 * width,
-                    pltpu.roll(wi, (lanes + width - base) % lanes, 1),
-                    jnp.where(lane < 3 * width, pltpu.roll(wc, (lanes + 2 * width - base) % lanes, 1), 0.0),
-                ),
-            )
+            block = jnp.zeros((8, lanes), jnp.float32)
+            for h in range(groups // 8):
+                for f in range(3):
+                    at = (h * 3 + f) * width
+                    moved = pltpu.roll(sums[f][h * 8 : h * 8 + 8], (lanes + at - base) % lanes, 1)
+                    block = jnp.where((lane >= at) & (lane < at + width), moved, block)
             pay[owner_ref[t]] = block
         pay_cp = pltpu.make_async_copy(pay, last_ref, osem.at[5])
         pay_cp.start()
@@ -239,14 +237,14 @@
     else:
         owner, pw_in, ws_in, rx_in, ifg_in, coh_in, pw_base = known
         nknown, tiles = NB, owner.shape[0]
-        out_shape = full + [jax.ShapeDtypeStruct((tiles, groups, lanes), jnp.float32)]
+        out_shape = full + [jax.ShapeDtypeStruct((tiles, 8, lanes), jnp.float32)]
         out_specs = [anyspace, anyspace, anyspace]
         in_specs = [pl.BlockSpec(memory_space=smem), pl.BlockSpec(memory_space=smem)] + [
             anyspace for _ in range(5)
         ] + [hbm for _ in sources]
         extra = [owner, pw_in, ws_in, rx_in, ifg_in, coh_in]
         aliases = {5: 0, 6: 1}
-        scratch += [pltpu.VMEM((tiles, groups, lanes), jnp.float32), pltpu.VMEM((3, groups, lanes), jnp.float32)]
+        scratch += [pltpu.VMEM((tiles, 8, lanes), jnp.float32), pltpu.VMEM((3, groups, lanes), jnp.float32)]
     scratch[1] = pltpu.VMEM((total - nknown, groups, cols), jnp.float32)
     scratch += [pltpu.SemaphoreType.DMA((6,))]
     return pl.pallas_call(
@@ -279,9 +277,14 @@
     )
     width = ifg_a.shape[-1] // owner.shape[0]
     sums = lax.all_to_all(slotted, "date", split_axis=0, concat_axis=0, tiled=True).sum(0)
-    network_mean = (
-        jnp.stack([sums[:, :width], sums[:, width : 2 * width]], 0) / (1.0 + sums[:, 2 * width : 3 * width])
-    )[None]
+    halves = ifg_a.shape[3] // 8
+
+    def field(f):
+        return jnp.concatenate(
+            [sums[:, (h * 3 + f) * width : (h * 3 + f + 1) * width] for h in range(halves)], 0
+        )
+
+    network_mean = (jnp.stack([field(0), field(1)], 0) / (1.0 + field(2)))[None]
     return (interferograms, coherence, network_mean)
 
 

time: 40.1 us -> 39.5 us (0.985)
  blocking collectives: 13.8 us -> 13.1 us
    all_to_all x1, blocking collectives: 13.8 us -> 13.1 us  [on_device(): lax.all_to_all(slotted, 'date', split_axis=0, concat_axis=0, tiled=True)]
    unnamed x11 -> x12, local copies, waits for them, and re-layouts: 2.67 us -> 2.75 us
where the time goes in v9:
time: 39.5 us; the launch traced here: 39.4 us
  blocking collectives  13.1 us (33%)
  Pallas kernels  10.2 us (26%)
  starting transfers between devices  5.5 us (14%)
  waiting for transfers between devices  5.47 us (14%)
  local copies, waits for them, and re-layouts  4.39 us (11%)
  between operations  0.67 us (2%)
    all_to_all x1, blocking collectives, on_device(): lax.all_to_all(slotted, 'date', split_axis=0, concat_axis=0, tiled=True)  13.1 us
    pallas_call x2, Pallas kernels, local_math(): pl.pallas_call(make_kernel(images, first, dates, rows, cols, nknown, tile...  10.2 us
    ppermute x1, starting transfers between devices, shifted(): return lax.ppermute(value, axis, pairs)  5.5 us
    ppermute x1, waiting for transfers between devices, shifted(): return lax.ppermute(value, axis, pairs)  5.47 us
    unnamed x12, local copies, waits for them, and re-layouts  2.75 us
    slice x1, local copies, waits for them, and re-layouts, on_device(): rim = shifted(slc[:NB], 'date', -1)  1.4 us
  transfers between devices with their start and end apart: 1, of which 1 were waited for; matrix products, arithmetic and copies ran while one was open for 0% of the time, Pallas kernels for 16%

profile of v9, /device:TPU:0, one launch (start us, length us, event | category | flops | bytes accessed | tf_op | source)
XLA Modules:
  0.0 39.4 jit_solution(8471313688767412239)
XLA Ops:
  0.6 0.0 copy-start.3
  0.6 1.4 %slice.25 = bf16[3,2,256,384]{3,2,1,0:T(8,128)(2,1)S(1)} slice(bf16[8,2,256,384]{3,2,1,0:T(8,128)(2,1)} %refs_7_.1), slice={[0:3], [0:2], [0:256], [0:384]} | slice | bytes 2359296 | tf_op jit(solution)/shard_map/slice | solution.py:264
  2.0 5.5 %collective-permute-start = (bf16[3,2,256,384]{3,2,1,0:T(8,128)(2,1)S(1)}, bf16[3,2,256,384]{3,2,1,0:T(8,128)(2,1)S(1)}, u32[]{:S(2)}, u32[]{:S(2)}) collective-permute-start(bf16[3,2,256,384]{3,2,1,0:T(8,128)(2,1)S(1)} %slice.25), channel_id=1, source_target_pairs={{0,30},{2,0},{4,2},{6,4},{8,6},{10,8},{12,10},{14,12},{16,14},{18,... | collective-permute-start | bytes 3538952 | tf_op jit(solution)/shard_map/ppermute | solution.py:16
  7.5 0.0 copy-done.3
  7.5 0.1 copy.17.refs_0_
  7.6 0.0 copy-start
  7.6 1.9 %copy-done = bf16[8,2,256,384]{3,2,1,0:T(8,128)(2,1)S(1)} copy-done((bf16[8,2,256,384]{3,2,1,0:T(8,128)(2,1)S(1)}, bf16[8,2,256,384]{3,2,1,0:T(8,128)(2,1)}, u32[]{:S(2)}) %copy-start) | copy-done | bytes 3145752
  9.5 0.0 copy-start.1
  9.5 0.0 copy-start.2
  9.5 6.3 %shard_map.58 = (f32[8,3,2,16,96]{4,3,2,1,0:T(8,128)}, f32[8,3,16,96]{3,2,1,0:T(8,128)}, f32[3,16,128]{2,1,0:T(8,128)S(1)}, f32[8,16,128]{2,1,0:T(8,128)S(1)}, f32[3,3,2,16,384]{4,3,2,1,0:T(8,128)S(1)}) custom-call(s32[8,3]{1,0:T(8,128)S(1)} %copy.17.refs_0_, bf16[8,2,256,384]{3,2,1,0:T(8,128)(2,1)S(1)} %copy-done), custom_call_target="tpu_custom_call" | custom-call | tf_op jit(solution)/shard_map/pallas_call | solution.py:250
  15.8 5.5 %collective-permute-done.refs_8_ = bf16[3,2,256,384]{3,2,1,0:T(8,128)(2,1)S(1)} collective-permute-done((bf16[3,2,256,384]{3,2,1,0:T(8,128)(2,1)S(1)}, bf16[3,2,256,384]{3,2,1,0:T(8,128)(2,1)S(1)}, u32[]{:S(2)}, u32[]{:S(2)}) %collective-permute-start) | collective-permute-done | bytes 1179680 | tf_op jit(solution)/shard_map/ppermute | solution.py:16
  21.3 0.0 copy-done.1
  21.3 0.0 copy-done.2
  21.3 3.9 %shard_map.59 = (f32[8,3,2,16,96]{4,3,2,1,0:T(8,128)}, f32[8,3,16,96]{3,2,1,0:T(8,128)}, f32[16,8,128]{2,1,0:T(8,128)S(1)}) custom-call(s32[3,3]{1,0:T(4,128)S(1)} %slice.24.refs_0_, s32[16]{0:T(128)S(1)} %copy-done.2, f32[8,16,128]{2,1,0:T(8,128)S(1)} %get-tuple-element.11.refs_2_, ...), custom_call_target="tpu_custom_call", output_to_operand_aliasing={{0}: (5, {}), {1}: (6, {})} | custom-call | tf_op jit(solution)/shard_map/pallas_call | solution.py:250
  25.2 13.1 %all_to_all.5 = f32[16,8,128]{2,1,0:T(8,128)S(1)} all-to-all(f32[16,8,128]{2,1,0:T(8,128)S(1)} %get-tuple-element.18), channel_id=1, replica_groups=mesh['date'=16,'strip'=2] {'date'}, dimensions={0} | all-to-all | bytes 131072 | tf_op jit(solution)/shard_map/all_to_all | solution.py:279
  38.3 0.1 fusion
  38.4 0.1 copy.24
  38.5 0.1 copy.25
  38.6 0.1 copy.19
  38.7 0.1 copy.20
  38.7 0.1 maximum_add_fusion
  38.8 0.6 %copy.23 = f32[1,2,16,6]{2,1,3,0:T(2,128)} copy(f32[1,2,16,6]{2,3,1,0:T(8,128)S(1)} %maximum_divide_fusion) | data formatting | bytes 1536
  (4 shorter events, 0.0 us)
Async XLA Ops:
  0.6 6.9 %copy-start.3 = (s32[8,3]{0,1:T(4,128)S(1)}, s32[8,3]{0,1:T(4,128)}, u32[]{:S(2)}) copy-start(s32[8,3]{0,1:T(4,128)} %param.4) | copy-start | bytes 292
  2.0 19.2 %collective-permute-start = (bf16[3,2,256,384]{3,2,1,0:T(8,128)(2,1)S(1)}, bf16[3,2,256,384]{3,2,1,0:T(8,128)(2,1)S(1)}, u32[]{:S(2)}, u32[]{:S(2)}) collective-permute-start(bf16[3,2,256,384]{3,2,1,0:T(8,128)(2,1)S(1)} %slice.25), channel_id=1, source_target_pairs={{0,30},{2,0},{4,2},{6,4},{8,6},{10,8},{12,10},{14,12},{16,14},{18,... | collective-permute-start | bytes 3538952 | tf_op jit(solution)/shard_map/ppermute | solution.py:16
  7.6 1.9 %copy-start = (bf16[8,2,256,384]{3,2,1,0:T(8,128)(2,1)S(1)}, bf16[8,2,256,384]{3,2,1,0:T(8,128)(2,1)}, u32[]{:S(2)}) copy-start(bf16[8,2,256,384]{3,2,1,0:T(8,128)(2,1)} %refs_7_.1) | copy-start | bytes 9437188
  9.5 11.7 %copy-start.1 = (bf16[8,2,256,384]{3,2,1,0:T(8,128)(2,1)S(1)}, bf16[8,2,256,384]{3,2,1,0:T(8,128)(2,1)}, u32[]{:S(2)}) copy-start(bf16[8,2,256,384]{3,2,1,0:T(8,128)(2,1)} %refs_7_.1) | copy-start | bytes 9437188
  9.5 11.7 %copy-start.2 = (s32[16]{0:T(128)S(1)}, s32[16]{0:T(128)}, u32[]{:S(2)}) copy-start(s32[16]{0:T(128)} %refs_1_.3) | copy-start | bytes 196

commit v10 on v9

--- a/solution.py
+++ b/solution.py
@@ -8,6 +8,7 @@
 NB = 3
 LR = 16
 LA = 4
+SLOT = 4
 
 
 def shifted(value, axis, steps):
@@ -179,15 +180,15 @@
                 cp.wait()
             return
         width = cells // tiles
-        lane = lax.broadcasted_iota(jnp.int32, (8, lanes), 1)
+        lane = lax.broadcasted_iota(jnp.int32, (SLOT, lanes), 1)
         sums = (wr, wi, wc)
         for t in range(tiles):
             base = t * width
-            block = jnp.zeros((8, lanes), jnp.float32)
-            for h in range(groups // 8):
+            block = jnp.zeros((SLOT, lanes), jnp.float32)
+            for h in range(groups // SLOT):
                 for f in range(3):
                     at = (h * 3 + f) * width
-                    moved = pltpu.roll(sums[f][h * 8 : h * 8 + 8], (lanes + at - base) % lanes, 1)
+                    moved = pltpu.roll(sums[f][h * SLOT : h * SLOT + SLOT], (lanes + at - base) % lanes, 1)
                     block = jnp.where((lane >= at) & (lane < at + width), moved, block)
             pay[owner_ref[t]] = block
         pay_cp = pltpu.make_async_copy(pay, last_ref, osem.at[5])
@@ -237,14 +238,14 @@
     else:
         owner, pw_in, ws_in, rx_in, ifg_in, coh_in, pw_base = known
         nknown, tiles = NB, owner.shape[0]
-        out_shape = full + [jax.ShapeDtypeStruct((tiles, 8, lanes), jnp.float32)]
+        out_shape = full + [jax.ShapeDtypeStruct((tiles, SLOT, lanes), jnp.float32)]
         out_specs = [anyspace, anyspace, anyspace]
         in_specs = [pl.BlockSpec(memory_space=smem), pl.BlockSpec(memory_space=smem)] + [
             anyspace for _ in range(5)
         ] + [hbm for _ in sources]
         extra = [owner, pw_in, ws_in, rx_in, ifg_in, coh_in]
         aliases = {5: 0, 6: 1}
-        scratch += [pltpu.VMEM((tiles, 8, lanes), jnp.float32), pltpu.VMEM((3, groups, lanes), jnp.float32)]
+        scratch += [pltpu.VMEM((tiles, SLOT, lanes), jnp.float32), pltpu.VMEM((3, groups, lanes), jnp.float32)]
     scratch[1] = pltpu.VMEM((total - nknown, groups, cols), jnp.float32)
     scratch += [pltpu.SemaphoreType.DMA((6,))]
     return pl.pallas_call(
@@ -277,7 +278,7 @@
     )
     width = ifg_a.shape[-1] // owner.shape[0]
     sums = lax.all_to_all(slotted, "date", split_axis=0, concat_axis=0, tiled=True).sum(0)
-    halves = ifg_a.shape[3] // 8
+    halves = ifg_a.shape[3] // SLOT
 
     def field(f):
         return jnp.concatenate(

time: 39.5 us -> 39 us (0.987)
  blocking collectives: 13.1 us -> 12 us
    all_to_all x1, blocking collectives: 13.1 us -> 12 us  [on_device(): lax.all_to_all(slotted, 'date', split_axis=0, concat_axis=0, tiled=True)]
    unnamed x12 -> x14, local copies, waits for them, and re-layouts: 2.75 us -> 2.96 us
where the time goes in v10:
time: 39 us; the launch traced here: 38.7 us
  blocking collectives  12 us (31%)
  Pallas kernels  10.3 us (26%)
  waiting for transfers between devices  5.62 us (14%)
  starting transfers between devices  5.5 us (14%)
  local copies, waits for them, and re-layouts  4.6 us (12%)
  between operations  0.68 us (2%)
    all_to_all x1, blocking collectives, on_device(): lax.all_to_all(slotted, 'date', split_axis=0, concat_axis=0, tiled=True)  12 us
    pallas_call x2, Pallas kernels, local_math(): pl.pallas_call(make_kernel(images, first, dates, rows, cols, nknown, tile...  10.3 us
    ppermute x1, waiting for transfers between devices, shifted(): return lax.ppermute(value, axis, pairs)  5.62 us
    ppermute x1, starting transfers between devices, shifted(): return lax.ppermute(value, axis, pairs)  5.5 us
    unnamed x14, local copies, waits for them, and re-layouts  2.96 us
    slice x1, local copies, waits for them, and re-layouts, on_device(): rim = shifted(slc[:NB], 'date', -1)  1.4 us
  transfers between devices with their start and end apart: 1, of which 1 were waited for; matrix products, arithmetic and copies ran while one was open for 0% of the time, Pallas kernels for 16%

profile of v10, /device:TPU:0, one launch (start us, length us, event | category | flops | bytes accessed | tf_op | source)
XLA Modules:
  0.0 38.7 jit_solution(4553634243071279311)
XLA Ops:
  0.6 0.0 copy-start.3
  0.6 1.4 %slice.43 = bf16[3,2,256,384]{3,2,1,0:T(8,128)(2,1)S(1)} slice(bf16[8,2,256,384]{3,2,1,0:T(8,128)(2,1)} %refs_7_.1), slice={[0:3], [0:2], [0:256], [0:384]} | slice | bytes 2359296 | tf_op jit(solution)/shard_map/slice | solution.py:265
  2.0 5.5 %collective-permute-start = (bf16[3,2,256,384]{3,2,1,0:T(8,128)(2,1)S(1)}, bf16[3,2,256,384]{3,2,1,0:T(8,128)(2,1)S(1)}, u32[]{:S(2)}, u32[]{:S(2)}) collective-permute-start(bf16[3,2,256,384]{3,2,1,0:T(8,128)(2,1)S(1)} %slice.43), channel_id=1, source_target_pairs={{0,30},{2,0},{4,2},{6,4},{8,6},{10,8},{12,10},{14,12},{16,14},{18,... | collective-permute-start | bytes 3538952 | tf_op jit(solution)/shard_map/ppermute | solution.py:17
  7.5 0.0 copy-done.3
  7.5 0.1 copy.17.refs_0_
  7.6 0.0 copy-start
  7.6 1.9 %copy-done = bf16[8,2,256,384]{3,2,1,0:T(8,128)(2,1)S(1)} copy-done((bf16[8,2,256,384]{3,2,1,0:T(8,128)(2,1)S(1)}, bf16[8,2,256,384]{3,2,1,0:T(8,128)(2,1)}, u32[]{:S(2)}) %copy-start) | copy-done | bytes 3145752
  9.5 0.0 copy-start.1
  9.5 0.0 copy-start.2
  9.5 6.1 %shard_map.58 = (f32[8,3,2,16,96]{4,3,2,1,0:T(8,128)}, f32[8,3,16,96]{3,2,1,0:T(8,128)}, f32[3,16,128]{2,1,0:T(8,128)S(1)}, f32[8,16,128]{2,1,0:T(8,128)S(1)}, f32[3,3,2,16,384]{4,3,2,1,0:T(8,128)S(1)}) custom-call(s32[8,3]{1,0:T(8,128)S(1)} %copy.17.refs_0_, bf16[8,2,256,384]{3,2,1,0:T(8,128)(2,1)S(1)} %copy-done), custom_call_target="tpu_custom_call" | custom-call | tf_op jit(solution)/shard_map/pallas_call | solution.py:251
  15.6 5.6 %collective-permute-done.refs_8_ = bf16[3,2,256,384]{3,2,1,0:T(8,128)(2,1)S(1)} collective-permute-done((bf16[3,2,256,384]{3,2,1,0:T(8,128)(2,1)S(1)}, bf16[3,2,256,384]{3,2,1,0:T(8,128)(2,1)S(1)}, u32[]{:S(2)}, u32[]{:S(2)}) %collective-permute-start) | collective-permute-done | bytes 1179680 | tf_op jit(solution)/shard_map/ppermute | solution.py:17
  21.3 0.0 copy-done.1
  21.3 0.0 copy-done.2
  21.3 4.2 %shard_map.59 = (f32[8,3,2,16,96]{4,3,2,1,0:T(8,128)}, f32[8,3,16,96]{3,2,1,0:T(8,128)}, f32[16,4,128]{2,1,0:T(4,128)S(1)}) custom-call(s32[3,3]{1,0:T(4,128)S(1)} %slice.42.refs_0_, s32[16]{0:T(128)S(1)} %copy-done.2, f32[8,16,128]{2,1,0:T(8,128)S(1)} %get-tuple-element.11.refs_2_, ...), custom_call_target="tpu_custom_call", output_to_operand_aliasing={{0}: (5, {}), {1}: (6, {})} | custom-call | tf_op jit(solution)/shard_map/pallas_call | solution.py:251
  25.4 12.0 %all_to_all.5 = f32[16,4,128]{2,1,0:T(4,128)S(1)} all-to-all(f32[16,4,128]{2,1,0:T(4,128)S(1)} %get-tuple-element.18), channel_id=1, replica_groups=mesh['date'=16,'strip'=2] {'date'}, dimensions={0} | all-to-all | bytes 65536 | tf_op jit(solution)/shard_map/all_to_all | solution.py:280
  37.4 0.1 fusion
  37.5 0.1 copy.26
  37.6 0.1 copy.28
  37.7 0.1 copy.27
  37.8 0.1 copy.29
  37.9 0.1 copy.19
  38.0 0.1 copy.20
  38.0 0.1 maximum_add_fusion
  38.1 0.6 %copy.25 = f32[1,2,16,6]{2,1,3,0:T(2,128)} copy(f32[1,2,16,6]{2,3,1,0:T(8,128)S(1)} %maximum_divide_fusion) | data formatting | bytes 1536
  (4 shorter events, 0.1 us)
Async XLA Ops:
  0.6 6.9 %copy-start.3 = (s32[8,3]{0,1:T(4,128)S(1)}, s32[8,3]{0,1:T(4,128)}, u32[]{:S(2)}) copy-start(s32[8,3]{0,1:T(4,128)} %param.4) | copy-start | bytes 292
  2.0 19.2 %collective-permute-start = (bf16[3,2,256,384]{3,2,1,0:T(8,128)(2,1)S(1)}, bf16[3,2,256,384]{3,2,1,0:T(8,128)(2,1)S(1)}, u32[]{:S(2)}, u32[]{:S(2)}) collective-permute-start(bf16[3,2,256,384]{3,2,1,0:T(8,128)(2,1)S(1)} %slice.43), channel_id=1, source_target_pairs={{0,30},{2,0},{4,2},{6,4},{8,6},{10,8},{12,10},{14,12},{16,14},{18,... | collective-permute-start | bytes 3538952 | tf_op jit(solution)/shard_map/ppermute | solution.py:17
  7.6 1.9 %copy-start = (bf16[8,2,256,384]{3,2,1,0:T(8,128)(2,1)S(1)}, bf16[8,2,256,384]{3,2,1,0:T(8,128)(2,1)}, u32[]{:S(2)}) copy-start(bf16[8,2,256,384]{3,2,1,0:T(8,128)(2,1)} %refs_7_.1) | copy-start | bytes 9437188
  9.5 11.7 %copy-start.1 = (bf16[8,2,256,384]{3,2,1,0:T(8,128)(2,1)S(1)}, bf16[8,2,256,384]{3,2,1,0:T(8,128)(2,1)}, u32[]{:S(2)}) copy-start(bf16[8,2,256,384]{3,2,1,0:T(8,128)(2,1)} %refs_7_.1) | copy-start | bytes 9437188
  9.5 11.7 %copy-start.2 = (s32[16]{0:T(128)S(1)}, s32[16]{0:T(128)}, u32[]{:S(2)}) copy-start(s32[16]{0:T(128)} %refs_1_.3) | copy-start | bytes 196

commit v11 on v10

--- a/solution.py
+++ b/solution.py
@@ -237,7 +237,7 @@
         aliases = {}
     else:
         owner, pw_in, ws_in, rx_in, ifg_in, coh_in, pw_base = known
-        nknown, tiles = NB, owner.shape[0]
+        nknown, tiles = pw_in.shape[0], owner.shape[0]
         out_shape = full + [jax.ShapeDtypeStruct((tiles, SLOT, lanes), jnp.float32)]
         out_specs = [anyspace, anyspace, anyspace]
         in_specs = [pl.BlockSpec(memory_space=smem), pl.BlockSpec(memory_space=smem)] + [
@@ -259,22 +259,110 @@
     )(offsets, *extra, *sources)
 
 
+def rim_step(offsets, racc_in, slc, rim, step, inner):
+    _, _, rows, cols = slc.shape
+    groups = rows // LR
+    ctiles = cols // 128
+    lanes = 128
+    own = slc.shape[0] - inner
+
+    def kernel(off_ref, slc_ref, rim_ref, racc_in_ref, racc_ref, pw_ref, xf, pacc):
+        for t in range(own):
+            xf[t] = slc_ref[inner + t].astype(jnp.float32)
+        xf[own] = rim_ref[0].astype(jnp.float32)
+        line = lax.broadcasted_iota(jnp.int32, (cols, lanes), 0)
+        cell = lax.broadcasted_iota(jnp.int32, (cols, lanes), 1)
+        pool = jnp.where(line // LA == cell, 1.0 / (LR * LA), 0.0).astype(jnp.bfloat16)
+        sub = lax.broadcasted_iota(jnp.int32, (8, 128), 0)
+        masks = {k: (sub % (2 * k)) < k for k in (4, 2, 1)}
+
+        def combine(x, y, k):
+            m = masks[k]
+            return jnp.where(m, x + pltpu.roll(x, 8 - k, 0), y + pltpu.roll(y, k, 0))
+
+        def fold(parts):
+            q = [combine(parts[g], parts[g + 4], 4) for g in range(4)]
+            r = [combine(q[0], q[2], 2), combine(q[1], q[3], 2)]
+            return combine(r[0], r[1], 1)
+
+        def rows_of(j, comp, g, ct):
+            return xf[j, comp, pl.ds(g * LR, LR), pl.ds(ct * 128, 128)]
+
+        def half(v):
+            return v[:8] + v[8:]
+
+        for ct in range(ctiles):
+            for blk in range(groups // 8):
+                parts = []
+                for g in range(blk * 8, blk * 8 + 8):
+                    x0 = rows_of(own, 0, g, ct)
+                    x1 = rows_of(own, 1, g, ct)
+                    parts.append(half(x0 * x0 + x1 * x1))
+                pacc[pl.ds(blk * 8, 8), pl.ds(ct * 128, 128)] = fold(parts)
+        pw_ref[0] = split_pool(pacc[...], pool)
+
+        def pairs(i, c):
+            for k in range(NB):
+
+                @pl.when(i + off_ref[i, k] == own + step)
+                def _():
+                    for ct in range(ctiles):
+                        for blk in range(groups // 8):
+                            re = []
+                            im = []
+                            for g in range(blk * 8, blk * 8 + 8):
+                                a0 = rows_of(i, 0, g, ct)
+                                a1 = rows_of(i, 1, g, ct)
+                                b0 = rows_of(own, 0, g, ct)
+                                b1 = rows_of(own, 1, g, ct)
+                                re.append(half(a0 * b0 + a1 * b1))
+                                im.append(half(a1 * b0 - a0 * b1))
+                            racc_ref[i, k, 0, pl.ds(blk * 8, 8), pl.ds(ct * 128, 128)] = fold(re)
+                            racc_ref[i, k, 1, pl.ds(blk * 8, 8), pl.ds(ct * 128, 128)] = fold(im)
+
+            return c
+
+        lax.fori_loop(0, own, pairs, 0)
+
+    vmem = pltpu.VMEM
+    return pl.pallas_call(
+        kernel,
+        out_shape=(
+            jax.ShapeDtypeStruct(racc_in.shape, jnp.float32),
+            jax.ShapeDtypeStruct((1, groups, lanes), jnp.float32),
+        ),
+        in_specs=[pl.BlockSpec(memory_space=pltpu.SMEM)] + [pl.BlockSpec(memory_space=vmem) for _ in range(3)],
+        out_specs=(pl.BlockSpec(memory_space=vmem), pl.BlockSpec(memory_space=vmem)),
+        scratch_shapes=[
+            pltpu.VMEM((own + 1, 2, rows, cols), jnp.float32),
+            pltpu.VMEM((groups, cols), jnp.float32),
+        ],
+        input_output_aliases={3: 0},
+        compiler_params=pltpu.CompilerParams(vmem_limit_bytes=48 * 1024 * 1024),
+    )(offsets, slc, rim, racc_in)
+
+
 def on_device(slc, offsets, owner):
     count = slc.shape[0]
     inner = count - NB
-    rim = shifted(slc[:NB], "date", -1)
+    rims = [shifted(slc[t : t + 1], "date", -1) for t in range(NB)]
     ifg_a, coh_a, ws_a, pw_a, rx_a = local_math(
         offsets, [slc], [(0, t) for t in range(count)], 0, inner, count, 0
     )
+    racc = rx_a
+    powers = [pw_a[inner:]]
+    for step in range(NB - 1):
+        racc, pw_step = rim_step(offsets[inner:], racc, slc, rims[step], step, inner)
+        powers.append(pw_step)
     interferograms, coherence, slotted = local_math(
         offsets[inner:],
-        [slc, rim],
-        [(0, inner + t) for t in range(NB)] + [(1, t) for t in range(NB)],
+        [slc] + rims,
+        [(0, inner + t) for t in range(NB)] + [(1 + t, 0) for t in range(NB)],
         0,
         NB,
         count,
         inner,
-        known=(owner, pw_a, ws_a, rx_a, ifg_a, coh_a, inner),
+        known=(owner, jnp.concatenate(powers, 0), ws_a, racc, ifg_a, coh_a, 0),
     )
     width = ifg_a.shape[-1] // owner.shape[0]
     sums = lax.all_to_all(slotted, "date", split_axis=0, concat_axis=0, tiled=True).sum(0)

time: 39 us -> 38.2 us (0.979)
  waiting for transfers between devices: 5.62 us -> 1.23 us
  Pallas kernels: 10.3 us -> 12.2 us
  starting transfers between devices: 5.5 us -> 6.24 us
  local copies, waits for them, and re-layouts: 4.6 us -> 5.23 us
    ppermute x1 -> x3, waiting for transfers between devices: 5.62 us -> 1.23 us  [shifted(): return lax.ppermute(value, axis, pairs)]
    pallas_call x0 -> x2, Pallas kernels: none -> 2.61 us  [rim_step(): pl.pallas_call(kernel, out_shape=(jax.ShapeDtypeStruct(racc_in.shape, jnp...]
    ppermute x1 -> x3, starting transfers between devices: 5.5 us -> 6.24 us  [shifted(): return lax.ppermute(value, axis, pairs)]
    unnamed x14 -> x12, local copies, waits for them, and re-layouts: 2.96 us -> 3.63 us
    pallas_call x2, Pallas kernels: 10.3 us -> 9.61 us  [local_math(): pl.pallas_call(make_kernel(images, first, dates, rows, cols, nknown, tile...]
    slice x1 -> x2, local copies, waits for them, and re-layouts: 1.4 us -> 1.36 us  [the longest x1 1.36 us: on_device(): rims = [shifted(slc[t:t + 1], 'date', -1) for t in range(NB)]]
  transfers between devices with their start and end apart: 1 -> 3, of which waited for: 1 -> 1; matrix products, arithmetic and copies ran while one was open for 0% -> 2% of each run, Pallas kernels for 16% -> 24%
where the time goes in v11:
time: 38.2 us; the launch traced here: 37.9 us
  Pallas kernels  12.2 us (32%)
  blocking collectives  12.1 us (32%)
  starting transfers between devices  6.24 us (16%)
  local copies, waits for them, and re-layouts  5.23 us (14%)
  waiting for transfers between devices  1.23 us (3%)
  between operations  0.73 us (2%)
    all_to_all x1, blocking collectives, on_device(): lax.all_to_all(slotted, 'date', split_axis=0, concat_axis=0, tiled=True)  12.1 us
    pallas_call x2, Pallas kernels, local_math(): pl.pallas_call(make_kernel(images, first, dates, rows, cols, nknown, tile...  9.61 us
    ppermute x3, starting transfers between devices, shifted(): return lax.ppermute(value, axis, pairs)  6.24 us
    unnamed x12, local copies, waits for them, and re-layouts  3.63 us
    pallas_call x2, Pallas kernels, rim_step(): pl.pallas_call(kernel, out_shape=(jax.ShapeDtypeStruct(racc_in.shape, jnp...  2.61 us
    slice x1, local copies, waits for them, and re-layouts, on_device(): rims = [shifted(slc[t:t + 1], 'date', -1) for t in range(NB)]  1.36 us
    ppermute x3, waiting for transfers between devices, shifted(): return lax.ppermute(value, axis, pairs)  1.23 us
  transfers between devices with their start and end apart: 3, of which 1 were waited for; matrix products, arithmetic and copies ran while one was open for 2% of the time, Pallas kernels for 24%

profile of v11, /device:TPU:0, one launch (start us, length us, event | category | flops | bytes accessed | tf_op | source)
XLA Modules:
  0.0 37.9 jit_solution(14800815449200231238)
XLA Ops:
  0.6 1.4 %fusion = (bf16[1,2,256,384]{3,2,1,0:T(8,128)(2,1)S(1)}, bf16[1,2,256,384]{3,2,1,0:T(8,128)(2,1)S(1)}, bf16[1,2,256,384]{3,2,1,0:T(8,128)(2,1)S(1)}) fusion(bf16[8,2,256,384]{3,2,1,0:T(8,128)(2,1)} %refs_7_.1), kind=kLoop, calls=%fused_computation.5 | loop fusion | bytes 2359296 | tf_op jit(solution)/shard_map/slice | solution.py:348
  2.0 5.5 %collective-permute-start = (bf16[1,2,256,384]{3,2,1,0:T(8,128)(2,1)S(1)}, bf16[1,2,256,384]{3,2,1,0:T(8,128)(2,1)S(1)}, u32[]{:S(2)}, u32[]{:S(2)}) collective-permute-start(bf16[1,2,256,384]{3,2,1,0:T(8,128)(2,1)S(1)} %get-tuple-element.38), channel_id=1, source_target_pairs={{0,30},{2,0},{4,2},{6,4},{8,6},{10,8},{12,10},{14,12},{16,14},{18,... | collective-permute-start | bytes 1179656 | tf_op jit(solution)/shard_map/ppermute | solution.py:17
  7.5 0.7 %collective-permute-start.1 = (bf16[1,2,256,384]{3,2,1,0:T(8,128)(2,1)S(1)}, bf16[1,2,256,384]{3,2,1,0:T(8,128)(2,1)S(1)}, u32[]{:S(2)}, u32[]{:S(2)}) collective-permute-start(bf16[1,2,256,384]{3,2,1,0:T(8,128)(2,1)S(1)} %get-tuple-element.37), channel_id=1, source_target_pairs={{0,30},{2,0},{4,2},{6,4},{8,6},{10,8},{12,10},{14,12},{16,14},{18,... | collective-permute-start | bytes 1179656 | tf_op jit(solution)/shard_map/ppermute | solution.py:17
  8.2 0.1 collective-permute-start.2
  8.2 0.8 %copy.19.refs_0_ = s32[8,3]{1,0:T(8,128)S(1)} copy(s32[8,3]{0,1:T(4,128)} %param.4) | data formatting | bytes 192 | tf_op args[1]
  9.0 0.0 copy-start
  9.0 1.9 %copy-done = bf16[8,2,256,384]{3,2,1,0:T(8,128)(2,1)S(1)} copy-done((bf16[8,2,256,384]{3,2,1,0:T(8,128)(2,1)S(1)}, bf16[8,2,256,384]{3,2,1,0:T(8,128)(2,1)}, u32[]{:S(2)}) %copy-start) | copy-done | bytes 3145752
  10.9 0.0 copy-start.1
  10.9 6.4 %shard_map.58 = (f32[8,3,2,16,96]{4,3,2,1,0:T(8,128)}, f32[8,3,16,96]{3,2,1,0:T(8,128)}, f32[3,16,128]{2,1,0:T(8,128)S(1)}, f32[8,16,128]{2,1,0:T(8,128)S(1)}, f32[3,3,2,16,384]{4,3,2,1,0:T(8,128)S(1)}) custom-call(s32[8,3]{1,0:T(8,128)S(1)} %copy.19.refs_0_, bf16[8,2,256,384]{3,2,1,0:T(8,128)(2,1)S(1)} %copy-done), custom_call_target="tpu_custom_call" | custom-call | tf_op jit(solution)/shard_map/pallas_call | solution.py:251
  17.3 0.0 collective-permute-done.rim_ref.refs_8_
  17.3 0.0 copy-done.1
  17.3 0.0 copy-start.2
  17.3 1.2 %shard_map.59 = (f32[3,3,2,16,384]{4,3,2,1,0:T(8,128)S(1)}, f32[1,16,128]{2,1,0:T(8,128)S(1)}) custom-call(s32[3,3]{1,0:T(4,128)S(1)} %slice.53.off_ref.refs_0_, bf16[8,2,256,384]{3,2,1,0:T(8,128)(2,1)S(1)} %copy-done.1, bf16[1,2,256,384]{3,2,1,0:T(8,128)(2,1)S(1)} %collective-permute-done.rim_ref.refs_8_, ...), custom_call_target="tpu_custom_call", output_to_operand_aliasing={{0}: (3, {})} | custom-call | tf_op jit(solution)/shard_map/pallas_call | solution.py:328
  18.6 0.0 collective-permute-done.1.rim_ref.refs_9_
  18.6 1.4 %shard_map.60 = (f32[3,3,2,16,384]{4,3,2,1,0:T(8,128)S(1)}, f32[1,16,128]{2,1,0:T(8,128)S(1)}) custom-call(s32[3,3]{1,0:T(4,128)S(1)} %slice.53.off_ref.refs_0_, bf16[8,2,256,384]{3,2,1,0:T(8,128)(2,1)S(1)} %copy-done.1, bf16[1,2,256,384]{3,2,1,0:T(8,128)(2,1)S(1)} %collective-permute-done.1.rim_ref.refs_9_, ...), custom_call_target="tpu_custom_call", output_to_operand_aliasing={{0}: (3, {})} | custom-call | tf_op jit(solution)/shard_map/pallas_call | solution.py:328
  20.0 1.2 %collective-permute-done.2.refs_10_ = bf16[1,2,256,384]{3,2,1,0:T(8,128)(2,1)S(1)} collective-permute-done((bf16[1,2,256,384]{3,2,1,0:T(8,128)(2,1)S(1)}, bf16[1,2,256,384]{3,2,1,0:T(8,128)(2,1)S(1)}, u32[]{:S(2)}, u32[]{:S(2)}) %collective-permute-start.2) | collective-permute-done | bytes 393248 | tf_op jit(solution)/shard_map/ppermute | solution.py:17
  21.2 0.0 copy-done.2
  21.2 3.2 %shard_map.61 = (f32[8,3,2,16,96]{4,3,2,1,0:T(8,128)}, f32[8,3,16,96]{3,2,1,0:T(8,128)}, f32[16,4,128]{2,1,0:T(4,128)S(1)}) custom-call(s32[3,3]{1,0:T(4,128)S(1)} %slice.53.off_ref.refs_0_, s32[16]{0:T(128)S(1)} %copy-done.2, f32[5,16,128]{2,1,0:T(8,128)S(1)} %pad_maximum_fusion.refs_2_, ...), custom_call_target="tpu_custom_call", output_to_operand_aliasing={{0}: (5, {}), {1}: (6, {})} | custom-call | tf_op jit(solution)/shard_map/pallas_call | solution.py:251
  24.4 12.1 %all_to_all.5 = f32[16,4,128]{2,1,0:T(4,128)S(1)} all-to-all(f32[16,4,128]{2,1,0:T(4,128)S(1)} %get-tuple-element.26), channel_id=1, replica_groups=mesh['date'=16,'strip'=2] {'date'}, dimensions={0} | all-to-all | bytes 65536 | tf_op jit(solution)/shard_map/all_to_all | solution.py:368
  36.6 0.1 fusion.1
  36.7 0.1 copy.28
  36.7 0.1 copy.30
  36.8 0.1 copy.29
  36.9 0.1 copy.31
  37.0 0.1 copy.21
  37.1 0.1 copy.22
  37.2 0.1 maximum_add_fusion
  37.3 0.6 %copy.27 = f32[1,2,16,6]{2,1,3,0:T(2,128)} copy(f32[1,2,16,6]{2,3,1,0:T(8,128)S(1)} %maximum_divide_fusion) | data formatting | bytes 1536
  (6 shorter events, 0.1 us)
Async XLA Ops:
  2.0 15.3 %collective-permute-start = (bf16[1,2,256,384]{3,2,1,0:T(8,128)(2,1)S(1)}, bf16[1,2,256,384]{3,2,1,0:T(8,128)(2,1)S(1)}, u32[]{:S(2)}, u32[]{:S(2)}) collective-permute-start(bf16[1,2,256,384]{3,2,1,0:T(8,128)(2,1)S(1)} %get-tuple-element.38), channel_id=1, source_target_pairs={{0,30},{2,0},{4,2},{6,4},{8,6},{10,8},{12,10},{14,12},{16,14},{18,... | collective-permute-start | bytes 1179656 | tf_op jit(solution)/shard_map/ppermute | solution.py:17
  7.5 11.1 %collective-permute-start.1 = (bf16[1,2,256,384]{3,2,1,0:T(8,128)(2,1)S(1)}, bf16[1,2,256,384]{3,2,1,0:T(8,128)(2,1)S(1)}, u32[]{:S(2)}, u32[]{:S(2)}) collective-permute-start(bf16[1,2,256,384]{3,2,1,0:T(8,128)(2,1)S(1)} %get-tuple-element.37), channel_id=1, source_target_pairs={{0,30},{2,0},{4,2},{6,4},{8,6},{10,8},{12,10},{14,12},{16,14},{18,... | collective-permute-start | bytes 1179656 | tf_op jit(solution)/shard_map/ppermute | solution.py:17
  8.2 13.0 %collective-permute-start.2 = (bf16[1,2,256,384]{3,2,1,0:T(8,128)(2,1)S(1)}, bf16[1,2,256,384]{3,2,1,0:T(8,128)(2,1)S(1)}, u32[]{:S(2)}, u32[]{:S(2)}) collective-permute-start(bf16[1,2,256,384]{3,2,1,0:T(8,128)(2,1)S(1)} %get-tuple-element.36), channel_id=1, source_target_pairs={{0,30},{2,0},{4,2},{6,4},{8,6},{10,8},{12,10},{14,12},{16,14},{18,... | collective-permute-start | bytes 1179656 | tf_op jit(solution)/shard_map/ppermute | solution.py:17
  9.0 1.9 %copy-start = (bf16[8,2,256,384]{3,2,1,0:T(8,128)(2,1)S(1)}, bf16[8,2,256,384]{3,2,1,0:T(8,128)(2,1)}, u32[]{:S(2)}) copy-start(bf16[8,2,256,384]{3,2,1,0:T(8,128)(2,1)} %refs_7_.1) | copy-start | bytes 9437188
  10.9 6.4 %copy-start.1 = (bf16[8,2,256,384]{3,2,1,0:T(8,128)(2,1)S(1)}, bf16[8,2,256,384]{3,2,1,0:T(8,128)(2,1)}, u32[]{:S(2)}) copy-start(bf16[8,2,256,384]{3,2,1,0:T(8,128)(2,1)} %refs_7_.1) | copy-start | bytes 9437188
  17.3 3.9 %copy-start.2 = (s32[16]{0:T(128)S(1)}, s32[16]{0:T(128)}, u32[]{:S(2)}) copy-start(s32[16]{0:T(128)} %refs_1_.3) | copy-start | bytes 196

commit v12 on v11

--- a/solution.py
+++ b/solution.py
@@ -56,7 +56,8 @@
             ws_cp.start()
             rx_cp.start()
         for t, (src, lead) in enumerate(images):
-            xf[t] = srcs[src][lead].astype(jnp.float32)
+            if t >= known or (t < NB and t + NB >= known):
+                xf[t] = srcs[src][lead].astype(jnp.float32)
 
         line = lax.broadcasted_iota(jnp.int32, (cols, lanes), 0)
         cell = lax.broadcasted_iota(jnp.int32, (cols, lanes), 1)

time: 38.2 us -> 38 us (level)
  no operation moved by 1% of the time
where the time goes in v12:
time: 38 us; the launch traced here: 37.7 us
  blocking collectives  12.3 us (32%)
  Pallas kernels  12 us (32%)
  starting transfers between devices  6.24 us (16%)
  local copies, waits for them, and re-layouts  5.23 us (14%)
  waiting for transfers between devices  1.08 us (3%)
  between operations  0.73 us (2%)
    all_to_all x1, blocking collectives, on_device(): lax.all_to_all(slotted, 'date', split_axis=0, concat_axis=0, tiled=True)  12.3 us
    pallas_call x2, Pallas kernels, local_math(): pl.pallas_call(make_kernel(images, first, dates, rows, cols, nknown, tile...  9.41 us
    ppermute x3, starting transfers between devices, shifted(): return lax.ppermute(value, axis, pairs)  6.24 us
    unnamed x12, local copies, waits for them, and re-layouts  3.63 us
    pallas_call x2, Pallas kernels, rim_step(): pl.pallas_call(kernel, out_shape=(jax.ShapeDtypeStruct(racc_in.shape, jnp...  2.61 us
    slice x1, local copies, waits for them, and re-layouts, on_device(): rims = [shifted(slc[t:t + 1], 'date', -1) for t in range(NB)]  1.36 us
    ppermute x3, waiting for transfers between devices, shifted(): return lax.ppermute(value, axis, pairs)  1.08 us
  transfers between devices with their start and end apart: 3, of which 1 were waited for; matrix products, arithmetic and copies ran while one was open for 2% of the time, Pallas kernels for 24%

profile of v12, /device:TPU:0, one launch (start us, length us, event | category | flops | bytes accessed | tf_op | source)
XLA Modules:
  0.0 37.7 jit_solution(4618772883637103713)
XLA Ops:
  0.6 1.4 %fusion = (bf16[1,2,256,384]{3,2,1,0:T(8,128)(2,1)S(1)}, bf16[1,2,256,384]{3,2,1,0:T(8,128)(2,1)S(1)}, bf16[1,2,256,384]{3,2,1,0:T(8,128)(2,1)S(1)}) fusion(bf16[8,2,256,384]{3,2,1,0:T(8,128)(2,1)} %refs_7_.1), kind=kLoop, calls=%fused_computation.5 | loop fusion | bytes 2359296 | tf_op jit(solution)/shard_map/slice | solution.py:349
  2.0 5.5 %collective-permute-start = (bf16[1,2,256,384]{3,2,1,0:T(8,128)(2,1)S(1)}, bf16[1,2,256,384]{3,2,1,0:T(8,128)(2,1)S(1)}, u32[]{:S(2)}, u32[]{:S(2)}) collective-permute-start(bf16[1,2,256,384]{3,2,1,0:T(8,128)(2,1)S(1)} %get-tuple-element.38), channel_id=1, source_target_pairs={{0,30},{2,0},{4,2},{6,4},{8,6},{10,8},{12,10},{14,12},{16,14},{18,... | collective-permute-start | bytes 1179656 | tf_op jit(solution)/shard_map/ppermute | solution.py:17
  7.5 0.7 %collective-permute-start.1 = (bf16[1,2,256,384]{3,2,1,0:T(8,128)(2,1)S(1)}, bf16[1,2,256,384]{3,2,1,0:T(8,128)(2,1)S(1)}, u32[]{:S(2)}, u32[]{:S(2)}) collective-permute-start(bf16[1,2,256,384]{3,2,1,0:T(8,128)(2,1)S(1)} %get-tuple-element.37), channel_id=1, source_target_pairs={{0,30},{2,0},{4,2},{6,4},{8,6},{10,8},{12,10},{14,12},{16,14},{18,... | collective-permute-start | bytes 1179656 | tf_op jit(solution)/shard_map/ppermute | solution.py:17
  8.2 0.1 collective-permute-start.2
  8.2 0.8 %copy.19.refs_0_ = s32[8,3]{1,0:T(8,128)S(1)} copy(s32[8,3]{0,1:T(4,128)} %param.4) | data formatting | bytes 192 | tf_op args[1]
  9.0 0.0 copy-start
  9.0 1.9 %copy-done = bf16[8,2,256,384]{3,2,1,0:T(8,128)(2,1)S(1)} copy-done((bf16[8,2,256,384]{3,2,1,0:T(8,128)(2,1)S(1)}, bf16[8,2,256,384]{3,2,1,0:T(8,128)(2,1)}, u32[]{:S(2)}) %copy-start) | copy-done | bytes 3145752
  10.9 0.0 copy-start.1
  10.9 6.6 %shard_map.58 = (f32[8,3,2,16,96]{4,3,2,1,0:T(8,128)}, f32[8,3,16,96]{3,2,1,0:T(8,128)}, f32[3,16,128]{2,1,0:T(8,128)S(1)}, f32[8,16,128]{2,1,0:T(8,128)S(1)}, f32[3,3,2,16,384]{4,3,2,1,0:T(8,128)S(1)}) custom-call(s32[8,3]{1,0:T(8,128)S(1)} %copy.19.refs_0_, bf16[8,2,256,384]{3,2,1,0:T(8,128)(2,1)S(1)} %copy-done), custom_call_target="tpu_custom_call" | custom-call | tf_op jit(solution)/shard_map/pallas_call | solution.py:252
  17.5 0.0 collective-permute-done.rim_ref.refs_8_
  17.5 0.0 copy-done.1
  17.5 0.0 copy-start.2
  17.5 1.5 %shard_map.59 = (f32[3,3,2,16,384]{4,3,2,1,0:T(8,128)S(1)}, f32[1,16,128]{2,1,0:T(8,128)S(1)}) custom-call(s32[3,3]{1,0:T(4,128)S(1)} %slice.53.off_ref.refs_0_, bf16[8,2,256,384]{3,2,1,0:T(8,128)(2,1)S(1)} %copy-done.1, bf16[1,2,256,384]{3,2,1,0:T(8,128)(2,1)S(1)} %collective-permute-done.rim_ref.refs_8_, ...), custom_call_target="tpu_custom_call", output_to_operand_aliasing={{0}: (3, {})} | custom-call | tf_op jit(solution)/shard_map/pallas_call | solution.py:329
  19.0 0.0 collective-permute-done.1.rim_ref.refs_9_
  19.0 1.1 %shard_map.60 = (f32[3,3,2,16,384]{4,3,2,1,0:T(8,128)S(1)}, f32[1,16,128]{2,1,0:T(8,128)S(1)}) custom-call(s32[3,3]{1,0:T(4,128)S(1)} %slice.53.off_ref.refs_0_, bf16[8,2,256,384]{3,2,1,0:T(8,128)(2,1)S(1)} %copy-done.1, bf16[1,2,256,384]{3,2,1,0:T(8,128)(2,1)S(1)} %collective-permute-done.1.rim_ref.refs_9_, ...), custom_call_target="tpu_custom_call", output_to_operand_aliasing={{0}: (3, {})} | custom-call | tf_op jit(solution)/shard_map/pallas_call | solution.py:329
  20.1 1.1 %collective-permute-done.2.refs_10_ = bf16[1,2,256,384]{3,2,1,0:T(8,128)(2,1)S(1)} collective-permute-done((bf16[1,2,256,384]{3,2,1,0:T(8,128)(2,1)S(1)}, bf16[1,2,256,384]{3,2,1,0:T(8,128)(2,1)S(1)}, u32[]{:S(2)}, u32[]{:S(2)}) %collective-permute-start.2) | collective-permute-done | bytes 393248 | tf_op jit(solution)/shard_map/ppermute | solution.py:17
  21.2 0.0 copy-done.2
  21.2 2.9 %shard_map.61 = (f32[8,3,2,16,96]{4,3,2,1,0:T(8,128)}, f32[8,3,16,96]{3,2,1,0:T(8,128)}, f32[16,4,128]{2,1,0:T(4,128)S(1)}) custom-call(s32[3,3]{1,0:T(4,128)S(1)} %slice.53.off_ref.refs_0_, s32[16]{0:T(128)S(1)} %copy-done.2, f32[5,16,128]{2,1,0:T(8,128)S(1)} %pad_maximum_fusion.refs_2_, ...), custom_call_target="tpu_custom_call", output_to_operand_aliasing={{0}: (5, {}), {1}: (6, {})} | custom-call | tf_op jit(solution)/shard_map/pallas_call | solution.py:252
  24.1 12.3 %all_to_all.5 = f32[16,4,128]{2,1,0:T(4,128)S(1)} all-to-all(f32[16,4,128]{2,1,0:T(4,128)S(1)} %get-tuple-element.26), channel_id=1, replica_groups=mesh['date'=16,'strip'=2] {'date'}, dimensions={0} | all-to-all | bytes 65536 | tf_op jit(solution)/shard_map/all_to_all | solution.py:369
  36.4 0.1 fusion.1
  36.5 0.1 copy.28
  36.5 0.1 copy.30
  36.6 0.1 copy.29
  36.7 0.1 copy.31
  36.8 0.1 copy.21
  36.9 0.1 copy.22
  37.0 0.1 maximum_add_fusion
  37.1 0.6 %copy.27 = f32[1,2,16,6]{2,1,3,0:T(2,128)} copy(f32[1,2,16,6]{2,3,1,0:T(8,128)S(1)} %maximum_divide_fusion) | data formatting | bytes 1536
  (6 shorter events, 0.1 us)
Async XLA Ops:
  2.0 15.5 %collective-permute-start = (bf16[1,2,256,384]{3,2,1,0:T(8,128)(2,1)S(1)}, bf16[1,2,256,384]{3,2,1,0:T(8,128)(2,1)S(1)}, u32[]{:S(2)}, u32[]{:S(2)}) collective-permute-start(bf16[1,2,256,384]{3,2,1,0:T(8,128)(2,1)S(1)} %get-tuple-element.38), channel_id=1, source_target_pairs={{0,30},{2,0},{4,2},{6,4},{8,6},{10,8},{12,10},{14,12},{16,14},{18,... | collective-permute-start | bytes 1179656 | tf_op jit(solution)/shard_map/ppermute | solution.py:17
  7.5 11.5 %collective-permute-start.1 = (bf16[1,2,256,384]{3,2,1,0:T(8,128)(2,1)S(1)}, bf16[1,2,256,384]{3,2,1,0:T(8,128)(2,1)S(1)}, u32[]{:S(2)}, u32[]{:S(2)}) collective-permute-start(bf16[1,2,256,384]{3,2,1,0:T(8,128)(2,1)S(1)} %get-tuple-element.37), channel_id=1, source_target_pairs={{0,30},{2,0},{4,2},{6,4},{8,6},{10,8},{12,10},{14,12},{16,14},{18,... | collective-permute-start | bytes 1179656 | tf_op jit(solution)/shard_map/ppermute | solution.py:17
  8.2 13.0 %collective-permute-start.2 = (bf16[1,2,256,384]{3,2,1,0:T(8,128)(2,1)S(1)}, bf16[1,2,256,384]{3,2,1,0:T(8,128)(2,1)S(1)}, u32[]{:S(2)}, u32[]{:S(2)}) collective-permute-start(bf16[1,2,256,384]{3,2,1,0:T(8,128)(2,1)S(1)} %get-tuple-element.36), channel_id=1, source_target_pairs={{0,30},{2,0},{4,2},{6,4},{8,6},{10,8},{12,10},{14,12},{16,14},{18,... | collective-permute-start | bytes 1179656 | tf_op jit(solution)/shard_map/ppermute | solution.py:17
  9.0 1.9 %copy-start = (bf16[8,2,256,384]{3,2,1,0:T(8,128)(2,1)S(1)}, bf16[8,2,256,384]{3,2,1,0:T(8,128)(2,1)}, u32[]{:S(2)}) copy-start(bf16[8,2,256,384]{3,2,1,0:T(8,128)(2,1)} %refs_7_.1) | copy-start | bytes 9437188
  10.9 6.6 %copy-start.1 = (bf16[8,2,256,384]{3,2,1,0:T(8,128)(2,1)S(1)}, bf16[8,2,256,384]{3,2,1,0:T(8,128)(2,1)}, u32[]{:S(2)}) copy-start(bf16[8,2,256,384]{3,2,1,0:T(8,128)(2,1)} %refs_7_.1) | copy-start | bytes 9437188
  17.5 3.7 %copy-start.2 = (s32[16]{0:T(128)S(1)}, s32[16]{0:T(128)}, u32[]{:S(2)}) copy-start(s32[16]{0:T(128)} %refs_1_.3) | copy-start | bytes 196

commit v13 on v12

--- a/solution.py
+++ b/solution.py
@@ -346,7 +346,8 @@
 def on_device(slc, offsets, owner):
     count = slc.shape[0]
     inner = count - NB
-    rims = [shifted(slc[t : t + 1], "date", -1) for t in range(NB)]
+    later = lax.optimization_barrier(slc)
+    rims = [shifted((slc if t == 0 else later)[t : t + 1], "date", -1) for t in range(NB)]
     ifg_a, coh_a, ws_a, pw_a, rx_a = local_math(
         offsets, [slc], [(0, t) for t in range(count)], 0, inner, count, 0
     )

time: 38 us -> 37.7 us (level)
  waiting for transfers between devices: 1.08 us -> 0.01 us
  local copies, waits for them, and re-layouts: 5.23 us -> 6.11 us
    ppermute x3, waiting for transfers between devices: 1.08 us -> 0.01 us  [shifted(): return lax.ppermute(value, axis, pairs)]
    slice x1 -> x2, local copies, waits for them, and re-layouts: 1.36 us -> 2.23 us  [on_device(): (slc if t == 0 else later)[t:t + 1]]
  transfers between devices with their start and end apart: 3 -> 3, of which waited for: 1 -> 0; matrix products, arithmetic and copies ran while one was open for 2% -> 5% of each run, Pallas kernels for 24% -> 24%
where the time goes in v13:
time: 37.7 us; the launch traced here: 37.4 us
  blocking collectives  12.1 us (32%)
  Pallas kernels  12 us (32%)
  starting transfers between devices  6.29 us (17%)
  local copies, waits for them, and re-layouts  6.11 us (16%)
  between operations  0.75 us (2%)
    all_to_all x1, blocking collectives, on_device(): lax.all_to_all(slotted, 'date', split_axis=0, concat_axis=0, tiled=True)  12.1 us
    pallas_call x2, Pallas kernels, local_math(): pl.pallas_call(make_kernel(images, first, dates, rows, cols, nknown, tile...  9.27 us
    ppermute x3, starting transfers between devices, shifted(): return lax.ppermute(value, axis, pairs)  6.29 us
    unnamed x12, local copies, waits for them, and re-layouts  3.63 us
    pallas_call x2, Pallas kernels, rim_step(): pl.pallas_call(kernel, out_shape=(jax.ShapeDtypeStruct(racc_in.shape, jnp...  2.76 us
    slice x2, local copies, waits for them, and re-layouts, on_device(): (slc if t == 0 else later)[t:t + 1]  2.23 us
  transfers between devices with their start and end apart: 3, of which 0 were waited for; matrix products, arithmetic and copies ran while one was open for 5% of the time, Pallas kernels for 24%

profile of v13, /device:TPU:0, one launch (start us, length us, event | category | flops | bytes accessed | tf_op | source)
XLA Modules:
  0.0 37.4 jit_solution(13033949705382783575)
XLA Ops:
  0.6 1.0 %slice.55 = bf16[1,2,256,384]{3,2,1,0:T(8,128)(2,1)S(1)} slice(bf16[8,2,256,384]{3,2,1,0:T(8,128)(2,1)} %refs_7_.1), slice={[0:1], [0:2], [0:256], [0:384]} | slice | bytes 786432 | tf_op jit(solution)/shard_map/slice | solution.py:350
  1.7 5.5 %collective-permute-start = (bf16[1,2,256,384]{3,2,1,0:T(8,128)(2,1)S(1)}, bf16[1,2,256,384]{3,2,1,0:T(8,128)(2,1)S(1)}, u32[]{:S(2)}, u32[]{:S(2)}) collective-permute-start(bf16[1,2,256,384]{3,2,1,0:T(8,128)(2,1)S(1)} %slice.55), channel_id=1, source_target_pairs={{0,30},{2,0},{4,2},{6,4},{8,6},{10,8},{12,10},{14,12},{16,14},{18,... | collective-permute-start | bytes 1179656 | tf_op jit(solution)/shard_map/ppermute | solution.py:17
  7.2 1.2 %fusion = (bf16[1,2,256,384]{3,2,1,0:T(8,128)(2,1)S(1)}, bf16[1,2,256,384]{3,2,1,0:T(8,128)(2,1)S(1)}) fusion(bf16[8,2,256,384]{3,2,1,0:T(8,128)(2,1)} %refs_7_.1), kind=kLoop, calls=%fused_computation.5 | loop fusion | bytes 1572864 | tf_op jit(solution)/shard_map/slice | solution.py:350
  8.4 0.7 %collective-permute-start.1 = (bf16[1,2,256,384]{3,2,1,0:T(8,128)(2,1)S(1)}, bf16[1,2,256,384]{3,2,1,0:T(8,128)(2,1)S(1)}, u32[]{:S(2)}, u32[]{:S(2)}) collective-permute-start(bf16[1,2,256,384]{3,2,1,0:T(8,128)(2,1)S(1)} %get-tuple-element.37), channel_id=1, source_target_pairs={{0,30},{2,0},{4,2},{6,4},{8,6},{10,8},{12,10},{14,12},{16,14},{18,... | collective-permute-start | bytes 1179656 | tf_op jit(solution)/shard_map/ppermute | solution.py:17
  9.1 0.1 collective-permute-start.2
  9.2 0.8 %copy.19.refs_0_ = s32[8,3]{1,0:T(8,128)S(1)} copy(s32[8,3]{0,1:T(4,128)} %param.4) | data formatting | bytes 192 | tf_op args[1]
  9.9 0.0 copy-start
  9.9 1.9 %copy-done = bf16[8,2,256,384]{3,2,1,0:T(8,128)(2,1)S(1)} copy-done((bf16[8,2,256,384]{3,2,1,0:T(8,128)(2,1)S(1)}, bf16[8,2,256,384]{3,2,1,0:T(8,128)(2,1)}, u32[]{:S(2)}) %copy-start) | copy-done | bytes 3145752
  11.8 0.0 copy-start.1
  11.8 6.4 %shard_map.58 = (f32[8,3,2,16,96]{4,3,2,1,0:T(8,128)}, f32[8,3,16,96]{3,2,1,0:T(8,128)}, f32[3,16,128]{2,1,0:T(8,128)S(1)}, f32[8,16,128]{2,1,0:T(8,128)S(1)}, f32[3,3,2,16,384]{4,3,2,1,0:T(8,128)S(1)}) custom-call(s32[8,3]{1,0:T(8,128)S(1)} %copy.19.refs_0_, bf16[8,2,256,384]{3,2,1,0:T(8,128)(2,1)S(1)} %copy-done), custom_call_target="tpu_custom_call" | custom-call | tf_op jit(solution)/shard_map/pallas_call | solution.py:252
  18.2 0.0 collective-permute-done.rim_ref.refs_8_
  18.2 0.0 copy-done.1
  18.3 0.0 copy-start.2
  18.3 1.1 %shard_map.59 = (f32[3,3,2,16,384]{4,3,2,1,0:T(8,128)S(1)}, f32[1,16,128]{2,1,0:T(8,128)S(1)}) custom-call(s32[3,3]{1,0:T(4,128)S(1)} %slice.53.off_ref.refs_0_, bf16[8,2,256,384]{3,2,1,0:T(8,128)(2,1)S(1)} %copy-done.1, bf16[1,2,256,384]{3,2,1,0:T(8,128)(2,1)S(1)} %collective-permute-done.rim_ref.refs_8_, ...), custom_call_target="tpu_custom_call", output_to_operand_aliasing={{0}: (3, {})} | custom-call | tf_op jit(solution)/shard_map/pallas_call | solution.py:329
  19.4 0.0 collective-permute-done.1.rim_ref.refs_9_
  19.4 1.7 %shard_map.60 = (f32[3,3,2,16,384]{4,3,2,1,0:T(8,128)S(1)}, f32[1,16,128]{2,1,0:T(8,128)S(1)}) custom-call(s32[3,3]{1,0:T(4,128)S(1)} %slice.53.off_ref.refs_0_, bf16[8,2,256,384]{3,2,1,0:T(8,128)(2,1)S(1)} %copy-done.1, bf16[1,2,256,384]{3,2,1,0:T(8,128)(2,1)S(1)} %collective-permute-done.1.rim_ref.refs_9_, ...), custom_call_target="tpu_custom_call", output_to_operand_aliasing={{0}: (3, {})} | custom-call | tf_op jit(solution)/shard_map/pallas_call | solution.py:329
  21.1 0.0 collective-permute-done.2.refs_10_
  21.1 0.0 copy-done.2
  21.1 2.9 %shard_map.61 = (f32[8,3,2,16,96]{4,3,2,1,0:T(8,128)}, f32[8,3,16,96]{3,2,1,0:T(8,128)}, f32[16,4,128]{2,1,0:T(4,128)S(1)}) custom-call(s32[3,3]{1,0:T(4,128)S(1)} %slice.53.off_ref.refs_0_, s32[16]{0:T(128)S(1)} %copy-done.2, f32[5,16,128]{2,1,0:T(8,128)S(1)} %pad_maximum_fusion.refs_2_, ...), custom_call_target="tpu_custom_call", output_to_operand_aliasing={{0}: (5, {}), {1}: (6, {})} | custom-call | tf_op jit(solution)/shard_map/pallas_call | solution.py:252
  24.0 12.1 %all_to_all.5 = f32[16,4,128]{2,1,0:T(4,128)S(1)} all-to-all(f32[16,4,128]{2,1,0:T(4,128)S(1)} %get-tuple-element.26), channel_id=1, replica_groups=mesh['date'=16,'strip'=2] {'date'}, dimensions={0} | all-to-all | bytes 65536 | tf_op jit(solution)/shard_map/all_to_all | solution.py:370
  36.1 0.1 fusion.1
  36.1 0.1 copy.28
  36.2 0.1 copy.30
  36.3 0.1 copy.29
  36.4 0.1 copy.31
  36.5 0.1 copy.21
  36.6 0.1 copy.22
  36.7 0.1 maximum_add_fusion
  36.8 0.6 %copy.27 = f32[1,2,16,6]{2,1,3,0:T(2,128)} copy(f32[1,2,16,6]{2,3,1,0:T(8,128)S(1)} %maximum_divide_fusion) | data formatting | bytes 1536
  (6 shorter events, 0.1 us)
Async XLA Ops:
  1.7 16.6 %collective-permute-start = (bf16[1,2,256,384]{3,2,1,0:T(8,128)(2,1)S(1)}, bf16[1,2,256,384]{3,2,1,0:T(8,128)(2,1)S(1)}, u32[]{:S(2)}, u32[]{:S(2)}) collective-permute-start(bf16[1,2,256,384]{3,2,1,0:T(8,128)(2,1)S(1)} %slice.55), channel_id=1, source_target_pairs={{0,30},{2,0},{4,2},{6,4},{8,6},{10,8},{12,10},{14,12},{16,14},{18,... | collective-permute-start | bytes 1179656 | tf_op jit(solution)/shard_map/ppermute | solution.py:17
  8.4 11.0 %collective-permute-start.1 = (bf16[1,2,256,384]{3,2,1,0:T(8,128)(2,1)S(1)}, bf16[1,2,256,384]{3,2,1,0:T(8,128)(2,1)S(1)}, u32[]{:S(2)}, u32[]{:S(2)}) collective-permute-start(bf16[1,2,256,384]{3,2,1,0:T(8,128)(2,1)S(1)} %get-tuple-element.37), channel_id=1, source_target_pairs={{0,30},{2,0},{4,2},{6,4},{8,6},{10,8},{12,10},{14,12},{16,14},{18,... | collective-permute-start | bytes 1179656 | tf_op jit(solution)/shard_map/ppermute | solution.py:17
  9.1 12.0 %collective-permute-start.2 = (bf16[1,2,256,384]{3,2,1,0:T(8,128)(2,1)S(1)}, bf16[1,2,256,384]{3,2,1,0:T(8,128)(2,1)S(1)}, u32[]{:S(2)}, u32[]{:S(2)}) collective-permute-start(bf16[1,2,256,384]{3,2,1,0:T(8,128)(2,1)S(1)} %get-tuple-element.36), channel_id=1, source_target_pairs={{0,30},{2,0},{4,2},{6,4},{8,6},{10,8},{12,10},{14,12},{16,14},{18,... | collective-permute-start | bytes 1179656 | tf_op jit(solution)/shard_map/ppermute | solution.py:17
  9.9 1.9 %copy-start = (bf16[8,2,256,384]{3,2,1,0:T(8,128)(2,1)S(1)}, bf16[8,2,256,384]{3,2,1,0:T(8,128)(2,1)}, u32[]{:S(2)}) copy-start(bf16[8,2,256,384]{3,2,1,0:T(8,128)(2,1)} %refs_7_.1) | copy-start | bytes 9437188
  11.8 6.4 %copy-start.1 = (bf16[8,2,256,384]{3,2,1,0:T(8,128)(2,1)S(1)}, bf16[8,2,256,384]{3,2,1,0:T(8,128)(2,1)}, u32[]{:S(2)}) copy-start(bf16[8,2,256,384]{3,2,1,0:T(8,128)(2,1)} %refs_7_.1) | copy-start | bytes 9437188
  18.3 2.8 %copy-start.2 = (s32[16]{0:T(128)S(1)}, s32[16]{0:T(128)}, u32[]{:S(2)}) copy-start(s32[16]{0:T(128)} %refs_1_.3) | copy-start | bytes 196

commit v14 on v13

--- a/solution.py
+++ b/solution.py
@@ -27,7 +27,7 @@
     return out + jnp.dot(lo, pool, preferred_element_type=jnp.float32)
 
 
-def make_kernel(images, first, dates, rows, cols, known, tiles, date0, pw_base):
+def make_kernel(images, first, dates, rows, cols, known, tiles, date0, pw_base, emit_ws):
     groups = rows // LR
     cells = cols // LA
     total = len(images)
@@ -91,11 +91,12 @@
                     pacc[j - known, pl.ds(blk * 8, 8), pl.ds(ct * 128, 128)] = fold(parts)
             return c
 
-        lax.fori_loop(known, total, power, 0)
         fresh = total - known
-        pw[pl.ds(known, fresh)] = split_pool(pacc[...].reshape(fresh * groups, cols), pool).reshape(
-            fresh, groups, lanes
-        )
+        if fresh:
+            lax.fori_loop(known, total, power, 0)
+            pw[pl.ds(known, fresh)] = split_pool(pacc[...].reshape(fresh * groups, cols), pool).reshape(
+                fresh, groups, lanes
+            )
         if known:
             pw_cp.wait()
         else:
@@ -173,7 +174,7 @@
         ]
         for cp in outs:
             cp.start()
-        if not known:
+        if not known or emit_ws:
             last_ref[0] = wr
             last_ref[1] = wi
             last_ref[2] = wc
@@ -201,7 +202,7 @@
     return kernel
 
 
-def local_math(offsets, sources, images, first, dates, count, date0, known=None):
+def local_math(offsets, sources, images, first, dates, count, date0, known=None, emit_ws=False):
     pair_dates = offsets.shape[0]
     _, _, rows, cols = sources[0].shape
     groups = rows // LR
@@ -239,18 +240,21 @@
     else:
         owner, pw_in, ws_in, rx_in, ifg_in, coh_in, pw_base = known
         nknown, tiles = pw_in.shape[0], owner.shape[0]
-        out_shape = full + [jax.ShapeDtypeStruct((tiles, SLOT, lanes), jnp.float32)]
-        out_specs = [anyspace, anyspace, anyspace]
+        if emit_ws:
+            out_shape = full + [jax.ShapeDtypeStruct((3, groups, lanes), jnp.float32)]
+        else:
+            out_shape = full + [jax.ShapeDtypeStruct((tiles, SLOT, lanes), jnp.float32)]
+        out_specs = [anyspace, anyspace, pl.BlockSpec(memory_space=vmem) if emit_ws else anyspace]
         in_specs = [pl.BlockSpec(memory_space=smem), pl.BlockSpec(memory_space=smem)] + [
             anyspace for _ in range(5)
         ] + [hbm for _ in sources]
         extra = [owner, pw_in, ws_in, rx_in, ifg_in, coh_in]
         aliases = {5: 0, 6: 1}
         scratch += [pltpu.VMEM((tiles, SLOT, lanes), jnp.float32), pltpu.VMEM((3, groups, lanes), jnp.float32)]
-    scratch[1] = pltpu.VMEM((total - nknown, groups, cols), jnp.float32)
+    scratch[1] = pltpu.VMEM((max(1, total - nknown), groups, cols), jnp.float32)
     scratch += [pltpu.SemaphoreType.DMA((6,))]
     return pl.pallas_call(
-        make_kernel(images, first, dates, rows, cols, nknown, tiles, date0, pw_base),
+        make_kernel(images, first, dates, rows, cols, nknown, tiles, date0, pw_base, emit_ws),
         out_shape=tuple(out_shape),
         in_specs=in_specs,
         out_specs=tuple(out_specs),
@@ -356,15 +360,28 @@
     for step in range(NB - 1):
         racc, pw_step = rim_step(offsets[inner:], racc, slc, rims[step], step, inner)
         powers.append(pw_step)
-    interferograms, coherence, slotted = local_math(
-        offsets[inner:],
-        [slc] + rims,
-        [(0, inner + t) for t in range(NB)] + [(1 + t, 0) for t in range(NB)],
+    powers = jnp.concatenate(powers, 0)
+    own = [(0, inner + t) for t in range(NB)]
+    ifg_p, coh_p, ws_p = local_math(
+        offsets[inner : count - 1],
+        [slc] + rims[: NB - 1],
+        own + [(1 + t, 0) for t in range(NB - 1)],
         0,
-        NB,
+        NB - 1,
         count,
         inner,
-        known=(owner, jnp.concatenate(powers, 0), ws_a, racc, ifg_a, coh_a, 0),
+        known=(owner, powers, ws_a, racc[: NB - 1], ifg_a, coh_a, 0),
+        emit_ws=True,
+    )
+    interferograms, coherence, slotted = local_math(
+        offsets[count - 1 :],
+        [slc] + rims,
+        own + [(1 + t, 0) for t in range(NB)],
+        NB - 1,
+        1,
+        count,
+        count - 1,
+        known=(owner, powers, ws_p, racc[NB - 1 :], ifg_p, coh_p, 0),
     )
     width = ifg_a.shape[-1] // owner.shape[0]
     sums = lax.all_to_all(slotted, "date", split_axis=0, concat_axis=0, tiled=True).sum(0)

time: 37.7 us -> 37.3 us (0.989)
  blocking collectives: 12.1 us -> 10.3 us
  Pallas kernels: 12 us -> 13.5 us
    all_to_all x1, blocking collectives: 12.1 us -> 10.3 us  [on_device(): lax.all_to_all(slotted, 'date', split_axis=0, concat_axis=0, tiled=True)]
    pallas_call x2 -> x3, Pallas kernels: 9.27 us -> 10.2 us  [local_math(): pl.pallas_call(make_kernel(images, first, dates, rows, cols, nknown, tile...]
    pallas_call x2, Pallas kernels: 2.76 us -> 3.23 us  [rim_step(): pl.pallas_call(kernel, out_shape=(jax.ShapeDtypeStruct(racc_in.shape, jnp...]
  transfers between devices with their start and end apart: 3 -> 3, of which waited for: 0 -> 0; matrix products, arithmetic and copies ran while one was open for 5% -> 5% of each run, Pallas kernels for 24% -> 30%
where the time goes in v14:
time: 37.3 us; the launch traced here: 37.1 us
  Pallas kernels  13.5 us (36%)
  blocking collectives  10.3 us (28%)
  starting transfers between devices  6.29 us (17%)
  local copies, waits for them, and re-layouts  6.14 us (16%)
  between operations  0.78 us (2%)
    all_to_all x1, blocking collectives, on_device(): lax.all_to_all(slotted, 'date', split_axis=0, concat_axis=0, tiled=True)  10.3 us
    pallas_call x3, Pallas kernels, local_math(): pl.pallas_call(make_kernel(images, first, dates, rows, cols, nknown, tile...  10.2 us
    ppermute x3, starting transfers between devices, shifted(): return lax.ppermute(value, axis, pairs)  6.29 us
    unnamed x12, local copies, waits for them, and re-layouts  3.62 us
    pallas_call x2, Pallas kernels, rim_step(): pl.pallas_call(kernel, out_shape=(jax.ShapeDtypeStruct(racc_in.shape, jnp...  3.23 us
    slice x2, local copies, waits for them, and re-layouts, on_device(): (slc if t == 0 else later)[t:t + 1]  2.23 us
  transfers between devices with their start and end apart: 3, of which 0 were waited for; matrix products, arithmetic and copies ran while one was open for 5% of the time, Pallas kernels for 30%

profile of v14, /device:TPU:0, one launch (start us, length us, event | category | flops | bytes accessed | tf_op | source)
XLA Modules:
  0.0 37.1 jit_solution(2897798184310735038)
XLA Ops:
  0.6 1.0 %slice.67 = bf16[1,2,256,384]{3,2,1,0:T(8,128)(2,1)S(1)} slice(bf16[8,2,256,384]{3,2,1,0:T(8,128)(2,1)} %refs_7_.3), slice={[0:1], [0:2], [0:256], [0:384]} | slice | bytes 786432 | tf_op jit(solution)/shard_map/slice | solution.py:354
  1.7 5.5 %collective-permute-start = (bf16[1,2,256,384]{3,2,1,0:T(8,128)(2,1)S(1)}, bf16[1,2,256,384]{3,2,1,0:T(8,128)(2,1)S(1)}, u32[]{:S(2)}, u32[]{:S(2)}) collective-permute-start(bf16[1,2,256,384]{3,2,1,0:T(8,128)(2,1)S(1)} %slice.67), channel_id=1, source_target_pairs={{0,30},{2,0},{4,2},{6,4},{8,6},{10,8},{12,10},{14,12},{16,14},{18,... | collective-permute-start | bytes 1179656 | tf_op jit(solution)/shard_map/ppermute | solution.py:17
  7.2 1.2 %fusion = (bf16[1,2,256,384]{3,2,1,0:T(8,128)(2,1)S(1)}, bf16[1,2,256,384]{3,2,1,0:T(8,128)(2,1)S(1)}) fusion(bf16[8,2,256,384]{3,2,1,0:T(8,128)(2,1)} %refs_7_.3), kind=kLoop, calls=%fused_computation.5 | loop fusion | bytes 1572864 | tf_op jit(solution)/shard_map/slice | solution.py:354
  8.4 0.7 %collective-permute-start.1 = (bf16[1,2,256,384]{3,2,1,0:T(8,128)(2,1)S(1)}, bf16[1,2,256,384]{3,2,1,0:T(8,128)(2,1)S(1)}, u32[]{:S(2)}, u32[]{:S(2)}) collective-permute-start(bf16[1,2,256,384]{3,2,1,0:T(8,128)(2,1)S(1)} %get-tuple-element.43), channel_id=1, source_target_pairs={{0,30},{2,0},{4,2},{6,4},{8,6},{10,8},{12,10},{14,12},{16,14},{18,... | collective-permute-start | bytes 1179656 | tf_op jit(solution)/shard_map/ppermute | solution.py:17
  9.1 0.1 collective-permute-start.2
  9.2 0.8 %copy.25.refs_0_ = s32[8,3]{1,0:T(8,128)S(1)} copy(s32[8,3]{0,1:T(4,128)} %param.4) | data formatting | bytes 192 | tf_op args[1]
  9.9 0.0 copy-start
  9.9 1.9 %copy-done = bf16[8,2,256,384]{3,2,1,0:T(8,128)(2,1)S(1)} copy-done((bf16[8,2,256,384]{3,2,1,0:T(8,128)(2,1)S(1)}, bf16[8,2,256,384]{3,2,1,0:T(8,128)(2,1)}, u32[]{:S(2)}) %copy-start) | copy-done | bytes 3145752
  11.8 0.0 copy-start.1
  11.8 6.1 %shard_map.58 = (f32[8,3,2,16,96]{4,3,2,1,0:T(8,128)}, f32[8,3,16,96]{3,2,1,0:T(8,128)}, f32[3,16,128]{2,1,0:T(8,128)S(1)}, f32[8,16,128]{2,1,0:T(8,128)S(1)}, f32[3,3,2,16,384]{4,3,2,1,0:T(8,128)S(1)}) custom-call(s32[8,3]{1,0:T(8,128)S(1)} %copy.25.refs_0_, bf16[8,2,256,384]{3,2,1,0:T(8,128)(2,1)S(1)} %copy-done), custom_call_target="tpu_custom_call" | custom-call | tf_op jit(solution)/shard_map/pallas_call | solution.py:256
  17.9 0.0 collective-permute-done.rim_ref.refs_8_
  18.0 0.0 copy-done.1
  18.0 2.0 %shard_map.59 = (f32[3,3,2,16,384]{4,3,2,1,0:T(8,128)S(1)}, f32[1,16,128]{2,1,0:T(8,128)S(1)}) custom-call(s32[3,3]{1,0:T(4,128)S(1)} %slice.66.off_ref, bf16[8,2,256,384]{3,2,1,0:T(8,128)(2,1)S(1)} %copy-done.1, bf16[1,2,256,384]{3,2,1,0:T(8,128)(2,1)S(1)} %collective-permute-done.rim_ref.refs_8_, ...), custom_call_target="tpu_custom_call", output_to_operand_aliasing={{0}: (3, {})} | custom-call | tf_op jit(solution)/shard_map/pallas_call | solution.py:333
  20.0 0.0 copy-start.2
  20.0 0.0 collective-permute-done.1.rim_ref.refs_9_
  20.0 1.2 %shard_map.60 = (f32[3,3,2,16,384]{4,3,2,1,0:T(8,128)S(1)}, f32[1,16,128]{2,1,0:T(8,128)S(1)}) custom-call(s32[3,3]{1,0:T(4,128)S(1)} %slice.66.off_ref, bf16[8,2,256,384]{3,2,1,0:T(8,128)(2,1)S(1)} %copy-done.1, bf16[1,2,256,384]{3,2,1,0:T(8,128)(2,1)S(1)} %collective-permute-done.1.rim_ref.refs_9_, ...), custom_call_target="tpu_custom_call", output_to_operand_aliasing={{0}: (3, {})} | custom-call | tf_op jit(solution)/shard_map/pallas_call | solution.py:333
  21.3 0.0 copy-done.2
  21.3 1.9 %shard_map.61 = (f32[8,3,2,16,96]{4,3,2,1,0:T(8,128)}, f32[8,3,16,96]{3,2,1,0:T(8,128)}, f32[3,16,128]{2,1,0:T(8,128)S(1)}) custom-call(s32[2,3]{1,0:T(2,128)S(1)} %slice.69.refs_0_, s32[16]{0:T(128)S(1)} %copy-done.2, f32[5,16,128]{2,1,0:T(8,128)S(1)} %pad_maximum_fusion.refs_2_, ...), custom_call_target="tpu_custom_call", output_to_operand_aliasing={{0}: (5, {}), {1}: (6, {})} | custom-call | tf_op jit(solution)/shard_map/pallas_call | solution.py:256
  23.2 0.0 collective-permute-done.2.refs_10_
  23.2 2.3 %shard_map.62 = (f32[8,3,2,16,96]{4,3,2,1,0:T(8,128)}, f32[8,3,16,96]{3,2,1,0:T(8,128)}, f32[16,4,128]{2,1,0:T(4,128)S(1)}) custom-call(s32[1,3]{1,0:T(1,128)S(1)} %slice.64.refs_0_, s32[16]{0:T(128)S(1)} %copy-done.2, f32[5,16,128]{2,1,0:T(8,128)S(1)} %pad_maximum_fusion.refs_2_, ...), custom_call_target="tpu_custom_call", output_to_operand_aliasing={{0}: (5, {}), {1}: (6, {})} | custom-call | tf_op jit(solution)/shard_map/pallas_call | solution.py:256
  25.5 10.3 %all_to_all.5 = f32[16,4,128]{2,1,0:T(4,128)S(1)} all-to-all(f32[16,4,128]{2,1,0:T(4,128)S(1)} %get-tuple-element.32), channel_id=1, replica_groups=mesh['date'=16,'strip'=2] {'date'}, dimensions={0} | all-to-all | bytes 65536 | tf_op jit(solution)/shard_map/all_to_all | solution.py:387
  35.8 0.1 fusion.1
  35.9 0.1 copy.36
  36.0 0.1 copy.38
  36.0 0.1 copy.37
  36.1 0.1 copy.39
  36.3 0.1 copy.29
  36.3 0.1 copy.30
  36.4 0.1 maximum_add_fusion
  36.5 0.6 %copy.35 = f32[1,2,16,6]{2,1,3,0:T(2,128)} copy(f32[1,2,16,6]{2,3,1,0:T(8,128)S(1)} %maximum_divide_fusion) | data formatting | bytes 1536
  (10 shorter events, 0.1 us)
Async XLA Ops:
  1.7 16.3 %collective-permute-start = (bf16[1,2,256,384]{3,2,1,0:T(8,128)(2,1)S(1)}, bf16[1,2,256,384]{3,2,1,0:T(8,128)(2,1)S(1)}, u32[]{:S(2)}, u32[]{:S(2)}) collective-permute-start(bf16[1,2,256,384]{3,2,1,0:T(8,128)(2,1)S(1)} %slice.67), channel_id=1, source_target_pairs={{0,30},{2,0},{4,2},{6,4},{8,6},{10,8},{12,10},{14,12},{16,14},{18,... | collective-permute-start | bytes 1179656 | tf_op jit(solution)/shard_map/ppermute | solution.py:17
  8.4 11.6 %collective-permute-start.1 = (bf16[1,2,256,384]{3,2,1,0:T(8,128)(2,1)S(1)}, bf16[1,2,256,384]{3,2,1,0:T(8,128)(2,1)S(1)}, u32[]{:S(2)}, u32[]{:S(2)}) collective-permute-start(bf16[1,2,256,384]{3,2,1,0:T(8,128)(2,1)S(1)} %get-tuple-element.43), channel_id=1, source_target_pairs={{0,30},{2,0},{4,2},{6,4},{8,6},{10,8},{12,10},{14,12},{16,14},{18,... | collective-permute-start | bytes 1179656 | tf_op jit(solution)/shard_map/ppermute | solution.py:17
  9.1 14.1 %collective-permute-start.2 = (bf16[1,2,256,384]{3,2,1,0:T(8,128)(2,1)S(1)}, bf16[1,2,256,384]{3,2,1,0:T(8,128)(2,1)S(1)}, u32[]{:S(2)}, u32[]{:S(2)}) collective-permute-start(bf16[1,2,256,384]{3,2,1,0:T(8,128)(2,1)S(1)} %get-tuple-element.42), channel_id=1, source_target_pairs={{0,30},{2,0},{4,2},{6,4},{8,6},{10,8},{12,10},{14,12},{16,14},{18,... | collective-permute-start | bytes 1179656 | tf_op jit(solution)/shard_map/ppermute | solution.py:17
  9.9 1.9 %copy-start = (bf16[8,2,256,384]{3,2,1,0:T(8,128)(2,1)S(1)}, bf16[8,2,256,384]{3,2,1,0:T(8,128)(2,1)}, u32[]{:S(2)}) copy-start(bf16[8,2,256,384]{3,2,1,0:T(8,128)(2,1)} %refs_7_.3) | copy-start | bytes 9437188
  11.8 6.1 %copy-start.1 = (bf16[8,2,256,384]{3,2,1,0:T(8,128)(2,1)S(1)}, bf16[8,2,256,384]{3,2,1,0:T(8,128)(2,1)}, u32[]{:S(2)}) copy-start(bf16[8,2,256,384]{3,2,1,0:T(8,128)(2,1)} %refs_7_.3) | copy-start | bytes 9437188
  20.0 1.3 %copy-start.2 = (s32[16]{0:T(128)S(1)}, s32[16]{0:T(128)}, u32[]{:S(2)}) copy-start(s32[16]{0:T(128)} %refs_1_.5) | copy-start | bytes 196

commit v15 on v14

--- a/solution.py
+++ b/solution.py
@@ -192,12 +192,9 @@
                     at = (h * 3 + f) * width
                     moved = pltpu.roll(sums[f][h * SLOT : h * SLOT + SLOT], (lanes + at - base) % lanes, 1)
                     block = jnp.where((lane >= at) & (lane < at + width), moved, block)
-            pay[owner_ref[t]] = block
-        pay_cp = pltpu.make_async_copy(pay, last_ref, osem.at[5])
-        pay_cp.start()
+            last_ref[owner_ref[t]] = block
         for cp in outs:
             cp.wait()
-        pay_cp.wait()
 
     return kernel
 
@@ -244,7 +241,7 @@
             out_shape = full + [jax.ShapeDtypeStruct((3, groups, lanes), jnp.float32)]
         else:
             out_shape = full + [jax.ShapeDtypeStruct((tiles, SLOT, lanes), jnp.float32)]
-        out_specs = [anyspace, anyspace, pl.BlockSpec(memory_space=vmem) if emit_ws else anyspace]
+        out_specs = [anyspace, anyspace, pl.BlockSpec(memory_space=vmem)]
         in_specs = [pl.BlockSpec(memory_space=smem), pl.BlockSpec(memory_space=smem)] + [
             anyspace for _ in range(5)
         ] + [hbm for _ in sources]

time: 37.3 us -> 37.3 us (level)
  no operation moved by 1% of the time
where the time goes in v15:
time: 37.3 us; the launch traced here: 36.9 us
  Pallas kernels  13.5 us (36%)
  blocking collectives  10.1 us (27%)
  starting transfers between devices  6.29 us (17%)
  local copies, waits for them, and re-layouts  6.14 us (16%)
  between operations  0.78 us (2%)
    pallas_call x3, Pallas kernels, local_math(): pl.pallas_call(make_kernel(images, first, dates, rows, cols, nknown, tile...  10.5 us
    all_to_all x1, blocking collectives, on_device(): lax.all_to_all(slotted, 'date', split_axis=0, concat_axis=0, tiled=True)  10.1 us
    ppermute x3, starting transfers between devices, shifted(): return lax.ppermute(value, axis, pairs)  6.29 us
    unnamed x12, local copies, waits for them, and re-layouts  3.62 us
    pallas_call x2, Pallas kernels, rim_step(): pl.pallas_call(kernel, out_shape=(jax.ShapeDtypeStruct(racc_in.shape, jnp...  2.93 us
    slice x2, local copies, waits for them, and re-layouts, on_device(): (slc if t == 0 else later)[t:t + 1]  2.23 us
  transfers between devices with their start and end apart: 3, of which 0 were waited for; matrix products, arithmetic and copies ran while one was open for 5% of the time, Pallas kernels for 30%

profile of v15, /device:TPU:0, one launch (start us, length us, event | category | flops | bytes accessed | tf_op | source)
XLA Modules:
  0.0 36.9 jit_solution(13853844111256162121)
XLA Ops:
  0.6 1.0 %slice.67 = bf16[1,2,256,384]{3,2,1,0:T(8,128)(2,1)S(1)} slice(bf16[8,2,256,384]{3,2,1,0:T(8,128)(2,1)} %refs_7_.3), slice={[0:1], [0:2], [0:256], [0:384]} | slice | bytes 786432 | tf_op jit(solution)/shard_map/slice | solution.py:351
  1.7 5.5 %collective-permute-start = (bf16[1,2,256,384]{3,2,1,0:T(8,128)(2,1)S(1)}, bf16[1,2,256,384]{3,2,1,0:T(8,128)(2,1)S(1)}, u32[]{:S(2)}, u32[]{:S(2)}) collective-permute-start(bf16[1,2,256,384]{3,2,1,0:T(8,128)(2,1)S(1)} %slice.67), channel_id=1, source_target_pairs={{0,30},{2,0},{4,2},{6,4},{8,6},{10,8},{12,10},{14,12},{16,14},{18,... | collective-permute-start | bytes 1179656 | tf_op jit(solution)/shard_map/ppermute | solution.py:17
  7.2 1.2 %fusion = (bf16[1,2,256,384]{3,2,1,0:T(8,128)(2,1)S(1)}, bf16[1,2,256,384]{3,2,1,0:T(8,128)(2,1)S(1)}) fusion(bf16[8,2,256,384]{3,2,1,0:T(8,128)(2,1)} %refs_7_.3), kind=kLoop, calls=%fused_computation.5 | loop fusion | bytes 1572864 | tf_op jit(solution)/shard_map/slice | solution.py:351
  8.4 0.7 %collective-permute-start.1 = (bf16[1,2,256,384]{3,2,1,0:T(8,128)(2,1)S(1)}, bf16[1,2,256,384]{3,2,1,0:T(8,128)(2,1)S(1)}, u32[]{:S(2)}, u32[]{:S(2)}) collective-permute-start(bf16[1,2,256,384]{3,2,1,0:T(8,128)(2,1)S(1)} %get-tuple-element.43), channel_id=1, source_target_pairs={{0,30},{2,0},{4,2},{6,4},{8,6},{10,8},{12,10},{14,12},{16,14},{18,... | collective-permute-start | bytes 1179656 | tf_op jit(solution)/shard_map/ppermute | solution.py:17
  9.1 0.1 collective-permute-start.2
  9.2 0.8 %copy.25.refs_0_ = s32[8,3]{1,0:T(8,128)S(1)} copy(s32[8,3]{0,1:T(4,128)} %param.4) | data formatting | bytes 192 | tf_op args[1]
  9.9 0.0 copy-start
  9.9 1.9 %copy-done = bf16[8,2,256,384]{3,2,1,0:T(8,128)(2,1)S(1)} copy-done((bf16[8,2,256,384]{3,2,1,0:T(8,128)(2,1)S(1)}, bf16[8,2,256,384]{3,2,1,0:T(8,128)(2,1)}, u32[]{:S(2)}) %copy-start) | copy-done | bytes 3145752
  11.8 0.0 copy-start.1
  11.8 6.3 %shard_map.58 = (f32[8,3,2,16,96]{4,3,2,1,0:T(8,128)}, f32[8,3,16,96]{3,2,1,0:T(8,128)}, f32[3,16,128]{2,1,0:T(8,128)S(1)}, f32[8,16,128]{2,1,0:T(8,128)S(1)}, f32[3,3,2,16,384]{4,3,2,1,0:T(8,128)S(1)}) custom-call(s32[8,3]{1,0:T(8,128)S(1)} %copy.25.refs_0_, bf16[8,2,256,384]{3,2,1,0:T(8,128)(2,1)S(1)} %copy-done), custom_call_target="tpu_custom_call" | custom-call | tf_op jit(solution)/shard_map/pallas_call | solution.py:253
  18.1 0.0 collective-permute-done.rim_ref.refs_8_
  18.1 0.0 copy-done.1
  18.1 1.6 %shard_map.59 = (f32[3,3,2,16,384]{4,3,2,1,0:T(8,128)S(1)}, f32[1,16,128]{2,1,0:T(8,128)S(1)}) custom-call(s32[3,3]{1,0:T(4,128)S(1)} %slice.66.off_ref, bf16[8,2,256,384]{3,2,1,0:T(8,128)(2,1)S(1)} %copy-done.1, bf16[1,2,256,384]{3,2,1,0:T(8,128)(2,1)S(1)} %collective-permute-done.rim_ref.refs_8_, ...), custom_call_target="tpu_custom_call", output_to_operand_aliasing={{0}: (3, {})} | custom-call | tf_op jit(solution)/shard_map/pallas_call | solution.py:330
  19.7 0.0 copy-start.2
  19.7 0.0 collective-permute-done.1.rim_ref.refs_9_
  19.7 1.4 %shard_map.60 = (f32[3,3,2,16,384]{4,3,2,1,0:T(8,128)S(1)}, f32[1,16,128]{2,1,0:T(8,128)S(1)}) custom-call(s32[3,3]{1,0:T(4,128)S(1)} %slice.66.off_ref, bf16[8,2,256,384]{3,2,1,0:T(8,128)(2,1)S(1)} %copy-done.1, bf16[1,2,256,384]{3,2,1,0:T(8,128)(2,1)S(1)} %collective-permute-done.1.rim_ref.refs_9_, ...), custom_call_target="tpu_custom_call", output_to_operand_aliasing={{0}: (3, {})} | custom-call | tf_op jit(solution)/shard_map/pallas_call | solution.py:330
  21.1 0.0 copy-done.2
  21.2 1.9 %shard_map.61 = (f32[8,3,2,16,96]{4,3,2,1,0:T(8,128)}, f32[8,3,16,96]{3,2,1,0:T(8,128)}, f32[3,16,128]{2,1,0:T(8,128)S(1)}) custom-call(s32[2,3]{1,0:T(2,128)S(1)} %slice.69.refs_0_, s32[16]{0:T(128)S(1)} %copy-done.2, f32[5,16,128]{2,1,0:T(8,128)S(1)} %pad_maximum_fusion.refs_2_, ...), custom_call_target="tpu_custom_call", output_to_operand_aliasing={{0}: (5, {}), {1}: (6, {})} | custom-call | tf_op jit(solution)/shard_map/pallas_call | solution.py:253
  23.0 0.0 collective-permute-done.2.refs_10_
  23.0 2.4 %shard_map.62 = (f32[8,3,2,16,96]{4,3,2,1,0:T(8,128)}, f32[8,3,16,96]{3,2,1,0:T(8,128)}, f32[16,4,128]{2,1,0:T(4,128)S(1)}) custom-call(s32[1,3]{1,0:T(1,128)S(1)} %slice.64.refs_0_, s32[16]{0:T(128)S(1)} %copy-done.2, f32[5,16,128]{2,1,0:T(8,128)S(1)} %pad_maximum_fusion.refs_2_, ...), custom_call_target="tpu_custom_call", output_to_operand_aliasing={{0}: (5, {}), {1}: (6, {})} | custom-call | tf_op jit(solution)/shard_map/pallas_call | solution.py:253
  25.5 10.1 %all_to_all.5 = f32[16,4,128]{2,1,0:T(4,128)S(1)} all-to-all(f32[16,4,128]{2,1,0:T(4,128)S(1)} %get-tuple-element.32), channel_id=1, replica_groups=mesh['date'=16,'strip'=2] {'date'}, dimensions={0} | all-to-all | bytes 65536 | tf_op jit(solution)/shard_map/all_to_all | solution.py:384
  35.6 0.1 fusion.1
  35.7 0.1 copy.36
  35.8 0.1 copy.38
  35.9 0.1 copy.37
  36.0 0.1 copy.39
  36.1 0.1 copy.29
  36.2 0.1 copy.30
  36.2 0.1 maximum_add_fusion
  36.3 0.6 %copy.35 = f32[1,2,16,6]{2,1,3,0:T(2,128)} copy(f32[1,2,16,6]{2,3,1,0:T(8,128)S(1)} %maximum_divide_fusion) | data formatting | bytes 1536
  (10 shorter events, 0.1 us)
Async XLA Ops:
  1.7 16.4 %collective-permute-start = (bf16[1,2,256,384]{3,2,1,0:T(8,128)(2,1)S(1)}, bf16[1,2,256,384]{3,2,1,0:T(8,128)(2,1)S(1)}, u32[]{:S(2)}, u32[]{:S(2)}) collective-permute-start(bf16[1,2,256,384]{3,2,1,0:T(8,128)(2,1)S(1)} %slice.67), channel_id=1, source_target_pairs={{0,30},{2,0},{4,2},{6,4},{8,6},{10,8},{12,10},{14,12},{16,14},{18,... | collective-permute-start | bytes 1179656 | tf_op jit(solution)/shard_map/ppermute | solution.py:17
  8.4 11.3 %collective-permute-start.1 = (bf16[1,2,256,384]{3,2,1,0:T(8,128)(2,1)S(1)}, bf16[1,2,256,384]{3,2,1,0:T(8,128)(2,1)S(1)}, u32[]{:S(2)}, u32[]{:S(2)}) collective-permute-start(bf16[1,2,256,384]{3,2,1,0:T(8,128)(2,1)S(1)} %get-tuple-element.43), channel_id=1, source_target_pairs={{0,30},{2,0},{4,2},{6,4},{8,6},{10,8},{12,10},{14,12},{16,14},{18,... | collective-permute-start | bytes 1179656 | tf_op jit(solution)/shard_map/ppermute | solution.py:17
  9.1 13.9 %collective-permute-start.2 = (bf16[1,2,256,384]{3,2,1,0:T(8,128)(2,1)S(1)}, bf16[1,2,256,384]{3,2,1,0:T(8,128)(2,1)S(1)}, u32[]{:S(2)}, u32[]{:S(2)}) collective-permute-start(bf16[1,2,256,384]{3,2,1,0:T(8,128)(2,1)S(1)} %get-tuple-element.42), channel_id=1, source_target_pairs={{0,30},{2,0},{4,2},{6,4},{8,6},{10,8},{12,10},{14,12},{16,14},{18,... | collective-permute-start | bytes 1179656 | tf_op jit(solution)/shard_map/ppermute | solution.py:17
  9.9 1.9 %copy-start = (bf16[8,2,256,384]{3,2,1,0:T(8,128)(2,1)S(1)}, bf16[8,2,256,384]{3,2,1,0:T(8,128)(2,1)}, u32[]{:S(2)}) copy-start(bf16[8,2,256,384]{3,2,1,0:T(8,128)(2,1)} %refs_7_.3) | copy-start | bytes 9437188
  11.8 6.3 %copy-start.1 = (bf16[8,2,256,384]{3,2,1,0:T(8,128)(2,1)S(1)}, bf16[8,2,256,384]{3,2,1,0:T(8,128)(2,1)}, u32[]{:S(2)}) copy-start(bf16[8,2,256,384]{3,2,1,0:T(8,128)(2,1)} %refs_7_.3) | copy-start | bytes 9437188
  19.7 1.5 %copy-start.2 = (s32[16]{0:T(128)S(1)}, s32[16]{0:T(128)}, u32[]{:S(2)}) copy-start(s32[16]{0:T(128)} %refs_1_.5) | copy-start | bytes 196

commit v16 on v14

--- a/solution.py
+++ b/solution.py
@@ -392,7 +392,8 @@
             [sums[:, (h * 3 + f) * width : (h * 3 + f + 1) * width] for h in range(halves)], 0
         )
 
-    network_mean = (jnp.stack([field(0), field(1)], 0) / (1.0 + field(2)))[None]
+    flipped = jnp.stack([field(0).T, field(1).T], 1) / (1.0 + field(2).T[:, None, :])
+    network_mean = jnp.transpose(flipped[None], (0, 2, 3, 1))
     return (interferograms, coherence, network_mean)
 
 

time: 37.3 us -> 37.2 us (level)
    pallas_call x3, Pallas kernels: 10.2 us -> 10.7 us  [local_math(): pl.pallas_call(make_kernel(images, first, dates, rows, cols, nknown, tile...]
    pallas_call x2, Pallas kernels: 3.23 us -> 2.77 us  [rim_step(): pl.pallas_call(kernel, out_shape=(jax.ShapeDtypeStruct(racc_in.shape, jnp...]
    unnamed x12 -> x8, local copies, waits for them, and re-layouts: 3.62 us -> 3.25 us
where the time goes in v16:
time: 37.2 us; the launch traced here: 36.7 us
  Pallas kernels  13.5 us (36%)
  blocking collectives  10.3 us (28%)
  starting transfers between devices  6.29 us (17%)
  local copies, waits for them, and re-layouts  5.85 us (16%)
  between operations  0.78 us (2%)
    pallas_call x3, Pallas kernels, local_math(): pl.pallas_call(make_kernel(images, first, dates, rows, cols, nknown, tile...  10.7 us
    all_to_all x1, blocking collectives, on_device(): lax.all_to_all(slotted, 'date', split_axis=0, concat_axis=0, tiled=True)  10.3 us
    ppermute x3, starting transfers between devices, shifted(): return lax.ppermute(value, axis, pairs)  6.29 us
    unnamed x8, local copies, waits for them, and re-layouts  3.25 us
    pallas_call x2, Pallas kernels, rim_step(): pl.pallas_call(kernel, out_shape=(jax.ShapeDtypeStruct(racc_in.shape, jnp...  2.77 us
    slice x2, local copies, waits for them, and re-layouts, on_device(): (slc if t == 0 else later)[t:t + 1]  2.23 us
  transfers between devices with their start and end apart: 3, of which 0 were waited for; matrix products, arithmetic and copies ran while one was open for 5% of the time, Pallas kernels for 30%

profile of v16, /device:TPU:0, one launch (start us, length us, event | category | flops | bytes accessed | tf_op | source)
XLA Modules:
  0.0 36.7 jit_solution(14418960396119868174)
XLA Ops:
  0.6 1.0 %slice.67 = bf16[1,2,256,384]{3,2,1,0:T(8,128)(2,1)S(1)} slice(bf16[8,2,256,384]{3,2,1,0:T(8,128)(2,1)} %refs_7_.3), slice={[0:1], [0:2], [0:256], [0:384]} | slice | bytes 786432 | tf_op jit(solution)/shard_map/slice | solution.py:354
  1.7 5.5 %collective-permute-start = (bf16[1,2,256,384]{3,2,1,0:T(8,128)(2,1)S(1)}, bf16[1,2,256,384]{3,2,1,0:T(8,128)(2,1)S(1)}, u32[]{:S(2)}, u32[]{:S(2)}) collective-permute-start(bf16[1,2,256,384]{3,2,1,0:T(8,128)(2,1)S(1)} %slice.67), channel_id=1, source_target_pairs={{0,30},{2,0},{4,2},{6,4},{8,6},{10,8},{12,10},{14,12},{16,14},{18,... | collective-permute-start | bytes 1179656 | tf_op jit(solution)/shard_map/ppermute | solution.py:17
  7.2 1.2 %fusion.2 = (bf16[1,2,256,384]{3,2,1,0:T(8,128)(2,1)S(1)}, bf16[1,2,256,384]{3,2,1,0:T(8,128)(2,1)S(1)}) fusion(bf16[8,2,256,384]{3,2,1,0:T(8,128)(2,1)} %refs_7_.3), kind=kLoop, calls=%fused_computation.7 | loop fusion | bytes 1572864 | tf_op jit(solution)/shard_map/slice | solution.py:354
  8.4 0.7 %collective-permute-start.1 = (bf16[1,2,256,384]{3,2,1,0:T(8,128)(2,1)S(1)}, bf16[1,2,256,384]{3,2,1,0:T(8,128)(2,1)S(1)}, u32[]{:S(2)}, u32[]{:S(2)}) collective-permute-start(bf16[1,2,256,384]{3,2,1,0:T(8,128)(2,1)S(1)} %get-tuple-element.40), channel_id=1, source_target_pairs={{0,30},{2,0},{4,2},{6,4},{8,6},{10,8},{12,10},{14,12},{16,14},{18,... | collective-permute-start | bytes 1179656 | tf_op jit(solution)/shard_map/ppermute | solution.py:17
  9.1 0.1 collective-permute-start.2
  9.2 0.8 %copy.17.refs_0_ = s32[8,3]{1,0:T(8,128)S(1)} copy(s32[8,3]{0,1:T(4,128)} %param.4) | data formatting | bytes 192 | tf_op args[1]
  9.9 0.0 copy-start
  9.9 1.9 %copy-done = bf16[8,2,256,384]{3,2,1,0:T(8,128)(2,1)S(1)} copy-done((bf16[8,2,256,384]{3,2,1,0:T(8,128)(2,1)S(1)}, bf16[8,2,256,384]{3,2,1,0:T(8,128)(2,1)}, u32[]{:S(2)}) %copy-start) | copy-done | bytes 3145752
  11.8 0.0 copy-start.1
  11.8 6.4 %shard_map.58 = (f32[8,3,2,16,96]{4,3,2,1,0:T(8,128)}, f32[8,3,16,96]{3,2,1,0:T(8,128)}, f32[3,16,128]{2,1,0:T(8,128)S(1)}, f32[8,16,128]{2,1,0:T(8,128)S(1)}, f32[3,3,2,16,384]{4,3,2,1,0:T(8,128)S(1)}) custom-call(s32[8,3]{1,0:T(8,128)S(1)} %copy.17.refs_0_, bf16[8,2,256,384]{3,2,1,0:T(8,128)(2,1)S(1)} %copy-done), custom_call_target="tpu_custom_call" | custom-call | tf_op jit(solution)/shard_map/pallas_call | solution.py:256
  18.2 0.0 collective-permute-done.rim_ref.refs_8_
  18.3 0.0 copy-done.1
  18.3 1.5 %shard_map.59 = (f32[3,3,2,16,384]{4,3,2,1,0:T(8,128)S(1)}, f32[1,16,128]{2,1,0:T(8,128)S(1)}) custom-call(s32[3,3]{1,0:T(4,128)S(1)} %slice.66.off_ref, bf16[8,2,256,384]{3,2,1,0:T(8,128)(2,1)S(1)} %copy-done.1, bf16[1,2,256,384]{3,2,1,0:T(8,128)(2,1)S(1)} %collective-permute-done.rim_ref.refs_8_, ...), custom_call_target="tpu_custom_call", output_to_operand_aliasing={{0}: (3, {})} | custom-call | tf_op jit(solution)/shard_map/pallas_call | solution.py:333
  19.8 0.0 copy-start.2
  19.8 0.0 collective-permute-done.1.rim_ref.refs_9_
  19.8 1.2 %shard_map.60 = (f32[3,3,2,16,384]{4,3,2,1,0:T(8,128)S(1)}, f32[1,16,128]{2,1,0:T(8,128)S(1)}) custom-call(s32[3,3]{1,0:T(4,128)S(1)} %slice.66.off_ref, bf16[8,2,256,384]{3,2,1,0:T(8,128)(2,1)S(1)} %copy-done.1, bf16[1,2,256,384]{3,2,1,0:T(8,128)(2,1)S(1)} %collective-permute-done.1.rim_ref.refs_9_, ...), custom_call_target="tpu_custom_call", output_to_operand_aliasing={{0}: (3, {})} | custom-call | tf_op jit(solution)/shard_map/pallas_call | solution.py:333
  21.1 0.0 copy-done.2
  21.1 1.9 %shard_map.61 = (f32[8,3,2,16,96]{4,3,2,1,0:T(8,128)}, f32[8,3,16,96]{3,2,1,0:T(8,128)}, f32[3,16,128]{2,1,0:T(8,128)S(1)}) custom-call(s32[2,3]{1,0:T(2,128)S(1)} %slice.69.refs_0_, s32[16]{0:T(128)S(1)} %copy-done.2, f32[5,16,128]{2,1,0:T(8,128)S(1)} %pad_maximum_fusion.refs_2_, ...), custom_call_target="tpu_custom_call", output_to_operand_aliasing={{0}: (5, {}), {1}: (6, {})} | custom-call | tf_op jit(solution)/shard_map/pallas_call | solution.py:256
  23.0 0.0 collective-permute-done.2.refs_10_
  23.0 2.4 %shard_map.62 = (f32[8,3,2,16,96]{4,3,2,1,0:T(8,128)}, f32[8,3,16,96]{3,2,1,0:T(8,128)}, f32[16,4,128]{2,1,0:T(4,128)S(1)}) custom-call(s32[1,3]{1,0:T(1,128)S(1)} %slice.64.refs_0_, s32[16]{0:T(128)S(1)} %copy-done.2, f32[5,16,128]{2,1,0:T(8,128)S(1)} %pad_maximum_fusion.refs_2_, ...), custom_call_target="tpu_custom_call", output_to_operand_aliasing={{0}: (5, {}), {1}: (6, {})} | custom-call | tf_op jit(solution)/shard_map/pallas_call | solution.py:256
  25.5 10.3 %all_to_all.5 = f32[16,4,128]{2,1,0:T(4,128)S(1)} all-to-all(f32[16,4,128]{2,1,0:T(4,128)S(1)} %get-tuple-element.32), channel_id=1, replica_groups=mesh['date'=16,'strip'=2] {'date'}, dimensions={0} | all-to-all | bytes 65536 | tf_op jit(solution)/shard_map/all_to_all | solution.py:387
  35.8 0.1 fusion.3
  35.9 0.1 copy.23
  36.0 0.1 copy.21
  36.1 0.1 copy.22
  36.1 0.6 %copy.24 = f32[1,2,16,6]{2,1,3,0:T(2,128)} copy(f32[1,2,16,6]{2,3,1,0:T(8,128)S(1)} %fusion) | data formatting | bytes 1536
  (11 shorter events, 0.1 us)
Async XLA Ops:
  1.7 16.6 %collective-permute-start = (bf16[1,2,256,384]{3,2,1,0:T(8,128)(2,1)S(1)}, bf16[1,2,256,384]{3,2,1,0:T(8,128)(2,1)S(1)}, u32[]{:S(2)}, u32[]{:S(2)}) collective-permute-start(bf16[1,2,256,384]{3,2,1,0:T(8,128)(2,1)S(1)} %slice.67), channel_id=1, source_target_pairs={{0,30},{2,0},{4,2},{6,4},{8,6},{10,8},{12,10},{14,12},{16,14},{18,... | collective-permute-start | bytes 1179656 | tf_op jit(solution)/shard_map/ppermute | solution.py:17
  8.4 11.5 %collective-permute-start.1 = (bf16[1,2,256,384]{3,2,1,0:T(8,128)(2,1)S(1)}, bf16[1,2,256,384]{3,2,1,0:T(8,128)(2,1)S(1)}, u32[]{:S(2)}, u32[]{:S(2)}) collective-permute-start(bf16[1,2,256,384]{3,2,1,0:T(8,128)(2,1)S(1)} %get-tuple-element.40), channel_id=1, source_target_pairs={{0,30},{2,0},{4,2},{6,4},{8,6},{10,8},{12,10},{14,12},{16,14},{18,... | collective-permute-start | bytes 1179656 | tf_op jit(solution)/shard_map/ppermute | solution.py:17
  9.1 13.9 %collective-permute-start.2 = (bf16[1,2,256,384]{3,2,1,0:T(8,128)(2,1)S(1)}, bf16[1,2,256,384]{3,2,1,0:T(8,128)(2,1)S(1)}, u32[]{:S(2)}, u32[]{:S(2)}) collective-permute-start(bf16[1,2,256,384]{3,2,1,0:T(8,128)(2,1)S(1)} %get-tuple-element.39), channel_id=1, source_target_pairs={{0,30},{2,0},{4,2},{6,4},{8,6},{10,8},{12,10},{14,12},{16,14},{18,... | collective-permute-start | bytes 1179656 | tf_op jit(solution)/shard_map/ppermute | solution.py:17
  9.9 1.9 %copy-start = (bf16[8,2,256,384]{3,2,1,0:T(8,128)(2,1)S(1)}, bf16[8,2,256,384]{3,2,1,0:T(8,128)(2,1)}, u32[]{:S(2)}) copy-start(bf16[8,2,256,384]{3,2,1,0:T(8,128)(2,1)} %refs_7_.3) | copy-start | bytes 9437188
  11.8 6.4 %copy-start.1 = (bf16[8,2,256,384]{3,2,1,0:T(8,128)(2,1)S(1)}, bf16[8,2,256,384]{3,2,1,0:T(8,128)(2,1)}, u32[]{:S(2)}) copy-start(bf16[8,2,256,384]{3,2,1,0:T(8,128)(2,1)} %refs_7_.3) | copy-start | bytes 9437188
  19.8 1.3 %copy-start.2 = (s32[16]{0:T(128)S(1)}, s32[16]{0:T(128)}, u32[]{:S(2)}) copy-start(s32[16]{0:T(128)} %refs_1_.5) | copy-start | bytes 196

commit v17 on v16

--- a/solution.py
+++ b/solution.py
@@ -55,9 +55,18 @@
             pw_cp.start()
             ws_cp.start()
             rx_cp.start()
-        for t, (src, lead) in enumerate(images):
-            if t >= known or (t < NB and t + NB >= known):
-                xf[t] = srcs[src][lead].astype(jnp.float32)
+        need = jnp.bool_(True)
+        if known:
+            need = jnp.bool_(False)
+            for i in range(racc.shape[0]):
+                for k in range(NB):
+                    need = jnp.logical_or(need, first + i + off_ref[i, k] >= known)
+
+        @pl.when(need)
+        def _():
+            for t, (src, lead) in enumerate(images):
+                if t >= known or (t < NB and t + NB >= known):
+                    xf[t] = srcs[src][lead].astype(jnp.float32)
 
         line = lax.broadcasted_iota(jnp.int32, (cols, lanes), 0)
         cell = lax.broadcasted_iota(jnp.int32, (cols, lanes), 1)
@@ -93,10 +102,13 @@
 
         fresh = total - known
         if fresh:
-            lax.fori_loop(known, total, power, 0)
-            pw[pl.ds(known, fresh)] = split_pool(pacc[...].reshape(fresh * groups, cols), pool).reshape(
-                fresh, groups, lanes
-            )
+
+            @pl.when(need)
+            def _():
+                lax.fori_loop(known, total, power, 0)
+                pw[pl.ds(known, fresh)] = split_pool(pacc[...].reshape(fresh * groups, cols), pool).reshape(
+                    fresh, groups, lanes
+                )
         if known:
             pw_cp.wait()
         else:

time: 37.2 us -> 36.8 us (0.989); the launches traced: 36.7 us -> 36.8 us
  no operation moved by 1% of the time
where the time goes in v17:
time: 36.8 us
  Pallas kernels  13.5 us (37%)
  blocking collectives  10.3 us (28%)
  starting transfers between devices  6.29 us (17%)
  local copies, waits for them, and re-layouts  5.85 us (16%)
  between operations  0.78 us (2%)
    pallas_call x3, Pallas kernels, local_math(): pl.pallas_call(make_kernel(images, first, dates, rows, cols, nknown, tile...  10.4 us
    all_to_all x1, blocking collectives, on_device(): lax.all_to_all(slotted, 'date', split_axis=0, concat_axis=0, tiled=True)  10.3 us
    ppermute x3, starting transfers between devices, shifted(): return lax.ppermute(value, axis, pairs)  6.29 us
    unnamed x8, local copies, waits for them, and re-layouts  3.25 us
    pallas_call x2, Pallas kernels, rim_step(): pl.pallas_call(kernel, out_shape=(jax.ShapeDtypeStruct(racc_in.shape, jnp...  3.06 us
    slice x2, local copies, waits for them, and re-layouts, on_device(): (slc if t == 0 else later)[t:t + 1]  2.23 us
  transfers between devices with their start and end apart: 3, of which 0 were waited for; matrix products, arithmetic and copies ran while one was open for 5% of the time, Pallas kernels for 30%

profile of v17, /device:TPU:0, one launch (start us, length us, event | category | flops | bytes accessed | tf_op | source)
XLA Modules:
  0.0 36.8 jit_solution(12749116988354857441)
XLA Ops:
  0.6 1.0 %slice.67 = bf16[1,2,256,384]{3,2,1,0:T(8,128)(2,1)S(1)} slice(bf16[8,2,256,384]{3,2,1,0:T(8,128)(2,1)} %refs_7_.3), slice={[0:1], [0:2], [0:256], [0:384]} | slice | bytes 786432 | tf_op jit(solution)/shard_map/slice | solution.py:366
  1.7 5.5 %collective-permute-start = (bf16[1,2,256,384]{3,2,1,0:T(8,128)(2,1)S(1)}, bf16[1,2,256,384]{3,2,1,0:T(8,128)(2,1)S(1)}, u32[]{:S(2)}, u32[]{:S(2)}) collective-permute-start(bf16[1,2,256,384]{3,2,1,0:T(8,128)(2,1)S(1)} %slice.67), channel_id=1, source_target_pairs={{0,30},{2,0},{4,2},{6,4},{8,6},{10,8},{12,10},{14,12},{16,14},{18,... | collective-permute-start | bytes 1179656 | tf_op jit(solution)/shard_map/ppermute | solution.py:17
  7.2 1.2 %fusion.2 = (bf16[1,2,256,384]{3,2,1,0:T(8,128)(2,1)S(1)}, bf16[1,2,256,384]{3,2,1,0:T(8,128)(2,1)S(1)}) fusion(bf16[8,2,256,384]{3,2,1,0:T(8,128)(2,1)} %refs_7_.3), kind=kLoop, calls=%fused_computation.7 | loop fusion | bytes 1572864 | tf_op jit(solution)/shard_map/slice | solution.py:366
  8.4 0.7 %collective-permute-start.1 = (bf16[1,2,256,384]{3,2,1,0:T(8,128)(2,1)S(1)}, bf16[1,2,256,384]{3,2,1,0:T(8,128)(2,1)S(1)}, u32[]{:S(2)}, u32[]{:S(2)}) collective-permute-start(bf16[1,2,256,384]{3,2,1,0:T(8,128)(2,1)S(1)} %get-tuple-element.40), channel_id=1, source_target_pairs={{0,30},{2,0},{4,2},{6,4},{8,6},{10,8},{12,10},{14,12},{16,14},{18,... | collective-permute-start | bytes 1179656 | tf_op jit(solution)/shard_map/ppermute | solution.py:17
  9.1 0.1 collective-permute-start.2
  9.2 0.8 %copy.17.refs_0_ = s32[8,3]{1,0:T(8,128)S(1)} copy(s32[8,3]{0,1:T(4,128)} %param.4) | data formatting | bytes 192 | tf_op args[1]
  9.9 0.0 copy-start
  9.9 1.9 %copy-done = bf16[8,2,256,384]{3,2,1,0:T(8,128)(2,1)S(1)} copy-done((bf16[8,2,256,384]{3,2,1,0:T(8,128)(2,1)S(1)}, bf16[8,2,256,384]{3,2,1,0:T(8,128)(2,1)}, u32[]{:S(2)}) %copy-start) | copy-done | bytes 3145752
  11.8 0.0 copy-start.1
  11.8 6.1 %shard_map.58 = (f32[8,3,2,16,96]{4,3,2,1,0:T(8,128)}, f32[8,3,16,96]{3,2,1,0:T(8,128)}, f32[3,16,128]{2,1,0:T(8,128)S(1)}, f32[8,16,128]{2,1,0:T(8,128)S(1)}, f32[3,3,2,16,384]{4,3,2,1,0:T(8,128)S(1)}) custom-call(s32[8,3]{1,0:T(8,128)S(1)} %copy.17.refs_0_, bf16[8,2,256,384]{3,2,1,0:T(8,128)(2,1)S(1)} %copy-done), custom_call_target="tpu_custom_call" | custom-call | tf_op jit(solution)/shard_map/pallas_call | solution.py:268
  17.9 0.0 collective-permute-done.rim_ref.refs_8_
  18.0 0.0 copy-done.1
  18.0 1.7 %shard_map.59 = (f32[3,3,2,16,384]{4,3,2,1,0:T(8,128)S(1)}, f32[1,16,128]{2,1,0:T(8,128)S(1)}) custom-call(s32[3,3]{1,0:T(4,128)S(1)} %slice.66.off_ref, bf16[8,2,256,384]{3,2,1,0:T(8,128)(2,1)S(1)} %copy-done.1, bf16[1,2,256,384]{3,2,1,0:T(8,128)(2,1)S(1)} %collective-permute-done.rim_ref.refs_8_, ...), custom_call_target="tpu_custom_call", output_to_operand_aliasing={{0}: (3, {})} | custom-call | tf_op jit(solution)/shard_map/pallas_call | solution.py:345
  19.7 0.0 copy-start.2
  19.7 0.0 collective-permute-done.1.rim_ref.refs_9_
  19.7 1.4 %shard_map.60 = (f32[3,3,2,16,384]{4,3,2,1,0:T(8,128)S(1)}, f32[1,16,128]{2,1,0:T(8,128)S(1)}) custom-call(s32[3,3]{1,0:T(4,128)S(1)} %slice.66.off_ref, bf16[8,2,256,384]{3,2,1,0:T(8,128)(2,1)S(1)} %copy-done.1, bf16[1,2,256,384]{3,2,1,0:T(8,128)(2,1)S(1)} %collective-permute-done.1.rim_ref.refs_9_, ...), custom_call_target="tpu_custom_call", output_to_operand_aliasing={{0}: (3, {})} | custom-call | tf_op jit(solution)/shard_map/pallas_call | solution.py:345
  21.1 0.0 copy-done.2
  21.1 1.8 %shard_map.61 = (f32[8,3,2,16,96]{4,3,2,1,0:T(8,128)}, f32[8,3,16,96]{3,2,1,0:T(8,128)}, f32[3,16,128]{2,1,0:T(8,128)S(1)}) custom-call(s32[2,3]{1,0:T(2,128)S(1)} %slice.69.refs_0_, s32[16]{0:T(128)S(1)} %copy-done.2, f32[5,16,128]{2,1,0:T(8,128)S(1)} %pad_maximum_fusion.refs_2_, ...), custom_call_target="tpu_custom_call", output_to_operand_aliasing={{0}: (5, {}), {1}: (6, {})} | custom-call | tf_op jit(solution)/shard_map/pallas_call | solution.py:268
  23.0 0.0 collective-permute-done.2.refs_10_
  23.0 2.5 %shard_map.62 = (f32[8,3,2,16,96]{4,3,2,1,0:T(8,128)}, f32[8,3,16,96]{3,2,1,0:T(8,128)}, f32[16,4,128]{2,1,0:T(4,128)S(1)}) custom-call(s32[1,3]{1,0:T(1,128)S(1)} %slice.64.refs_0_, s32[16]{0:T(128)S(1)} %copy-done.2, f32[5,16,128]{2,1,0:T(8,128)S(1)} %pad_maximum_fusion.refs_2_, ...), custom_call_target="tpu_custom_call", output_to_operand_aliasing={{0}: (5, {}), {1}: (6, {})} | custom-call | tf_op jit(solution)/shard_map/pallas_call | solution.py:268
  25.5 10.3 %all_to_all.5 = f32[16,4,128]{2,1,0:T(4,128)S(1)} all-to-all(f32[16,4,128]{2,1,0:T(4,128)S(1)} %get-tuple-element.32), channel_id=1, replica_groups=mesh['date'=16,'strip'=2] {'date'}, dimensions={0} | all-to-all | bytes 65536 | tf_op jit(solution)/shard_map/all_to_all | solution.py:399
  35.8 0.1 fusion.3
  35.9 0.1 copy.23
  36.0 0.1 copy.21
  36.1 0.1 copy.22
  36.2 0.6 %copy.24 = f32[1,2,16,6]{2,1,3,0:T(2,128)} copy(f32[1,2,16,6]{2,3,1,0:T(8,128)S(1)} %fusion) | data formatting | bytes 1536
  (11 shorter events, 0.1 us)
Async XLA Ops:
  1.7 16.3 %collective-permute-start = (bf16[1,2,256,384]{3,2,1,0:T(8,128)(2,1)S(1)}, bf16[1,2,256,384]{3,2,1,0:T(8,128)(2,1)S(1)}, u32[]{:S(2)}, u32[]{:S(2)}) collective-permute-start(bf16[1,2,256,384]{3,2,1,0:T(8,128)(2,1)S(1)} %slice.67), channel_id=1, source_target_pairs={{0,30},{2,0},{4,2},{6,4},{8,6},{10,8},{12,10},{14,12},{16,14},{18,... | collective-permute-start | bytes 1179656 | tf_op jit(solution)/shard_map/ppermute | solution.py:17
  8.4 11.3 %collective-permute-start.1 = (bf16[1,2,256,384]{3,2,1,0:T(8,128)(2,1)S(1)}, bf16[1,2,256,384]{3,2,1,0:T(8,128)(2,1)S(1)}, u32[]{:S(2)}, u32[]{:S(2)}) collective-permute-start(bf16[1,2,256,384]{3,2,1,0:T(8,128)(2,1)S(1)} %get-tuple-element.40), channel_id=1, source_target_pairs={{0,30},{2,0},{4,2},{6,4},{8,6},{10,8},{12,10},{14,12},{16,14},{18,... | collective-permute-start | bytes 1179656 | tf_op jit(solution)/shard_map/ppermute | solution.py:17
  9.1 13.9 %collective-permute-start.2 = (bf16[1,2,256,384]{3,2,1,0:T(8,128)(2,1)S(1)}, bf16[1,2,256,384]{3,2,1,0:T(8,128)(2,1)S(1)}, u32[]{:S(2)}, u32[]{:S(2)}) collective-permute-start(bf16[1,2,256,384]{3,2,1,0:T(8,128)(2,1)S(1)} %get-tuple-element.39), channel_id=1, source_target_pairs={{0,30},{2,0},{4,2},{6,4},{8,6},{10,8},{12,10},{14,12},{16,14},{18,... | collective-permute-start | bytes 1179656 | tf_op jit(solution)/shard_map/ppermute | solution.py:17
  9.9 1.9 %copy-start = (bf16[8,2,256,384]{3,2,1,0:T(8,128)(2,1)S(1)}, bf16[8,2,256,384]{3,2,1,0:T(8,128)(2,1)}, u32[]{:S(2)}) copy-start(bf16[8,2,256,384]{3,2,1,0:T(8,128)(2,1)} %refs_7_.3) | copy-start | bytes 9437188
  11.8 6.1 %copy-start.1 = (bf16[8,2,256,384]{3,2,1,0:T(8,128)(2,1)S(1)}, bf16[8,2,256,384]{3,2,1,0:T(8,128)(2,1)}, u32[]{:S(2)}) copy-start(bf16[8,2,256,384]{3,2,1,0:T(8,128)(2,1)} %refs_7_.3) | copy-start | bytes 9437188
  19.7 1.5 %copy-start.2 = (s32[16]{0:T(128)S(1)}, s32[16]{0:T(128)}, u32[]{:S(2)}) copy-start(s32[16]{0:T(128)} %refs_1_.5) | copy-start | bytes 196

commit v18 on v16

--- a/solution.py
+++ b/solution.py
@@ -94,9 +94,10 @@
         fresh = total - known
         if fresh:
             lax.fori_loop(known, total, power, 0)
-            pw[pl.ds(known, fresh)] = split_pool(pacc[...].reshape(fresh * groups, cols), pool).reshape(
-                fresh, groups, lanes
-            )
+            if not known:
+                pw[pl.ds(known, fresh)] = split_pool(pacc[...].reshape(fresh * groups, cols), pool).reshape(
+                    fresh, groups, lanes
+                )
         if known:
             pw_cp.wait()
         else:
@@ -138,7 +139,13 @@
         lax.fori_loop(0, racc.shape[0], pairs, 0)
         if not known:
             racc_x[...] = racc[pl.ds(dates, racc.shape[0] - dates)]
-        pooled = split_pool(racc[pl.ds(0, dates)].reshape(dates * NB * 2 * groups, cols), pool)
+        pair_rows = racc[pl.ds(0, dates)].reshape(dates * NB * 2 * groups, cols)
+        if known and fresh:
+            both = split_pool(jnp.concatenate([pacc[...].reshape(fresh * groups, cols), pair_rows], 0), pool)
+            pw[pl.ds(known, fresh)] = both[: fresh * groups].reshape(fresh, groups, lanes)
+            pooled = both[fresh * groups :]
+        else:
+            pooled = split_pool(pair_rows, pool)
         pooled = pooled.reshape(dates, NB, 2, groups, lanes)
         ifg_s[...] = pooled[..., :cells]
 

time: 37.2 us -> 37 us (level)
    pallas_call x3, Pallas kernels: 10.7 us -> 10.3 us  [local_math(): pl.pallas_call(make_kernel(images, first, dates, rows, cols, nknown, tile...]
where the time goes in v18:
time: 37 us; the launch traced here: 36.8 us
  Pallas kernels  13.3 us (36%)
  blocking collectives  10.4 us (28%)
  starting transfers between devices  6.29 us (17%)
  local copies, waits for them, and re-layouts  5.85 us (16%)
  between operations  0.78 us (2%)
    all_to_all x1, blocking collectives, on_device(): lax.all_to_all(slotted, 'date', split_axis=0, concat_axis=0, tiled=True)  10.4 us
    pallas_call x3, Pallas kernels, local_math(): pl.pallas_call(make_kernel(images, first, dates, rows, cols, nknown, tile...  10.3 us
    ppermute x3, starting transfers between devices, shifted(): return lax.ppermute(value, axis, pairs)  6.29 us
    unnamed x8, local copies, waits for them, and re-layouts  3.25 us
    pallas_call x2, Pallas kernels, rim_step(): pl.pallas_call(kernel, out_shape=(jax.ShapeDtypeStruct(racc_in.shape, jnp...  3.06 us
    slice x2, local copies, waits for them, and re-layouts, on_device(): (slc if t == 0 else later)[t:t + 1]  2.23 us
  transfers between devices with their start and end apart: 3, of which 0 were waited for; matrix products, arithmetic and copies ran while one was open for 5% of the time, Pallas kernels for 30%

profile of v18, /device:TPU:0, one launch (start us, length us, event | category | flops | bytes accessed | tf_op | source)
XLA Modules:
  0.0 36.8 jit_solution(15143147823494852652)
XLA Ops:
  0.6 1.0 %slice.67 = bf16[1,2,256,384]{3,2,1,0:T(8,128)(2,1)S(1)} slice(bf16[8,2,256,384]{3,2,1,0:T(8,128)(2,1)} %refs_7_.3), slice={[0:1], [0:2], [0:256], [0:384]} | slice | bytes 786432 | tf_op jit(solution)/shard_map/slice | solution.py:361
  1.7 5.5 %collective-permute-start = (bf16[1,2,256,384]{3,2,1,0:T(8,128)(2,1)S(1)}, bf16[1,2,256,384]{3,2,1,0:T(8,128)(2,1)S(1)}, u32[]{:S(2)}, u32[]{:S(2)}) collective-permute-start(bf16[1,2,256,384]{3,2,1,0:T(8,128)(2,1)S(1)} %slice.67), channel_id=1, source_target_pairs={{0,30},{2,0},{4,2},{6,4},{8,6},{10,8},{12,10},{14,12},{16,14},{18,... | collective-permute-start | bytes 1179656 | tf_op jit(solution)/shard_map/ppermute | solution.py:17
  7.2 1.2 %fusion.2 = (bf16[1,2,256,384]{3,2,1,0:T(8,128)(2,1)S(1)}, bf16[1,2,256,384]{3,2,1,0:T(8,128)(2,1)S(1)}) fusion(bf16[8,2,256,384]{3,2,1,0:T(8,128)(2,1)} %refs_7_.3), kind=kLoop, calls=%fused_computation.7 | loop fusion | bytes 1572864 | tf_op jit(solution)/shard_map/slice | solution.py:361
  8.4 0.7 %collective-permute-start.1 = (bf16[1,2,256,384]{3,2,1,0:T(8,128)(2,1)S(1)}, bf16[1,2,256,384]{3,2,1,0:T(8,128)(2,1)S(1)}, u32[]{:S(2)}, u32[]{:S(2)}) collective-permute-start(bf16[1,2,256,384]{3,2,1,0:T(8,128)(2,1)S(1)} %get-tuple-element.40), channel_id=1, source_target_pairs={{0,30},{2,0},{4,2},{6,4},{8,6},{10,8},{12,10},{14,12},{16,14},{18,... | collective-permute-start | bytes 1179656 | tf_op jit(solution)/shard_map/ppermute | solution.py:17
  9.1 0.1 collective-permute-start.2
  9.2 0.8 %copy.17.refs_0_ = s32[8,3]{1,0:T(8,128)S(1)} copy(s32[8,3]{0,1:T(4,128)} %param.4) | data formatting | bytes 192 | tf_op args[1]
  9.9 0.0 copy-start
  9.9 1.9 %copy-done = bf16[8,2,256,384]{3,2,1,0:T(8,128)(2,1)S(1)} copy-done((bf16[8,2,256,384]{3,2,1,0:T(8,128)(2,1)S(1)}, bf16[8,2,256,384]{3,2,1,0:T(8,128)(2,1)}, u32[]{:S(2)}) %copy-start) | copy-done | bytes 3145752
  11.8 0.0 copy-start.1
  11.8 6.3 %shard_map.58 = (f32[8,3,2,16,96]{4,3,2,1,0:T(8,128)}, f32[8,3,16,96]{3,2,1,0:T(8,128)}, f32[3,16,128]{2,1,0:T(8,128)S(1)}, f32[8,16,128]{2,1,0:T(8,128)S(1)}, f32[3,3,2,16,384]{4,3,2,1,0:T(8,128)S(1)}) custom-call(s32[8,3]{1,0:T(8,128)S(1)} %copy.17.refs_0_, bf16[8,2,256,384]{3,2,1,0:T(8,128)(2,1)S(1)} %copy-done), custom_call_target="tpu_custom_call" | custom-call | tf_op jit(solution)/shard_map/pallas_call | solution.py:263
  18.1 0.0 collective-permute-done.rim_ref.refs_8_
  18.1 0.0 copy-done.1
  18.1 1.5 %shard_map.59 = (f32[3,3,2,16,384]{4,3,2,1,0:T(8,128)S(1)}, f32[1,16,128]{2,1,0:T(8,128)S(1)}) custom-call(s32[3,3]{1,0:T(4,128)S(1)} %slice.66.off_ref, bf16[8,2,256,384]{3,2,1,0:T(8,128)(2,1)S(1)} %copy-done.1, bf16[1,2,256,384]{3,2,1,0:T(8,128)(2,1)S(1)} %collective-permute-done.rim_ref.refs_8_, ...), custom_call_target="tpu_custom_call", output_to_operand_aliasing={{0}: (3, {})} | custom-call | tf_op jit(solution)/shard_map/pallas_call | solution.py:340
  19.7 0.0 copy-start.2
  19.7 0.0 collective-permute-done.1.rim_ref.refs_9_
  19.7 1.5 %shard_map.60 = (f32[3,3,2,16,384]{4,3,2,1,0:T(8,128)S(1)}, f32[1,16,128]{2,1,0:T(8,128)S(1)}) custom-call(s32[3,3]{1,0:T(4,128)S(1)} %slice.66.off_ref, bf16[8,2,256,384]{3,2,1,0:T(8,128)(2,1)S(1)} %copy-done.1, bf16[1,2,256,384]{3,2,1,0:T(8,128)(2,1)S(1)} %collective-permute-done.1.rim_ref.refs_9_, ...), custom_call_target="tpu_custom_call", output_to_operand_aliasing={{0}: (3, {})} | custom-call | tf_op jit(solution)/shard_map/pallas_call | solution.py:340
  21.3 0.0 copy-done.2
  21.3 1.9 %shard_map.61 = (f32[8,3,2,16,96]{4,3,2,1,0:T(8,128)}, f32[8,3,16,96]{3,2,1,0:T(8,128)}, f32[3,16,128]{2,1,0:T(8,128)S(1)}) custom-call(s32[2,3]{1,0:T(2,128)S(1)} %slice.69.refs_0_, s32[16]{0:T(128)S(1)} %copy-done.2, f32[5,16,128]{2,1,0:T(8,128)S(1)} %pad_maximum_fusion.refs_2_, ...), custom_call_target="tpu_custom_call", output_to_operand_aliasing={{0}: (5, {}), {1}: (6, {})} | custom-call | tf_op jit(solution)/shard_map/pallas_call | solution.py:263
  23.1 0.0 collective-permute-done.2.refs_10_
  23.2 2.2 %shard_map.62 = (f32[8,3,2,16,96]{4,3,2,1,0:T(8,128)}, f32[8,3,16,96]{3,2,1,0:T(8,128)}, f32[16,4,128]{2,1,0:T(4,128)S(1)}) custom-call(s32[1,3]{1,0:T(1,128)S(1)} %slice.64.refs_0_, s32[16]{0:T(128)S(1)} %copy-done.2, f32[5,16,128]{2,1,0:T(8,128)S(1)} %pad_maximum_fusion.refs_2_, ...), custom_call_target="tpu_custom_call", output_to_operand_aliasing={{0}: (5, {}), {1}: (6, {})} | custom-call | tf_op jit(solution)/shard_map/pallas_call | solution.py:263
  25.3 10.4 %all_to_all.5 = f32[16,4,128]{2,1,0:T(4,128)S(1)} all-to-all(f32[16,4,128]{2,1,0:T(4,128)S(1)} %get-tuple-element.32), channel_id=1, replica_groups=mesh['date'=16,'strip'=2] {'date'}, dimensions={0} | all-to-all | bytes 65536 | tf_op jit(solution)/shard_map/all_to_all | solution.py:394
  35.8 0.1 fusion.3
  35.9 0.1 copy.23
  36.0 0.1 copy.21
  36.1 0.1 copy.22
  36.2 0.6 %copy.24 = f32[1,2,16,6]{2,1,3,0:T(2,128)} copy(f32[1,2,16,6]{2,3,1,0:T(8,128)S(1)} %fusion) | data formatting | bytes 1536
  (11 shorter events, 0.1 us)
Async XLA Ops:
  1.7 16.4 %collective-permute-start = (bf16[1,2,256,384]{3,2,1,0:T(8,128)(2,1)S(1)}, bf16[1,2,256,384]{3,2,1,0:T(8,128)(2,1)S(1)}, u32[]{:S(2)}, u32[]{:S(2)}) collective-permute-start(bf16[1,2,256,384]{3,2,1,0:T(8,128)(2,1)S(1)} %slice.67), channel_id=1, source_target_pairs={{0,30},{2,0},{4,2},{6,4},{8,6},{10,8},{12,10},{14,12},{16,14},{18,... | collective-permute-start | bytes 1179656 | tf_op jit(solution)/shard_map/ppermute | solution.py:17
  8.4 11.3 %collective-permute-start.1 = (bf16[1,2,256,384]{3,2,1,0:T(8,128)(2,1)S(1)}, bf16[1,2,256,384]{3,2,1,0:T(8,128)(2,1)S(1)}, u32[]{:S(2)}, u32[]{:S(2)}) collective-permute-start(bf16[1,2,256,384]{3,2,1,0:T(8,128)(2,1)S(1)} %get-tuple-element.40), channel_id=1, source_target_pairs={{0,30},{2,0},{4,2},{6,4},{8,6},{10,8},{12,10},{14,12},{16,14},{18,... | collective-permute-start | bytes 1179656 | tf_op jit(solution)/shard_map/ppermute | solution.py:17
  9.1 14.1 %collective-permute-start.2 = (bf16[1,2,256,384]{3,2,1,0:T(8,128)(2,1)S(1)}, bf16[1,2,256,384]{3,2,1,0:T(8,128)(2,1)S(1)}, u32[]{:S(2)}, u32[]{:S(2)}) collective-permute-start(bf16[1,2,256,384]{3,2,1,0:T(8,128)(2,1)S(1)} %get-tuple-element.39), channel_id=1, source_target_pairs={{0,30},{2,0},{4,2},{6,4},{8,6},{10,8},{12,10},{14,12},{16,14},{18,... | collective-permute-start | bytes 1179656 | tf_op jit(solution)/shard_map/ppermute | solution.py:17
  9.9 1.9 %copy-start = (bf16[8,2,256,384]{3,2,1,0:T(8,128)(2,1)S(1)}, bf16[8,2,256,384]{3,2,1,0:T(8,128)(2,1)}, u32[]{:S(2)}) copy-start(bf16[8,2,256,384]{3,2,1,0:T(8,128)(2,1)} %refs_7_.3) | copy-start | bytes 9437188
  11.8 6.3 %copy-start.1 = (bf16[8,2,256,384]{3,2,1,0:T(8,128)(2,1)S(1)}, bf16[8,2,256,384]{3,2,1,0:T(8,128)(2,1)}, u32[]{:S(2)}) copy-start(bf16[8,2,256,384]{3,2,1,0:T(8,128)(2,1)} %refs_7_.3) | copy-start | bytes 9437188
  19.7 1.6 %copy-start.2 = (s32[16]{0:T(128)S(1)}, s32[16]{0:T(128)}, u32[]{:S(2)}) copy-start(s32[16]{0:T(128)} %refs_1_.5) | copy-start | bytes 196
